TPU v7x, 256 devices: a whole 4x4x8 slice. The times are simulated.
256 devices in a mesh: seq: 16 (over x, y), exp: 16 (over z, core).
Axes of the slice: x: 4, y: 4, z: 8, core: 2. Of those that a mesh axis runs over, the one named last changes fastest.
Arguments:
- mixer_input: bfloat16 [16384, 4096], P('seq', 'exp'), may hold values from -6 to 6
- gate_input: bfloat16 [16384, 4096], P('seq', 'exp'), may hold values from -6 to 6
- write_keys: bfloat16 [16384, 128], P('seq'), may hold values from -6 to 6
- read_queries: bfloat16 [16384, 128], P('seq'), may hold values from -0.5 to 0.5
- step_size: float32 [64, 16384], P('exp', 'seq'), may hold values from 0 to 1, as said below
- log_decay: float32 [64, 16384], P('exp', 'seq'), may hold values from -1 to 0, as said below
- skip_gain: float32 [64], P('exp'), may hold values from 0.5 to 1.5
- out_weight: bfloat16 [4096, 2048], P('exp'), may hold values from -0.09375 to 0.09375
- residual: bfloat16 [16384, 2048], P(('seq', 'exp')), may hold values from -6 to 6
- norm_gain: float32 [2048], replicated, may hold values from 0.25 to 1.75
- routes: int32 [16384, 6], P(('seq', 'exp')), may hold values from 0 to 63, all different within a row; in each aligned block of 64 rows (0 to 63, 64 to 127, ...) at most 8 rows name the same one
- route_weight: float32 [16384, 6], P(('seq', 'exp')), may hold values from 0.1 to 0.5
- expert_gate: bfloat16 [256, 352, 2048], P(('seq', 'exp')), may hold values from -0.125 to 0.125
- expert_up: bfloat16 [256, 352, 2048], P(('seq', 'exp')), may hold values from -0.125 to 0.125
- expert_down: bfloat16 [256, 352, 2048], P(('seq', 'exp')), may hold values from -0.15625 to 0.15625
Outputs:
- block_output: bfloat16 [16384, 2048], P(('seq', 'exp'))
Inputs may be any that keep to these rules, and one draw needn't show every extreme that they name: `routes`: each row names 6 different experts; in each aligned block of 64 rows (the rows of one device) no expert is named by more than 8 rows, a bound that some block reaches. `step_size`: positive. `log_decay`: not positive.
All inputs are finite; a program needn't handle non-finite values.
Results may differ from a plain program's by a relative error of at most 0.015.
Values may be sent and summed in bfloat16 or wider, within the bound.
No kernel may reach another device: no remote copies, remote signals or barrier semaphores. Data moves between devices by JAX's collectives and lax.ppermute only.
A program may use at most 128 MiB of HBM per device.

v0:
```python
import jax
import jax.numpy as jnp
from jax import lax
from jax.sharding import PartitionSpec as P

HEAD_DIM = 64
STATE = 128
TOP = 6
SPLIT = 4
STRETCH = 256


def prefix(shard, axis, join, neutral):
    place = lax.axis_index(axis)
    gathered = jax.tree.map(
        lambda a, kind: lax.all_gather(a.astype(kind), axis), shard, (jnp.bfloat16, jnp.bfloat16)
    )
    state = jax.tree.map(lambda a, e: jnp.zeros_like(a) + jnp.asarray(e, a.dtype), shard, neutral)

    def one(turn, state):
        return join(
            state,
            jax.tree.map(
                lambda a, own: lax.dynamic_index_in_dim(a, turn, 0, False).astype(own.dtype),
                gathered,
                shard,
            ),
        )

    return lax.fori_loop(0, place, one, state)


def join_states(earlier, later_part):
    return (
        earlier[0] + later_part[0],
        jnp.exp(later_part[0])[:, None, None] * earlier[1] + later_part[1],
    )


def shards(
    mixer_input,
    gate_input,
    write_keys,
    read_queries,
    step_size,
    log_decay,
    skip_gain,
    out_weight,
    residual,
    norm_gain,
    routes,
    route_weight,
    expert_gate,
    expert_up,
    expert_down,
):
    length = mixer_input.shape[0]
    head_count = step_size.shape[0]
    blocks = length // STRETCH
    inputs = mixer_input.reshape(blocks, STRETCH, head_count, HEAD_DIM)
    key_rows = write_keys.reshape(blocks, STRETCH, STATE)
    queries = read_queries.reshape(blocks, STRETCH, STATE)
    step_rows = step_size.reshape(head_count, blocks, STRETCH).transpose(1, 0, 2)
    cumulative = jnp.cumsum(log_decay.reshape(head_count, blocks, STRETCH), axis=2).transpose(
        1, 0, 2
    )
    location_values = jnp.arange(STRETCH, dtype=jnp.int32)
    causal = location_values[:, None] >= location_values[None, :]
    scores = jnp.einsum("cin,cjn->cij", queries, key_rows, preferred_element_type=jnp.float32)
    spread = cumulative[:, :, :, None] - cumulative[:, :, None, :]
    decays = jnp.where(causal, jnp.exp(jnp.where(causal, spread, 0.0)), 0.0)
    mixing = (scores[:, None] * decays * step_rows[:, :, None, :]).astype(jnp.bfloat16)
    local_out = jnp.einsum("chij,cjhp->cihp", mixing, inputs, preferred_element_type=jnp.float32)
    tail_scale = jnp.exp(cumulative[:, :, -1:] - cumulative) * step_rows
    weighted = (inputs.astype(jnp.float32) * tail_scale.transpose(0, 2, 1)[..., None]).astype(
        jnp.bfloat16
    )
    block_state = jnp.einsum(
        "cjhp,cjn->chpn", weighted, key_rows, preferred_element_type=jnp.float32
    )
    totals = cumulative[:, :, -1]

    def advance(carry_state, pieces):
        block_total, fresh_state = pieces
        return (jnp.exp(block_total)[:, None, None] * carry_state + fresh_state, carry_state)

    zero_state = jnp.zeros((head_count, HEAD_DIM, STATE), jnp.float32)
    end_local, entering_local = lax.scan(advance, zero_state, (totals, block_state))
    device_decay = jnp.sum(totals, axis=0)
    before = prefix(
        (device_decay, end_local), "seq", join_states, (jnp.zeros_like(device_decay), zero_state)
    )
    before_state = before[1]
    before_blocks = jnp.cumsum(totals, axis=0) - totals
    entering = jnp.exp(before_blocks)[:, :, None, None] * before_state[None] + entering_local
    carried = jnp.einsum(
        "cin,chpn->cihp", queries.astype(jnp.float32), entering, precision=lax.Precision.HIGHEST
    )
    carried = carried * jnp.exp(cumulative).transpose(0, 2, 1)[..., None]
    result = local_out + carried + skip_gain[None, None, :, None] * inputs.astype(jnp.float32)
    gated_out = (
        result.reshape(length, head_count * HEAD_DIM) * jax.nn.silu(gate_input.astype(jnp.float32))
    ).astype(jnp.bfloat16)
    row_count = residual.shape[0]
    mixer_out = lax.psum_scatter(
        jnp.dot(gated_out, out_weight, preferred_element_type=jnp.float32).astype(jnp.bfloat16),
        "exp",
        scatter_dimension=0,
        tiled=True,
    ).astype(jnp.float32)
    stream = (residual.astype(jnp.float32) + mixer_out).astype(jnp.bfloat16)
    widened = stream.astype(jnp.float32)
    normed = (
        widened * lax.rsqrt(jnp.mean(widened * widened, axis=-1, keepdims=True) + 1e-06) * norm_gain
    ).astype(jnp.bfloat16)
    seq_count = lax.axis_size("seq")
    exp_count = lax.axis_size("exp")
    row_experts = exp_count // SPLIT
    experts = seq_count * row_experts
    capacity = min(row_count, max(2, (4 * TOP * row_count + 3 * experts - 1) // (3 * experts)))
    flat_routes = routes.reshape(-1)
    onehot = (flat_routes[:, None] == jnp.arange(experts, dtype=jnp.int32)[None, :]).astype(
        jnp.int32
    )
    earlier_count = jnp.cumsum(onehot, axis=0) - onehot
    slot_index = jnp.sum(earlier_count * onehot, axis=1)
    target = (
        flat_routes % row_experts * (seq_count * capacity)
        + flat_routes // row_experts * capacity
        + slot_index
    )
    owner_row = jnp.arange(flat_routes.shape[0], dtype=jnp.int32) // TOP
    source = jnp.zeros((experts * capacity,), jnp.int32).at[target].set(owner_row)
    filled = jnp.zeros((experts * capacity,), jnp.bool_).at[target].set(True)
    outgoing = jnp.where(filled[:, None], normed[source], jnp.zeros((), jnp.bfloat16))
    outgoing = outgoing.reshape(row_experts, seq_count, capacity, -1)
    arrived = lax.all_to_all(outgoing, "seq", split_axis=1, concat_axis=1, tiled=True)
    copies = jnp.repeat(arrived, SPLIT, axis=0)
    block = lax.all_to_all(copies, "exp", split_axis=0, concat_axis=0, tiled=True)
    flat_rows = block.reshape(-1, block.shape[-1])
    contract = (((1,), (1,)), ((), ()))
    gate_val = lax.dot_general(
        flat_rows, expert_gate[0], contract, preferred_element_type=jnp.float32
    )
    up_val = lax.dot_general(flat_rows, expert_up[0], contract, preferred_element_type=jnp.float32)
    activated = (jax.nn.silu(gate_val) * up_val).astype(jnp.bfloat16)
    piece_out = jnp.dot(activated, expert_down[0], preferred_element_type=jnp.float32).astype(
        jnp.bfloat16
    )
    piece_out = piece_out.reshape(block.shape)
    returned = lax.all_to_all(
        lax.all_to_all(piece_out, "seq", split_axis=1, concat_axis=1, tiled=True),
        "exp",
        split_axis=0,
        concat_axis=0,
        tiled=True,
    )
    summed = jnp.sum(
        returned.reshape(row_experts, SPLIT, seq_count, capacity, -1).astype(jnp.float32), axis=1
    )
    results = summed.reshape(experts * capacity, -1)[target]
    expert_sum = jnp.sum(
        (results * route_weight.reshape(-1)[:, None]).reshape(row_count, TOP, -1), axis=1
    )
    return (stream.astype(jnp.float32) + expert_sum).astype(jnp.bfloat16)


def solution(mesh):
    return jax.shard_map(
        shards,
        mesh=mesh,
        in_specs=(
            P("seq", "exp"),
            P("seq", "exp"),
            P("seq", None),
            P("seq", None),
            P("exp", "seq"),
            P("exp", "seq"),
            P("exp"),
            P("exp", None),
            P(("seq", "exp"), None),
            P(),
            P(("seq", "exp"), None),
            P(("seq", "exp"), None),
            P(("seq", "exp"), None, None),
            P(("seq", "exp"), None, None),
            P(("seq", "exp"), None, None),
        ),
        out_specs=P(("seq", "exp"), None),
        check_vma=False,
    )
```

profile of v0, /device:TPU:1, one launch (start us, length us, event | category | flops | bytes accessed | tf_op | source)
XLA Modules:
  0.0 738.1 jit_solution(7842727586102235308)
XLA Ops:
  6.5 0.9 reshape.254
  7.4 4.8 reduce-window.14
  12.3 0.1 copy.65
  12.5 0.1 copy.66
  12.6 0.1 broadcast_add_fusion
  12.7 0.3 copy.67
  13.0 0.8 copy-done.6
  13.8 2.0 reshape.309
  15.8 0.5 copy.72
  16.5 1.3 fusion.29
  17.8 3.1 while.26
  17.8 0.7 bitcast_dynamic-update-slice_fusion.2
  18.6 0.7 bitcast_dynamic-update-slice_fusion.2
  19.4 0.7 bitcast_dynamic-update-slice_fusion.2
  20.2 0.7 bitcast_dynamic-update-slice_fusion.2
  20.8 0.1 bitcast_add_fusion.2
  20.9 0.6 convert_element_type.96
  21.7 0.6 dynamic-slice
  23.0 0.2 dynamic-update-slice
  23.2 34.3 %all-reduce = bf16[64]{0:T(256)(128)(2,1)S(1)} all-reduce(bf16[64]{0:T(256)(128)(2,1)S(1)} %dynamic-update-slice), channel_id=2, replica_groups=mesh['seq'=16,'exp'=16] {'seq'}, use_global_device_ids=true, to_apply=%add | all-reduce | flops 64 | bytes 256
  57.5 0.1 reshape.299
  57.6 2.1 copy.77
  59.7 0.7 subtract_exponential_fusion
  60.4 0.3 fusion.58
  60.7 1.4 fusion.14
  62.1 9.7 %all-gather.4.cloned.1.call-done = bf16[64,64,128]{2,1,0:T(8,128)(2,1)} async-done(((bf16[4,64,128]{2,1,0:T(8,128)(2,1)}), bf16[64,64,128]{2,1,0:T(8,128)(2,1)}) %all-gather.4.cloned.1.call-update) | async-done | bytes 1048592 | tf_op jit(solution)/shard_map/all_gather | solution.py:16
  71.9 1.9 fusion.17
  73.8 0.7 copy.76
  74.5 0.2 copy.98
  74.7 3.3 convolution_convert_fusion.1
  78.1 0.7 copy-done.10
  78.7 0.1 copy.78
  78.8 0.1 eq.31
  78.9 0.1 eq.27
  79.1 0.1 reshape.259
  79.3 0.9 reduce-window.16
  80.2 0.2 slice_reduce_fusion
  80.4 0.1 fusion.39
  80.6 2.9 scatter_custom_fusion.1
  83.5 2.1 scatter_custom_fusion
  85.7 0.1 broadcast_in_dim.75
  85.8 66.6 %reduce-scatter.2.cloned.1.call-done = bf16[64,2048]{1,0:T(8,128)(2,1)} async-done(((bf16[1024,2048]{1,0:T(8,128)(2,1)}), bf16[64,2048]{1,0:T(8,128)(2,1)}) %reduce-scatter.2.cloned.1.call-update) | async-done | bytes 262160 | tf_op jit(solution)/shard_map/reduce_scatter | solution.py:105
  152.5 1.1 fusion.24
  153.6 1.1 fusion.26
  154.7 3.3 gather_fusion
  158.0 1.8 copy_select_fusion
  159.8 29.3 %all_to_all.20 = bf16[4,16,8,2048]{3,2,0,1:T(8,128)(2,1)S(1)} all-to-all(bf16[4,16,8,2048]{3,2,0,1:T(8,128)(2,1)S(1)} %copy_select_fusion), channel_id=1, replica_groups=mesh['seq'=16,'exp'=16] {'seq'}, dimensions={1} | all-to-all | bytes 4194304 | tf_op jit(solution)/shard_map/all_to_all | solution.py:137
  189.2 0.2 copy.84
  189.4 1.1 broadcast_in_dim.79
  190.5 198.7 %all_to_all.21 = bf16[16,16,8,2048]{3,2,1,0:T(8,128)(2,1)S(1)} all-to-all(bf16[16,16,8,2048]{3,2,1,0:T(8,128)(2,1)S(1)} %bitcast.116), channel_id=1, replica_groups=mesh['seq'=16,'exp'=16] {'exp'}, dimensions={0} | all-to-all | bytes 16777216 | tf_op jit(solution)/shard_map/all_to_all | solution.py:139
  389.2 3.2 fusion.12
  392.5 3.5 fusion.2
  396.0 6.8 convolution_convert_fusion
  402.8 8.3 %copy.85 = bf16[16,16,8,2048]{3,2,0,1:T(8,128)(2,1)} copy(bf16[16,16,8,2048]{3,2,1,0:T(8,128)(2,1)} %bitcast.120) | data formatting | bytes 16777216 | tf_op jit(solution)/shard_map/reshape | solution.py:150
  411.1 100.0 %all_to_all.22 = bf16[16,16,8,2048]{3,2,0,1:T(8,128)(2,1)} all-to-all(bf16[16,16,8,2048]{3,2,0,1:T(8,128)(2,1)} %copy.85), channel_id=1, replica_groups=mesh['seq'=16,'exp'=16] {'seq'}, dimensions={1} | all-to-all | bytes 16777216 | tf_op jit(solution)/shard_map/all_to_all | solution.py:152
  511.1 8.3 %copy.86 = bf16[16,16,8,2048]{3,2,1,0:T(8,128)(2,1)} copy(bf16[16,16,8,2048]{3,2,0,1:T(8,128)(2,1)} %all_to_all.22) | data formatting | bytes 16777216 | tf_op jit(solution)/shard_map/all_to_all | solution.py:152
  519.4 4.8 all-to-all-start.3
  524.2 0.1 copy.89
  524.3 182.6 %all-to-all-done.3 = bf16[16,16,8,2048]{3,2,1,0:T(8,128)(2,1)} async-done(((bf16[16,16,8,2048]{3,2,1,0:T(8,128)(2,1)}), bf16[16,16,8,2048]{3,2,1,0:T(8,128)(2,1)}, u32[]{:S(2)}, u32[]{:S(2)}) %all-to-all-start.3) | async-done | bytes 8388640 | tf_op jit(solution)/shard_map/all_to_all | solution.py:151
  706.9 7.8 %convert_reduce_fusion = f32[4,16,8,2048]{3,2,1,0:T(8,128)} fusion(bf16[16,16,8,2048]{3,2,1,0:T(8,128)(2,1)} %all-to-all-done.3), kind=kLoop, calls=%fused_computation.11 | loop fusion | flops 7340032 | bytes 12582912 | tf_op jit(solution)/shard_map/reduce_sum | solution.py:158
  714.7 7.3 gather_fusion.1
  722.0 4.7 gather.13
  726.7 3.8 multiply_reduce_fusion
  730.5 0.8 fusion.27
  (69 shorter events, 0.9 us)
Async XLA Ops:
  6.5 389.5 %copy-start = (bf16[1,352,2048]{2,1,0:T(8,128)(2,1)S(1)}, bf16[1,352,2048]{2,1,0:T(8,128)(2,1)}, u32[]{:S(2)}) copy-start(bf16[1,352,2048]{2,1,0:T(8,128)(2,1)} %param.33) | copy-start | bytes 4325380
  6.5 9.8 %copy-start.8 = (f32[4,1024]{1,0:T(4,128)S(1)}, f32[4,1024]{1,0:T(4,128)}, u32[]{:S(2)}) copy-start(f32[4,1024]{1,0:T(4,128)} %param.23) | copy-start | bytes 49156
  6.5 65.3 %all-gather.4.cloned.1.call-start = ((), (), s32[]{:S(2)}) async-start(), calls=%async_computation.6 | async-start | bytes 1114112 | tf_op jit(solution)/shard_map/all_gather | solution.py:16
  13.0 0.8 copy-start.6
  15.8 5.9 copy-start.16
  16.5 43.9 %copy-start.4 = (bf16[1024,128]{1,0:T(8,128)(2,1)S(1)}, bf16[1024,128]{1,0:T(8,128)(2,1)}, u32[]{:S(2)}) copy-start(bf16[1024,128]{1,0:T(8,128)(2,1)} %param.22) | copy-start | bytes 786436
  16.5 43.9 %copy-start.5 = (bf16[1024,128]{1,0:T(8,128)(2,1)S(1)}, bf16[1024,128]{1,0:T(8,128)(2,1)}, u32[]{:S(2)}) copy-start(bf16[1024,128]{1,0:T(8,128)(2,1)} %param.21) | copy-start | bytes 786436
  21.6 130.9 %reduce-scatter.2.cloned.1.call-start = ((), (), s32[]{:S(2)}) async-start(), calls=%async_computation.5 | async-start | bytes 4456448 | tf_op jit(solution)/shard_map/reduce_scatter | solution.py:105
  60.7 11.2 %copy-start.12 = (f32[4]{0:T(128)S(1)}, f32[4]{0:T(128)}, u32[]{:S(2)}) copy-start(f32[4]{0:T(128)} %param.25) | copy-start | bytes 52
  71.9 2.8 copy-start.7
  71.9 2.8 copy-start.15
  78.0 0.7 copy-start.10
  78.0 74.4 %copy-start.2 = (bf16[64,2048]{1,0:T(8,128)(2,1)S(1)}, bf16[64,2048]{1,0:T(8,128)(2,1)}, u32[]{:S(2)}) copy-start(bf16[64,2048]{1,0:T(8,128)(2,1)} %param.27) | copy-start | bytes 786436
  78.0 75.6 %copy-start.9 = (f32[2048]{0:T(1024)S(1)}, f32[2048]{0:T(1024)}, u32[]{:S(2)}) copy-start(f32[2048]{0:T(1024)} %param.28) | copy-start | bytes 24580
  190.5 198.7 %copy-start.13 = (bf16[1,352,2048]{2,1,0:T(8,128)(2,1)S(1)}, bf16[1,352,2048]{2,1,0:T(8,128)(2,1)}, u32[]{:S(2)}) copy-start(bf16[1,352,2048]{2,1,0:T(8,128)(2,1)} %param.31) | copy-start | bytes 4325380
  389.2 3.2 copy-start.14
  519.4 4.8 copy-start.11
  519.4 187.5 %all-to-all-start.3 = ((bf16[16,16,8,2048]{3,2,1,0:T(8,128)(2,1)}), bf16[16,16,8,2048]{3,2,1,0:T(8,128)(2,1)}, u32[]{:S(2)}, u32[]{:S(2)}) async-start(bf16[16,16,8,2048]{3,2,1,0:T(8,128)(2,1)} %copy.86), calls=%async_computation.4 | async-start | bytes 16777216 | tf_op jit(solution)/shard_map/all_to_all | solution.py:151
  722.0 9.3 %copy-start.1 = (bf16[1,352,2048]{2,1,0:T(8,128)(2,1)S(1)}, bf16[1,352,2048]{2,1,0:T(8,128)(2,1)}, u32[]{:S(2)}) copy-start(bf16[1,352,2048]{2,1,0:T(8,128)(2,1)} %param.33) | copy-start | bytes 4325380
  726.7 3.8 copy-start.3
Sparse Core Ops, SparseCore 0:
  21.7 50.0 all-gather.3
  78.2 74.2 reduce-scatter.1
where the time goes:
time: 740 us; the launch traced here: 738 us
  blocking collectives  362 us (49%)
  waiting for transfers between devices  259 us (35%)
  local copies, waits for them, and re-layouts  48.7 us (7%)
  other arithmetic  26.9 us (4%)
  matrix products  21.7 us (3%)
  between operations  14.5 us (2%)
    all_to_all x1, blocking collectives, shards(): lax.all_to_all(copies, 'exp', split_axis=0, concat_axis=0, tiled=True)  199 us
    all_to_all x1, waiting for transfers between devices, shards(): lax.all_to_all(lax.all_to_all(piece_out, 'seq', split_axis=1, concat_axis...  183 us
    all_to_all x1, blocking collectives, shards(): lax.all_to_all(piece_out, 'seq', split_axis=1, concat_axis=1, tiled=True)  100 us
    reduce_scatter x1, waiting for transfers between devices, shards(): lax.psum_scatter(jnp.dot(gated_out, out_weight, preferred_element_type=jn...  66.6 us
    unnamed x1, blocking collectives  34.3 us
    all_to_all x1, blocking collectives, shards(): lax.all_to_all(outgoing, 'seq', split_axis=1, concat_axis=1, tiled=True)  29.3 us
  transfers between devices with their start and end apart: 3, of which 3 were waited for; matrix products, arithmetic and copies ran while one was open for 2% of the time, Pallas kernels for 0%

commit v1 on v0

--- a/solution.py
+++ b/solution.py
@@ -1,25 +1,31 @@
 import jax
 import jax.numpy as jnp
 from jax import lax
-from jax.sharding import PartitionSpec as P
+from jax.sharding import Mesh, PartitionSpec as P
 
 HEAD_DIM = 64
 STATE = 128
 TOP = 6
 SPLIT = 4
 STRETCH = 256
+EXP = ("eh", "pz", "c")
 
 
 def prefix(shard, axis, join, neutral):
     place = lax.axis_index(axis)
-    gathered = jax.tree.map(
-        lambda a, kind: lax.all_gather(a.astype(kind), axis), shard, (jnp.bfloat16, jnp.bfloat16)
+    decay, state = shard
+    packed = jnp.concatenate(
+        [state.reshape(state.shape[0], -1), jnp.broadcast_to(decay[:, None], (decay.shape[0], STATE))],
+        axis=1,
     )
-    state = jax.tree.map(lambda a, e: jnp.zeros_like(a) + jnp.asarray(e, a.dtype), shard, neutral)
+    gathered = lax.all_gather(packed.astype(jnp.bfloat16), axis)
+    cut = state.shape[1] * state.shape[2]
+    gathered = (gathered[:, :, cut], gathered[:, :, :cut].reshape((-1,) + state.shape))
+    start = jax.tree.map(lambda a, e: jnp.zeros_like(a) + jnp.asarray(e, a.dtype), shard, neutral)
 
-    def one(turn, state):
+    def one(turn, carry):
         return join(
-            state,
+            carry,
             jax.tree.map(
                 lambda a, own: lax.dynamic_index_in_dim(a, turn, 0, False).astype(own.dtype),
                 gathered,
@@ -27,7 +33,7 @@
             ),
         )
 
-    return lax.fori_loop(0, place, one, state)
+    return lax.fori_loop(0, place, one, start)
 
 
 def join_states(earlier, later_part):
@@ -104,7 +110,7 @@
     row_count = residual.shape[0]
     mixer_out = lax.psum_scatter(
         jnp.dot(gated_out, out_weight, preferred_element_type=jnp.float32).astype(jnp.bfloat16),
-        "exp",
+        EXP,
         scatter_dimension=0,
         tiled=True,
     ).astype(jnp.float32)
@@ -114,7 +120,7 @@
         widened * lax.rsqrt(jnp.mean(widened * widened, axis=-1, keepdims=True) + 1e-06) * norm_gain
     ).astype(jnp.bfloat16)
     seq_count = lax.axis_size("seq")
-    exp_count = lax.axis_size("exp")
+    exp_count = lax.axis_size(EXP)
     row_experts = exp_count // SPLIT
     experts = seq_count * row_experts
     capacity = min(row_count, max(2, (4 * TOP * row_count + 3 * experts - 1) // (3 * experts)))
@@ -135,8 +141,9 @@
     outgoing = jnp.where(filled[:, None], normed[source], jnp.zeros((), jnp.bfloat16))
     outgoing = outgoing.reshape(row_experts, seq_count, capacity, -1)
     arrived = lax.all_to_all(outgoing, "seq", split_axis=1, concat_axis=1, tiled=True)
-    copies = jnp.repeat(arrived, SPLIT, axis=0)
-    block = lax.all_to_all(copies, "exp", split_axis=0, concat_axis=0, tiled=True)
+    arrived = lax.all_to_all(arrived, "eh", split_axis=0, concat_axis=0, tiled=True)
+    block = lax.all_gather(arrived, "pz")
+    block = lax.all_gather(block, "c")
     flat_rows = block.reshape(-1, block.shape[-1])
     contract = (((1,), (1,)), ((), ()))
     gate_val = lax.dot_general(
@@ -148,16 +155,11 @@
         jnp.bfloat16
     )
     piece_out = piece_out.reshape(block.shape)
-    returned = lax.all_to_all(
-        lax.all_to_all(piece_out, "seq", split_axis=1, concat_axis=1, tiled=True),
-        "exp",
-        split_axis=0,
-        concat_axis=0,
-        tiled=True,
-    )
-    summed = jnp.sum(
-        returned.reshape(row_experts, SPLIT, seq_count, capacity, -1).astype(jnp.float32), axis=1
-    )
+    piece_sum = lax.psum_scatter(piece_out, "c", scatter_dimension=0, tiled=True)[0]
+    piece_sum = lax.psum_scatter(piece_sum, "pz", scatter_dimension=0, tiled=True)[0]
+    returned = lax.all_to_all(piece_sum, "eh", split_axis=0, concat_axis=0, tiled=True)
+    returned = lax.all_to_all(returned, "seq", split_axis=1, concat_axis=1, tiled=True)
+    summed = returned.astype(jnp.float32)
     results = summed.reshape(experts * capacity, -1)[target]
     expert_sum = jnp.sum(
         (results * route_weight.reshape(-1)[:, None]).reshape(row_count, TOP, -1), axis=1
@@ -166,26 +168,29 @@
 
 
 def solution(mesh):
+    seq_n = mesh.shape["seq"]
+    exp_n = mesh.shape["exp"]
+    grid = Mesh(mesh.devices.reshape(seq_n, exp_n // SPLIT, 2, SPLIT // 2), ("seq",) + EXP)
     return jax.shard_map(
         shards,
-        mesh=mesh,
+        mesh=grid,
         in_specs=(
-            P("seq", "exp"),
-            P("seq", "exp"),
+            P("seq", EXP),
+            P("seq", EXP),
             P("seq", None),
             P("seq", None),
-            P("exp", "seq"),
-            P("exp", "seq"),
-            P("exp"),
-            P("exp", None),
-            P(("seq", "exp"), None),
+            P(EXP, "seq"),
+            P(EXP, "seq"),
+            P(EXP),
+            P(EXP, None),
+            P(("seq",) + EXP, None),
             P(),
-            P(("seq", "exp"), None),
-            P(("seq", "exp"), None),
-            P(("seq", "exp"), None, None),
-            P(("seq", "exp"), None, None),
-            P(("seq", "exp"), None, None),
+            P(("seq",) + EXP, None),
+            P(("seq",) + EXP, None),
+            P(("seq",) + EXP, None, None),
+            P(("seq",) + EXP, None, None),
+            P(("seq",) + EXP, None, None),
         ),
-        out_specs=P(("seq", "exp"), None),
+        out_specs=P(("seq",) + EXP, None),
         check_vma=False,
     )

time: 740 us -> 561 us (0.76)
  the two profiles are of different devices: /device:TPU:1 before, /device:TPU:32 now
where the time goes in v1:
time: 561 us; the launch traced here: 559 us
  waiting for transfers between devices  308 us (55%)
  blocking collectives  147 us (26%)
  local copies, waits for them, and re-layouts  38.7 us (7%)
  matrix products  25.2 us (4%)
  other arithmetic  19.2 us (3%)
  between operations  13.9 us (2%)
  starting transfers between devices  7.15 us (1%)
    reduce_scatter x1, waiting for transfers between devices, shards(): lax.psum_scatter(jnp.dot(gated_out, out_weight, preferred_element_type=jn...  65 us
    reduce_scatter x1, waiting for transfers between devices, shards(): lax.psum_scatter(piece_sum, 'pz', scatter_dimension=0, tiled=True)[0]  62 us
    all_to_all x1, blocking collectives, shards(): lax.all_to_all(piece_sum, 'eh', split_axis=0, concat_axis=0, tiled=True)  57.6 us
    all_gather x1, waiting for transfers between devices, shards(): block = lax.all_gather(arrived, 'pz')  56 us
    all_to_all x1, blocking collectives, shards(): lax.all_to_all(arrived, 'eh', split_axis=0, concat_axis=0, tiled=True)  54.9 us
    all_gather x1, waiting for transfers between devices, prefix(): gathered = lax.all_gather(packed.astype(jnp.bfloat16), axis)  44.9 us
    all_to_all x1, blocking collectives, shards(): lax.all_to_all(outgoing, 'seq', split_axis=1, concat_axis=1, tiled=True)  34.2 us
    all_gather x1, waiting for transfers between devices, shards(): block = lax.all_gather(block, 'c')  28.5 us
  transfers between devices with their start and end apart: 7, of which 7 were waited for; matrix products, arithmetic and copies ran while one was open for 2% of the time, Pallas kernels for 0%

profile of v1, /device:TPU:32, one launch (start us, length us, event | category | flops | bytes accessed | tf_op | source)
XLA Modules:
  0.0 559.2 jit_solution(7416483822542595895)
XLA Ops:
  6.6 0.9 reshape.282
  7.4 4.8 reduce-window.14
  12.3 0.1 copy.74
  12.5 0.1 copy.75
  12.7 0.3 copy.76
  13.0 0.8 copy-done.7
  13.8 2.0 reshape.335
  15.8 0.5 copy.81
  16.5 0.3 fusion.29
  16.8 3.1 while.26
  16.8 0.7 bitcast_dynamic-update-slice_fusion.2
  17.6 0.7 bitcast_dynamic-update-slice_fusion.2
  18.4 0.7 bitcast_dynamic-update-slice_fusion.2
  19.2 0.7 bitcast_dynamic-update-slice_fusion.2
  20.1 0.7 pad_maximum_fusion
  20.9 2.0 copy.88
  23.0 0.7 subtract_exponential_fusion
  23.7 0.3 fusion.58
  24.0 2.5 fusion.14
  26.4 44.9 %all-gather.6.cloned.1.call-done = bf16[16,4,8320]{2,1,0:T(4,128)(2,1)} async-done(((bf16[1,4,8320]{2,1,0:T(4,128)(2,1)}), bf16[16,4,8320]{2,1,0:T(4,128)(2,1)}) %all-gather.6.cloned.1.call-update) | async-done | bytes 1064976 | tf_op jit(solution)/shard_map/all_gather | solution.py:21
  71.3 1.6 slice.37
  73.0 1.9 reshape.286
  74.9 0.1 copy.85
  75.0 0.1 copy.86
  75.1 2.1 fusion.17
  77.3 0.7 copy.87
  78.0 0.2 copy.106
  78.2 0.1 copy-done.8
  78.3 0.3 copy-done.18
  78.7 3.3 convolution_convert_fusion.1
  82.0 0.6 copy-done.12
  82.8 0.1 eq.31
  82.9 0.1 eq.27
  83.0 0.1 reshape.288
  83.2 0.9 reduce-window.16
  84.1 0.2 slice_reduce_fusion
  84.4 0.1 fusion.39
  84.5 2.9 scatter_custom_fusion.1
  87.5 2.1 scatter_custom_fusion
  89.8 65.0 %reduce-scatter.4.cloned.1.call-done = bf16[64,2048]{1,0:T(8,128)(2,1)} async-done(((bf16[1024,2048]{1,0:T(8,128)(2,1)}), bf16[64,2048]{1,0:T(8,128)(2,1)}) %reduce-scatter.4.cloned.1.call-update) | async-done | bytes 262160 | tf_op jit(solution)/shard_map/reduce_scatter | solution.py:111
  154.7 1.1 fusion.24
  155.9 1.1 fusion.26
  157.0 3.3 gather_fusion
  160.3 1.8 copy_select_fusion
  162.1 34.2 %all_to_all.20 = bf16[4,16,8,2048]{3,2,0,1:T(8,128)(2,1)S(1)} all-to-all(bf16[4,16,8,2048]{3,2,0,1:T(8,128)(2,1)S(1)} %copy_select_fusion), channel_id=1, replica_groups=mesh['seq'=16,'eh'=4,'pz'=2,'c'=2] {'seq'}, dimensions={1} | all-to-all | bytes 4194304 | tf_op jit(solution)/shard_map/all_to_all | solution.py:143
  196.3 0.1 copy.95
  196.4 54.9 %all_to_all.21 = bf16[4,16,8,2048]{3,2,1,0:T(8,128)(2,1)} all-to-all(bf16[4,16,8,2048]{3,2,1,0:T(8,128)(2,1)S(1)} %copy.95), channel_id=1, replica_groups=mesh['seq'=16,'eh'=4,'pz'=2,'c'=2] {'eh'}, dimensions={0} | all-to-all | bytes 4194304 | tf_op jit(solution)/shard_map/all_to_all | solution.py:144
  251.3 56.0 %all-gather.8.cloned.1.call-done = bf16[8,16,8,2048]{3,2,1,0:T(8,128)(2,1)} async-done(((bf16[4,16,8,2048]{3,2,1,0:T(8,128)(2,1)}), bf16[8,16,8,2048]{3,2,1,0:T(8,128)(2,1)}) %all-gather.8.cloned.1.call-update) | async-done | bytes 4194320 | tf_op jit(solution)/shard_map/all_gather | solution.py:145
  307.4 28.5 %all-gather.10.cloned.1.call-done = bf16[4,4,16,8,2048]{4,3,2,1,0:T(8,128)(2,1)} async-done(((bf16[2,4,16,8,2048]{4,3,2,1,0:T(8,128)(2,1)}), bf16[4,4,16,8,2048]{4,3,2,1,0:T(8,128)(2,1)}) %all-gather.10.cloned.1.call-update) | async-done | bytes 8388624 | tf_op jit(solution)/shard_map/all_gather | solution.py:146
  335.9 6.3 %fusion.12 = f32[2048,352]{0,1:T(8,128)S(1)} fusion(bf16[2048,2048]{1,0:T(8,128)(2,1)} %bitcast.132, bf16[1,352,2048]{2,1,0:T(8,128)(2,1)S(1)} %copy-done.16), kind=kOutput, calls=%fused_computation.27 | convolution fusion | flops 2952790016 | bytes 12713984 | tf_op jit(solution)/shard_map/dot_general | solution.py:149
  342.3 3.5 fusion.2
  345.8 6.9 %convolution_convert_fusion = bf16[2048,2048]{1,0:T(8,128)(2,1)} fusion(bf16[2048,352]{0,1:T(8,128)(2,1)S(1)} %fusion.2, bf16[1,352,2048]{2,1,0:T(8,128)(2,1)S(1)} %copy-done), kind=kOutput, calls=%fused_computation.11 | convolution fusion | flops 2956984320 | bytes 11272192 | tf_op jit(solution)/shard_map/dot_general | solution.py:154
  352.8 23.6 %reduce-scatter.6.cloned.1.call-done = bf16[1,2,4,16,8,2048]{5,4,3,2,1,0:T(8,128)(2,1)} async-done(((bf16[2,2,4,16,8,2048]{5,4,3,2,1,0:T(8,128)(2,1)}), bf16[1,2,4,16,8,2048]{5,4,3,2,1,0:T(8,128)(2,1)}) %reduce-scatter.6.cloned.1.call-update) | async-done | bytes 4194320 | tf_op jit(solution)/shard_map/reduce_scatter | solution.py:158
  376.4 62.0 %reduce-scatter.8.cloned.1.call-done = bf16[1,4,16,8,2048]{4,3,2,1,0:T(8,128)(2,1)} async-done(((bf16[2,4,16,8,2048]{4,3,2,1,0:T(8,128)(2,1)}), bf16[1,4,16,8,2048]{4,3,2,1,0:T(8,128)(2,1)}) %reduce-scatter.8.cloned.1.call-update) | async-done | bytes 2097168 | tf_op jit(solution)/shard_map/reduce_scatter | solution.py:159
  438.4 57.6 %all_to_all.22 = bf16[4,16,8,2048]{3,2,1,0:T(8,128)(2,1)S(1)} all-to-all(bf16[4,16,8,2048]{3,2,1,0:T(8,128)(2,1)} %bitcast.119), channel_id=1, replica_groups=mesh['seq'=16,'eh'=4,'pz'=2,'c'=2] {'eh'}, dimensions={0} | all-to-all | bytes 4194304 | tf_op jit(solution)/shard_map/all_to_all | solution.py:160
  496.0 1.5 copy.96
  497.5 6.9 %all-to-all-start.3 = ((bf16[4,16,8,2048]{3,2,0,1:T(8,128)(2,1)}), bf16[4,16,8,2048]{3,2,0,1:T(8,128)(2,1)S(1)}, u32[]{:S(2)}, u32[]{:S(2)}) async-start(bf16[4,16,8,2048]{3,2,0,1:T(8,128)(2,1)} %copy.96), calls=%async_computation.6 | async-start | bytes 4194304 | tf_op jit(solution)/shard_map/all_to_all | solution.py:161
  504.5 0.7 copy.98
  505.2 28.2 %all-to-all-done.3 = bf16[4,16,8,2048]{3,2,0,1:T(8,128)(2,1)S(1)} async-done(((bf16[4,16,8,2048]{3,2,0,1:T(8,128)(2,1)}), bf16[4,16,8,2048]{3,2,0,1:T(8,128)(2,1)S(1)}, u32[]{:S(2)}, u32[]{:S(2)}) %all-to-all-start.3) | async-done | bytes 2097184 | tf_op jit(solution)/shard_map/all_to_all | solution.py:161
  533.3 2.5 copy.97
  535.8 7.3 %gather_fusion.1 = f32[384,2048]{1,0:T(8,128)} fusion(f32[512,2048]{1,0:T(8,128)} %bitcast.113, s32[1024]{0:T(1024)S(1)} %pad_clamp_fusion), kind=kCustom, calls=%fused_computation.1 | custom fusion | bytes 6292992 | tf_op jit(solution)/shard_map/gather | solution.py:163
  543.1 4.6 gather.13
  547.7 3.8 multiply_reduce_fusion
  551.5 0.8 fusion.27
  (87 shorter events, 1.6 us)
Async XLA Ops:
  6.5 339.3 %copy-start = (bf16[1,352,2048]{2,1,0:T(8,128)(2,1)S(1)}, bf16[1,352,2048]{2,1,0:T(8,128)(2,1)}, u32[]{:S(2)}) copy-start(bf16[1,352,2048]{2,1,0:T(8,128)(2,1)} %param.33) | copy-start | bytes 4325380
  6.5 9.9 %copy-start.10 = (f32[4,1024]{1,0:T(4,128)S(1)}, f32[4,1024]{1,0:T(4,128)}, u32[]{:S(2)}) copy-start(f32[4,1024]{1,0:T(4,128)} %param.23) | copy-start | bytes 49156
  6.5 9.9 %copy-start.5 = (bf16[1024,128]{1,0:T(8,128)(2,1)S(1)}, bf16[1024,128]{1,0:T(8,128)(2,1)}, u32[]{:S(2)}) copy-start(bf16[1024,128]{1,0:T(8,128)(2,1)} %param.21) | copy-start | bytes 786436
  6.5 64.8 %all-gather.6.cloned.1.call-start = ((), (), s32[]{:S(2)}) async-start(), calls=%async_computation.7 | async-start | bytes 1131520 | tf_op jit(solution)/shard_map/all_gather | solution.py:21
  13.0 0.8 copy-start.7
  16.8 6.9 %copy-start.4 = (bf16[1024,128]{1,0:T(8,128)(2,1)S(1)}, bf16[1024,128]{1,0:T(8,128)(2,1)}, u32[]{:S(2)}) copy-start(bf16[1024,128]{1,0:T(8,128)(2,1)} %param.22) | copy-start | bytes 786436
  16.8 6.8 %copy-start.6 = (bf16[1024,128]{1,0:T(8,128)(2,1)S(1)}, bf16[1024,128]{1,0:T(8,128)(2,1)}, u32[]{:S(2)}) copy-start(bf16[1024,128]{1,0:T(8,128)(2,1)} %param.21) | copy-start | bytes 786436
  20.8 134.0 %reduce-scatter.4.cloned.1.call-start = ((), (), s32[]{:S(2)}) async-start(), calls=%async_computation.8 | async-start | bytes 4456448 | tf_op jit(solution)/shard_map/reduce_scatter | solution.py:111
  26.4 48.7 %copy-start.14 = (f32[4]{0:T(128)S(1)}, f32[4]{0:T(128)}, u32[]{:S(2)}) copy-start(f32[4]{0:T(128)} %param.25) | copy-start | bytes 52
  71.3 3.6 slice-start
  77.3 1.0 copy-start.8
  77.3 1.4 copy-start.18
  82.0 0.7 copy-start.12
  82.0 72.8 %copy-start.1 = (bf16[64,2048]{1,0:T(8,128)(2,1)S(1)}, bf16[64,2048]{1,0:T(8,128)(2,1)}, u32[]{:S(2)}) copy-start(bf16[64,2048]{1,0:T(8,128)(2,1)} %param.27) | copy-start | bytes 786436
  82.0 73.9 %copy-start.11 = (f32[2048]{0:T(1024)S(1)}, f32[2048]{0:T(1024)}, u32[]{:S(2)}) copy-start(f32[2048]{0:T(1024)} %param.28) | copy-start | bytes 24580
  82.0 225.3 %all-gather.8.cloned.1.call-start = ((), (), s32[]{:S(2)}) async-start(), calls=%async_computation.11 | async-start | bytes 6291456 | tf_op jit(solution)/shard_map/all_gather | solution.py:145
  251.3 84.7 %copy-start.16 = (bf16[1,352,2048]{2,1,0:T(8,128)(2,1)S(1)}, bf16[1,352,2048]{2,1,0:T(8,128)(2,1)}, u32[]{:S(2)}) copy-start(bf16[1,352,2048]{2,1,0:T(8,128)(2,1)} %param.31) | copy-start | bytes 4325380
  251.3 84.6 %all-gather.10.cloned.1.call-start = ((), (), s32[]{:S(2)}) async-start(), calls=%async_computation.12 | async-start | bytes 12582912 | tf_op jit(solution)/shard_map/all_gather | solution.py:146
  307.4 69.0 %reduce-scatter.6.cloned.1.call-start = ((), (), s32[]{:S(2)}) async-start(), calls=%async_computation.9 | async-start | bytes 12582912 | tf_op jit(solution)/shard_map/reduce_scatter | solution.py:158
  335.9 6.4 %copy-start.15 = (bf16[4,4,16,8,2048]{4,3,2,1,0:T(8,128)(2,1)S(1)}, bf16[4,4,16,8,2048]{4,3,2,1,0:T(8,128)(2,1)}, u32[]{:S(2)}) copy-start(bf16[4,4,16,8,2048]{4,3,2,1,0:T(8,128)(2,1)} %all-gather.10.cloned.1.call-done) | copy-start | bytes 25165828
  335.9 6.4 %copy-start.17 = (bf16[1,352,2048]{2,1,0:T(8,128)(2,1)S(1)}, bf16[1,352,2048]{2,1,0:T(8,128)(2,1)}, u32[]{:S(2)}) copy-start(bf16[1,352,2048]{2,1,0:T(8,128)(2,1)} %param.32) | copy-start | bytes 4325380
  352.7 85.7 %reduce-scatter.8.cloned.1.call-start = ((), (), s32[]{:S(2)}) async-start(), calls=%async_computation.10 | async-start | bytes 6291456 | tf_op jit(solution)/shard_map/reduce_scatter | solution.py:159
  497.5 7.0 %copy-start.13 = (f32[64,6]{0,1:T(8,128)S(1)}, f32[64,6]{0,1:T(8,128)}, u32[]{:S(2)}) copy-start(f32[64,6]{0,1:T(8,128)} %param.30) | copy-start | bytes 4612
  497.5 35.8 %all-to-all-start.3 = ((bf16[4,16,8,2048]{3,2,0,1:T(8,128)(2,1)}), bf16[4,16,8,2048]{3,2,0,1:T(8,128)(2,1)S(1)}, u32[]{:S(2)}, u32[]{:S(2)}) async-start(bf16[4,16,8,2048]{3,2,0,1:T(8,128)(2,1)} %copy.96), calls=%async_computation.6 | async-start | bytes 4194304 | tf_op jit(solution)/shard_map/all_to_all | solution.py:161
  543.1 4.6 copy-start.9
  547.7 3.8 copy-start.2
  547.7 3.8 copy-start.3
Sparse Core Ops, SparseCore 0:
  20.9 50.4 all-gather.5
  82.1 72.5 reduce-scatter.3
  251.4 55.8 all-gather.7
  309.0 26.8 all-gather.9
  352.9 23.4 reduce-scatter.5
  379.0 59.4 reduce-scatter.7

commit v2 on v1

--- a/solution.py
+++ b/solution.py
@@ -9,6 +9,26 @@
 SPLIT = 4
 STRETCH = 256
 EXP = ("eh", "pz", "c")
+JOINT = True
+PZ_SWAP = True
+C_SWAP = True
+MIX_TWO = True
+
+
+def pair_swap(x, axis):
+    return lax.ppermute(x, axis, perm=[(0, 1), (1, 0)])
+
+
+def pair_gather(x, axis, swap):
+    if swap:
+        return jnp.stack([x, pair_swap(x, axis)])
+    return lax.all_gather(x, axis)
+
+
+def pair_reduce(x, axis, swap):
+    if swap:
+        return (x[0].astype(jnp.float32) + pair_swap(x[1], axis).astype(jnp.float32)).astype(x.dtype)
+    return lax.psum_scatter(x, axis, scatter_dimension=0, tiled=True)[0]
 
 
 def prefix(shard, axis, join, neutral):
@@ -108,12 +128,20 @@
         result.reshape(length, head_count * HEAD_DIM) * jax.nn.silu(gate_input.astype(jnp.float32))
     ).astype(jnp.bfloat16)
     row_count = residual.shape[0]
-    mixer_out = lax.psum_scatter(
-        jnp.dot(gated_out, out_weight, preferred_element_type=jnp.float32).astype(jnp.bfloat16),
-        EXP,
-        scatter_dimension=0,
-        tiled=True,
-    ).astype(jnp.float32)
+    projected = jnp.dot(gated_out, out_weight, preferred_element_type=jnp.float32).astype(
+        jnp.bfloat16
+    )
+    if MIX_TWO:
+        cores = lax.axis_size("c")
+        projected = projected.reshape(-1, cores, row_count, projected.shape[-1]).transpose(1, 0, 2, 3)
+        projected = lax.psum_scatter(projected, "c", scatter_dimension=0, tiled=True)[0]
+        mixer_out = lax.psum_scatter(
+            projected, ("eh", "pz"), scatter_dimension=0, tiled=True
+        )[0].astype(jnp.float32)
+    else:
+        mixer_out = lax.psum_scatter(projected, EXP, scatter_dimension=0, tiled=True).astype(
+            jnp.float32
+        )
     stream = (residual.astype(jnp.float32) + mixer_out).astype(jnp.bfloat16)
     widened = stream.astype(jnp.float32)
     normed = (
@@ -130,20 +158,27 @@
     )
     earlier_count = jnp.cumsum(onehot, axis=0) - onehot
     slot_index = jnp.sum(earlier_count * onehot, axis=1)
-    target = (
-        flat_routes % row_experts * (seq_count * capacity)
-        + flat_routes // row_experts * capacity
-        + slot_index
-    )
+    if JOINT:
+        target = flat_routes * capacity + slot_index
+    else:
+        target = (
+            flat_routes % row_experts * (seq_count * capacity)
+            + flat_routes // row_experts * capacity
+            + slot_index
+        )
     owner_row = jnp.arange(flat_routes.shape[0], dtype=jnp.int32) // TOP
     source = jnp.zeros((experts * capacity,), jnp.int32).at[target].set(owner_row)
     filled = jnp.zeros((experts * capacity,), jnp.bool_).at[target].set(True)
     outgoing = jnp.where(filled[:, None], normed[source], jnp.zeros((), jnp.bfloat16))
-    outgoing = outgoing.reshape(row_experts, seq_count, capacity, -1)
-    arrived = lax.all_to_all(outgoing, "seq", split_axis=1, concat_axis=1, tiled=True)
-    arrived = lax.all_to_all(arrived, "eh", split_axis=0, concat_axis=0, tiled=True)
-    block = lax.all_gather(arrived, "pz")
-    block = lax.all_gather(block, "c")
+    if JOINT:
+        outgoing = outgoing.reshape(experts, capacity, -1)
+        arrived = lax.all_to_all(outgoing, ("seq", "eh"), split_axis=0, concat_axis=0, tiled=True)
+    else:
+        outgoing = outgoing.reshape(row_experts, seq_count, capacity, -1)
+        arrived = lax.all_to_all(outgoing, "seq", split_axis=1, concat_axis=1, tiled=True)
+        arrived = lax.all_to_all(arrived, "eh", split_axis=0, concat_axis=0, tiled=True)
+    block = pair_gather(arrived, "pz", PZ_SWAP)
+    block = pair_gather(block, "c", C_SWAP)
     flat_rows = block.reshape(-1, block.shape[-1])
     contract = (((1,), (1,)), ((), ()))
     gate_val = lax.dot_general(
@@ -155,10 +190,13 @@
         jnp.bfloat16
     )
     piece_out = piece_out.reshape(block.shape)
-    piece_sum = lax.psum_scatter(piece_out, "c", scatter_dimension=0, tiled=True)[0]
-    piece_sum = lax.psum_scatter(piece_sum, "pz", scatter_dimension=0, tiled=True)[0]
-    returned = lax.all_to_all(piece_sum, "eh", split_axis=0, concat_axis=0, tiled=True)
-    returned = lax.all_to_all(returned, "seq", split_axis=1, concat_axis=1, tiled=True)
+    piece_sum = pair_reduce(piece_out, "c", C_SWAP)
+    piece_sum = pair_reduce(piece_sum, "pz", PZ_SWAP)
+    if JOINT:
+        returned = lax.all_to_all(piece_sum, ("seq", "eh"), split_axis=0, concat_axis=0, tiled=True)
+    else:
+        returned = lax.all_to_all(piece_sum, "eh", split_axis=0, concat_axis=0, tiled=True)
+        returned = lax.all_to_all(returned, "seq", split_axis=1, concat_axis=1, tiled=True)
     summed = returned.astype(jnp.float32)
     results = summed.reshape(experts * capacity, -1)[target]
     expert_sum = jnp.sum(

time: 561 us -> 453 us (0.81)
  the two profiles are of different devices: /device:TPU:32 before, /device:TPU:1 now
where the time goes in v2:
time: 453 us; the launch traced here: 451 us
  waiting for transfers between devices  269 us (59%)
  blocking collectives  63.1 us (14%)
  local copies, waits for them, and re-layouts  39.3 us (9%)
  other arithmetic  33.5 us (7%)
  matrix products  22 us (5%)
  between operations  13.6 us (3%)
  starting transfers between devices  10.2 us (2%)
    ppermute x4, waiting for transfers between devices, pair_swap(): return lax.ppermute(x, axis, perm=[(0, 1), (1, 0)])  106 us
    all_to_all x1, blocking collectives, shards(): lax.all_to_all(outgoing, ('seq', 'eh'), split_axis=0, concat_axis=0, tile...  63.1 us
    all_to_all x1, waiting for transfers between devices, shards(): lax.all_to_all(piece_sum, ('seq', 'eh'), split_axis=0, concat_axis=0, til...  52.1 us
    all_gather x1, waiting for transfers between devices, prefix(): gathered = lax.all_gather(packed.astype(jnp.bfloat16), axis)  44.7 us
    reduce_scatter x1, waiting for transfers between devices, shards(): lax.psum_scatter(projected, ('eh', 'pz'), scatter_dimension=0, tiled=True)  34.3 us
    reduce_scatter x1, waiting for transfers between devices, shards(): lax.psum_scatter(projected, 'c', scatter_dimension=0, tiled=True)[0]  32.7 us
    gather x2, local copies, waits for them, and re-layouts, shards(): results = summed.reshape(experts * capacity, -1)[target]  11.9 us
  transfers between devices with their start and end apart: 8, of which 8 were waited for; matrix products, arithmetic and copies ran while one was open for 3% of the time, Pallas kernels for 0%

profile of v2, /device:TPU:1, one launch (start us, length us, event | category | flops | bytes accessed | tf_op | source)
XLA Modules:
  0.0 451.3 jit_solution(12378660069646420340)
XLA Ops:
  6.5 0.9 reshape.199
  7.4 4.8 %reduce-window.14 = f32[4,4,2,128]{3,2,1,0:T(2,128)S(1)} reduce-window(f32[4,4,2,128]{3,2,1,0:T(2,128)S(1)} %reshape.199, f32[]{:T(128)} %constant.46.clone.1), window={size=1x1x1x128 pad=0_0x0_0x0_0x127_0}, to_apply=%region_0.0 | reduce-window | flops 520192 | bytes 32772 | tf_op jit(solution)/shard_map/reduce-window
  12.7 0.3 copy.53
  13.0 0.8 copy-done.8
  13.8 2.0 reshape.251
  15.8 0.5 copy.58
  16.4 0.8 fusion.46
  17.2 1.2 fusion.32
  18.5 3.1 while.26
  18.5 0.7 bitcast_dynamic-update-slice_fusion.2
  19.3 0.7 bitcast_dynamic-update-slice_fusion.2
  20.1 0.7 bitcast_dynamic-update-slice_fusion.2
  20.8 0.7 bitcast_dynamic-update-slice_fusion.2
  21.7 0.7 pad_maximum_fusion.2
  22.6 2.0 copy.65
  24.6 0.7 subtract_exponential_fusion
  25.3 0.3 fusion.62
  25.6 2.5 fusion.17
  28.1 44.7 %all-gather.2.cloned.1.call-done = bf16[16,4,8320]{2,1,0:T(4,128)(2,1)} async-done(((bf16[1,4,8320]{2,1,0:T(4,128)(2,1)}), bf16[16,4,8320]{2,1,0:T(4,128)(2,1)}) %all-gather.2.cloned.1.call-update) | async-done | bytes 1064976 | tf_op jit(solution)/shard_map/all_gather | solution.py:41
  72.7 1.6 slice.55
  74.4 1.9 reshape.203
  76.6 2.2 fusion.20
  78.8 0.7 copy.64
  79.5 0.2 copy.79
  79.7 1.4 convolution_convert_fusion.1
  81.1 2.2 copy.84
  83.4 32.7 %reduce-scatter.3.cloned.1.call-done = bf16[1,8,64,2048]{3,2,1,0:T(8,128)(2,1)} async-done(((bf16[2,8,64,2048]{3,2,1,0:T(8,128)(2,1)}), bf16[1,8,64,2048]{3,2,1,0:T(8,128)(2,1)}) %reduce-scatter.3.cloned.1.call-update) | async-done | bytes 2097168 | tf_op jit(solution)/shard_map/reduce_scatter | solution.py:137
  116.4 0.1 eq.25
  116.5 0.9 reduce-window.16
  117.4 0.2 slice_reduce_fusion
  117.8 0.1 mul.156
  118.1 2.9 scatter_custom_fusion.1
  121.0 2.1 scatter_custom_fusion
  123.3 34.3 %reduce-scatter.5.cloned.1.call-done = bf16[1,64,2048]{2,1,0:T(8,128)(2,1)} async-done(((bf16[8,64,2048]{2,1,0:T(8,128)(2,1)}), bf16[1,64,2048]{2,1,0:T(8,128)(2,1)}) %reduce-scatter.5.cloned.1.call-update) | async-done | bytes 262160 | tf_op jit(solution)/shard_map/reduce_scatter | solution.py:138
  157.6 1.1 fusion.27
  158.8 1.1 fusion.29
  159.9 3.3 gather_fusion
  163.2 1.8 bitcast_select_fusion
  165.0 63.1 %all_to_all.10 = bf16[64,8,2048]{2,1,0:T(8,128)(2,1)S(1)} all-to-all(bf16[64,8,2048]{2,1,0:T(8,128)(2,1)S(1)} %bitcast_select_fusion), channel_id=1, replica_groups=mesh['seq'=16,'eh'=4,'pz'=2,'c'=2] {'seq','eh'}, dimensions={0} | all-to-all | bytes 4194304 | tf_op jit(solution)/shard_map/all_to_all | solution.py:175
  228.1 45.2 %collective-permute-done = bf16[64,8,2048]{2,1,0:T(8,128)(2,1)S(1)} collective-permute-done((bf16[64,8,2048]{2,1,0:T(8,128)(2,1)S(1)}, bf16[64,8,2048]{2,1,0:T(8,128)(2,1)S(1)}, u32[]{:S(2)}, u32[]{:S(2)}) %collective-permute-start) | collective-permute-done | bytes 2097184 | tf_op jit(solution)/shard_map/ppermute | solution.py:19
  273.3 0.6 fusion.60
  273.8 3.0 collective-permute-start.1
  276.8 6.8 %collective-permute-done.1 = bf16[2,64,8,2048]{3,2,1,0:T(8,128)(2,1)S(1)} collective-permute-done((bf16[2,64,8,2048]{3,2,1,0:T(8,128)(2,1)S(1)}, bf16[2,64,8,2048]{3,2,1,0:T(8,128)(2,1)S(1)}, u32[]{:S(2)}, u32[]{:S(2)}) %collective-permute-start.1) | collective-permute-done | bytes 4194336 | tf_op jit(solution)/shard_map/ppermute | solution.py:19
  283.6 2.0 copy-done.2
  285.6 6.2 %pad_maximum_fusion = bf16[2,2,64,8,2048]{4,3,2,1,0:T(8,128)(2,1)} fusion(bf16[1,2,64,8,2048]{4,3,2,1,0:T(8,128)(2,1)} %bitcast.147, bf16[1,2,64,8,2048]{4,3,2,1,0:T(8,128)(2,1)S(1)} %get-tuple-element.135), kind=kLoop, calls=%fused_computation.11 | loop fusion | flops 4194304 | bytes 16777216 | tf_op jit(solution)/shard_map/stack | solution.py:24
  291.7 6.4 %fusion.12 = f32[2048,352]{0,1:T(8,128)S(1)} fusion(bf16[2048,2048]{1,0:T(8,128)(2,1)} %bitcast.142, bf16[1,352,2048]{2,1,0:T(8,128)(2,1)} %param.32), kind=kOutput, calls=%fused_computation.35 | convolution fusion | flops 2952790016 | bytes 12713984 | tf_op jit(solution)/shard_map/dot_general | solution.py:187
  298.1 0.3 copy-done.16
  298.4 3.2 fusion.14
  301.6 4.9 %convolution_convert_fusion = bf16[2048,2048]{1,0:T(8,128)(2,1)S(1)} fusion(f32[2048,352]{0,1:T(8,128)S(1)} %fusion.12, f32[2048,352]{0,1:T(8,128)S(1)} %fusion.14, bf16[1,352,2048]{2,1,0:T(8,128)(2,1)S(1)} %copy-done), kind=kOutput, calls=%fused_computation.14 | convolution fusion | flops 2961309696 | bytes 15597568 | tf_op jit(solution)/shard_map/dot_general | solution.py:189
  306.5 0.9 fusion.61
  307.5 0.7 collective-permute-start.2
  308.1 6.8 %collective-permute-done.2 = bf16[2,64,8,2048]{3,2,1,0:T(8,128)(2,1)S(1)} collective-permute-done((bf16[2,64,8,2048]{3,2,1,0:T(8,128)(2,1)S(1)}, bf16[2,64,8,2048]{3,2,1,0:T(8,128)(2,1)S(1)}, u32[]{:S(2)}, u32[]{:S(2)}) %collective-permute-start.2) | collective-permute-done | bytes 4194336 | tf_op jit(solution)/shard_map/ppermute | solution.py:19
  314.9 2.3 fusion.2
  317.2 0.2 slice_bitcast_fusion
  317.6 46.8 %collective-permute-done.3 = bf16[64,8,2048]{2,1,0:T(8,128)(2,1)S(1)} collective-permute-done((bf16[64,8,2048]{2,1,0:T(8,128)(2,1)S(1)}, bf16[64,8,2048]{2,1,0:T(8,128)(2,1)S(1)}, u32[]{:S(2)}, u32[]{:S(2)}) %collective-permute-start.3) | collective-permute-done | bytes 2097184 | tf_op jit(solution)/shard_map/ppermute | solution.py:19
  364.4 2.1 fusion.3
  366.5 6.4 %all-to-all-start.1 = ((bf16[64,8,2048]{2,1,0:T(8,128)(2,1)}), bf16[64,8,2048]{2,1,0:T(8,128)(2,1)S(1)}, u32[]{:S(2)}, u32[]{:S(2)}) async-start(bf16[64,8,2048]{2,1,0:T(8,128)(2,1)} %fusion.3), calls=%async_computation.3 | async-start | bytes 4194304 | tf_op jit(solution)/shard_map/all_to_all | solution.py:196
  372.9 0.7 copy.71
  373.6 52.1 %all-to-all-done.1 = bf16[64,8,2048]{2,1,0:T(8,128)(2,1)S(1)} async-done(((bf16[64,8,2048]{2,1,0:T(8,128)(2,1)}), bf16[64,8,2048]{2,1,0:T(8,128)(2,1)S(1)}, u32[]{:S(2)}, u32[]{:S(2)}) %all-to-all-start.1) | async-done | bytes 2097184 | tf_op jit(solution)/shard_map/all_to_all | solution.py:196
  425.8 2.5 bitcast_convert_fusion
  428.2 7.3 %gather_fusion.1 = f32[384,2048]{1,0:T(8,128)} fusion(f32[512,2048]{1,0:T(8,128)} %bitcast_convert_fusion, s32[1024]{0:T(1024)S(1)} %pad_clamp_fusion), kind=kCustom, calls=%fused_computation.1 | custom fusion | bytes 6292992 | tf_op jit(solution)/shard_map/gather | solution.py:201
  435.5 4.6 %gather.13 = f32[64,6,2048]{2,1,0:T(8,128)} reshape(f32[384,2048]{1,0:T(8,128)} %gather_fusion.1) | data formatting | bytes 6291456 | tf_op jit(solution)/shard_map/gather | solution.py:201
  440.1 3.8 multiply_reduce_fusion
  443.9 0.8 fusion.30
  (88 shorter events, 2.2 us)
Async XLA Ops:
  6.5 295.0 %copy-start = (bf16[1,352,2048]{2,1,0:T(8,128)(2,1)S(1)}, bf16[1,352,2048]{2,1,0:T(8,128)(2,1)}, u32[]{:S(2)}) copy-start(bf16[1,352,2048]{2,1,0:T(8,128)(2,1)} %param.33) | copy-start | bytes 4325380
  6.5 66.2 %all-gather.2.cloned.1.call-start = ((), (), s32[]{:S(2)}) async-start(), calls=%async_computation.4 | async-start | bytes 1131520 | tf_op jit(solution)/shard_map/all_gather | solution.py:41
  13.0 0.8 copy-start.8
  13.8 8.7 %copy-start.11 = (f32[4,1024]{1,0:T(4,128)S(1)}, f32[4,1024]{1,0:T(4,128)}, u32[]{:S(2)}) copy-start(f32[4,1024]{1,0:T(4,128)} %param.23) | copy-start | bytes 49156
  15.8 9.5 %copy-start.6 = (bf16[1024,128]{1,0:T(8,128)(2,1)S(1)}, bf16[1024,128]{1,0:T(8,128)(2,1)}, u32[]{:S(2)}) copy-start(bf16[1024,128]{1,0:T(8,128)(2,1)} %param.22) | copy-start | bytes 786436
  16.4 8.9 %copy-start.7 = (bf16[1024,128]{1,0:T(8,128)(2,1)S(1)}, bf16[1024,128]{1,0:T(8,128)(2,1)}, u32[]{:S(2)}) copy-start(bf16[1024,128]{1,0:T(8,128)(2,1)} %param.21) | copy-start | bytes 786436
  22.4 93.7 %reduce-scatter.3.cloned.1.call-start = ((), (), s32[]{:S(2)}) async-start(), calls=%async_computation.5 | async-start | bytes 6291456 | tf_op jit(solution)/shard_map/reduce_scatter | solution.py:137
  28.1 48.5 %copy-start.15 = (f32[4]{0:T(128)S(1)}, f32[4]{0:T(128)}, u32[]{:S(2)}) copy-start(f32[4]{0:T(128)} %param.25) | copy-start | bytes 52
  72.7 3.6 slice-start
  76.5 3.2 copy-start.9
  76.5 3.2 copy-start.17
  83.3 32.8 %copy-start.12 = (s32[64,6]{0,1:T(8,128)S(1)}, s32[64,6]{0,1:T(8,128)}, u32[]{:S(2)}) copy-start(s32[64,6]{0,1:T(8,128)} %param.29) | copy-start | bytes 4612
  83.3 74.3 %copy-start.3 = (bf16[64,2048]{1,0:T(8,128)(2,1)S(1)}, bf16[64,2048]{1,0:T(8,128)(2,1)}, u32[]{:S(2)}) copy-start(bf16[64,2048]{1,0:T(8,128)(2,1)} %param.27) | copy-start | bytes 786436
  83.3 75.5 %copy-start.13 = (f32[2048]{0:T(1024)S(1)}, f32[2048]{0:T(1024)}, u32[]{:S(2)}) copy-start(f32[2048]{0:T(1024)} %param.28) | copy-start | bytes 24580
  83.4 74.3 %reduce-scatter.5.cloned.1.call-start = ((), (), s32[]{:S(2)}) async-start(), calls=%async_computation.6 | async-start | bytes 2359296 | tf_op jit(solution)/shard_map/reduce_scatter | solution.py:138
  228.1 45.2 %collective-permute-start = (bf16[64,8,2048]{2,1,0:T(8,128)(2,1)S(1)}, bf16[64,8,2048]{2,1,0:T(8,128)(2,1)S(1)}, u32[]{:S(2)}, u32[]{:S(2)}) collective-permute-start(bf16[64,8,2048]{2,1,0:T(8,128)(2,1)S(1)} %all_to_all.10), channel_id=1, source_target_pairs={{0,2},{2,0},{1,3},{3,1},{4,6},{6,4},{5,7},{7,5},{8,10},{10,8},{9,1... | collective-permute-start | bytes 6291464 | tf_op jit(solution)/shard_map/ppermute | solution.py:19
  273.8 9.8 %collective-permute-start.1 = (bf16[2,64,8,2048]{3,2,1,0:T(8,128)(2,1)S(1)}, bf16[2,64,8,2048]{3,2,1,0:T(8,128)(2,1)S(1)}, u32[]{:S(2)}, u32[]{:S(2)}) collective-permute-start(bf16[2,64,8,2048]{3,2,1,0:T(8,128)(2,1)S(1)} %get-tuple-element.136), channel_id=1, source_target_pairs={{0,1},{1,0},{2,3},{3,2},{4,5},{5,4},{6,7},{7,6},{8,9},{9,8},{10,11... | collective-permute-start | bytes 12582920 | tf_op jit(solution)/shard_map/ppermute | solution.py:19
  283.6 2.0 copy-start.2
  291.7 6.4 %copy-start.1 = (bf16[2,2,64,8,2048]{4,3,2,1,0:T(8,128)(2,1)S(1)}, bf16[2,2,64,8,2048]{4,3,2,1,0:T(8,128)(2,1)}, u32[]{:S(2)}) copy-start(bf16[2,2,64,8,2048]{4,3,2,1,0:T(8,128)(2,1)} %pad_maximum_fusion) | copy-start | bytes 25165828
  291.7 6.6 %copy-start.16 = (bf16[1,352,2048]{2,1,0:T(8,128)(2,1)S(1)}, bf16[1,352,2048]{2,1,0:T(8,128)(2,1)}, u32[]{:S(2)}) copy-start(bf16[1,352,2048]{2,1,0:T(8,128)(2,1)} %param.31) | copy-start | bytes 4325380
  307.5 7.5 %collective-permute-start.2 = (bf16[2,64,8,2048]{3,2,1,0:T(8,128)(2,1)S(1)}, bf16[2,64,8,2048]{3,2,1,0:T(8,128)(2,1)S(1)}, u32[]{:S(2)}, u32[]{:S(2)}) collective-permute-start(bf16[2,64,8,2048]{3,2,1,0:T(8,128)(2,1)S(1)} %bitcast.148), channel_id=1, source_target_pairs={{0,1},{1,0},{2,3},{3,2},{4,5},{5,4},{6,7},{7,6},{8,9},{9,8},{10,11... | collective-permute-start | bytes 12582920 | tf_op jit(solution)/shard_map/ppermute | solution.py:19
  317.5 55.5 %copy-start.14 = (f32[64,6]{0,1:T(8,128)S(1)}, f32[64,6]{0,1:T(8,128)}, u32[]{:S(2)}) copy-start(f32[64,6]{0,1:T(8,128)} %param.30) | copy-start | bytes 4612
  317.5 46.9 %collective-permute-start.3 = (bf16[64,8,2048]{2,1,0:T(8,128)(2,1)S(1)}, bf16[64,8,2048]{2,1,0:T(8,128)(2,1)S(1)}, u32[]{:S(2)}, u32[]{:S(2)}) collective-permute-start(bf16[64,8,2048]{2,1,0:T(8,128)(2,1)S(1)} %slice_bitcast_fusion), channel_id=1, source_target_pairs={{0,2},{2,0},{1,3},{3,1},{4,6},{6,4},{5,7},{7,5},{8,10},{10,8},{9,1... | collective-permute-start | bytes 6291464 | tf_op jit(solution)/shard_map/ppermute | solution.py:19
  366.5 59.2 %all-to-all-start.1 = ((bf16[64,8,2048]{2,1,0:T(8,128)(2,1)}), bf16[64,8,2048]{2,1,0:T(8,128)(2,1)S(1)}, u32[]{:S(2)}, u32[]{:S(2)}) async-start(bf16[64,8,2048]{2,1,0:T(8,128)(2,1)} %fusion.3), calls=%async_computation.3 | async-start | bytes 4194304 | tf_op jit(solution)/shard_map/all_to_all | solution.py:196
  435.5 4.6 %copy-start.10 = (f32[64,6]{1,0:T(8,128)S(1)}, f32[64,6]{1,0:T(8,128)}, u32[]{:S(2)}) copy-start(f32[64,6]{1,0:T(8,128)} %copy.71) | copy-start | bytes 4612
  440.1 3.8 copy-start.4
  440.1 3.8 copy-start.5
Sparse Core Ops, SparseCore 0:
  22.5 50.1 all-gather.1
  83.5 32.5 reduce-scatter.2
  118.8 38.7 reduce-scatter.4

commit v3 on v2

--- a/solution.py
+++ b/solution.py
@@ -13,6 +13,37 @@
 PZ_SWAP = True
 C_SWAP = True
 MIX_TWO = True
+MIX_SWAP = True
+PREFIX_SCAN = True
+
+
+def scan_prefix(decay, state, axis):
+    count = lax.axis_size(axis)
+    cut = state.shape[1] * state.shape[2]
+    heads = state.shape[0]
+
+    def split(packed):
+        return packed[:, cut], packed[:, :cut].reshape(state.shape)
+
+    def join(earlier, later):
+        early_decay, early_state = split(earlier)
+        late_decay, late_state = split(later)
+        total = early_decay + late_decay
+        carried = jnp.exp(late_decay)[:, None, None] * early_state + late_state
+        return jnp.concatenate(
+            [carried.reshape(heads, cut), jnp.broadcast_to(total[:, None], (heads, STATE))], axis=1
+        )
+
+    packed = jnp.concatenate(
+        [state.reshape(heads, cut), jnp.broadcast_to(decay[:, None], (heads, STATE))], axis=1
+    )
+    packed = lax.ppermute(packed, axis, perm=[(i, i + 1) for i in range(count - 1)])
+    shift = 1
+    while shift < count:
+        moved = lax.ppermute(packed, axis, perm=[(i, i + shift) for i in range(count - shift)])
+        packed = join(moved, packed)
+        shift *= 2
+    return split(packed)
 
 
 def pair_swap(x, axis):
@@ -113,9 +144,12 @@
     zero_state = jnp.zeros((head_count, HEAD_DIM, STATE), jnp.float32)
     end_local, entering_local = lax.scan(advance, zero_state, (totals, block_state))
     device_decay = jnp.sum(totals, axis=0)
-    before = prefix(
-        (device_decay, end_local), "seq", join_states, (jnp.zeros_like(device_decay), zero_state)
-    )
+    if PREFIX_SCAN:
+        before = scan_prefix(device_decay, end_local, "seq")
+    else:
+        before = prefix(
+            (device_decay, end_local), "seq", join_states, (jnp.zeros_like(device_decay), zero_state)
+        )
     before_state = before[1]
     before_blocks = jnp.cumsum(totals, axis=0) - totals
     entering = jnp.exp(before_blocks)[:, :, None, None] * before_state[None] + entering_local
@@ -134,7 +168,20 @@
     if MIX_TWO:
         cores = lax.axis_size("c")
         projected = projected.reshape(-1, cores, row_count, projected.shape[-1]).transpose(1, 0, 2, 3)
-        projected = lax.psum_scatter(projected, "c", scatter_dimension=0, tiled=True)[0]
+        if MIX_SWAP:
+            core = lax.axis_index("c")
+            projected = pair_reduce(
+                jnp.stack(
+                    [
+                        lax.dynamic_index_in_dim(projected, core, 0, False),
+                        lax.dynamic_index_in_dim(projected, 1 - core, 0, False),
+                    ]
+                ),
+                "c",
+                True,
+            )
+        else:
+            projected = lax.psum_scatter(projected, "c", scatter_dimension=0, tiled=True)[0]
         mixer_out = lax.psum_scatter(
             projected, ("eh", "pz"), scatter_dimension=0, tiled=True
         )[0].astype(jnp.float32)

time: 453 us -> 422 us (0.932)
  waiting for transfers between devices: 269 us -> 199 us
  starting transfers between devices: 10.2 us -> 41.6 us
  other arithmetic: 33.5 us -> 43.7 us
    all_gather x1 -> x0, waiting for transfers between devices: 44.7 us -> none  [prefix(): gathered = lax.all_gather(packed.astype(jnp.bfloat16), axis)]
    reduce_scatter x1 -> x0, waiting for transfers between devices: 32.7 us -> none  [shards(): lax.psum_scatter(projected, 'c', scatter_dimension=0, tiled=True)[0]]
    ppermute x0 -> x5, starting transfers between devices: none -> 26.6 us  [the longest x4 22.6 us: scan_prefix(): lax.ppermute(packed, axis, perm=[(i, i + shift) for i in range(count - sh...]
    ppermute x0 -> x5, waiting for transfers between devices: none -> 5.92 us  [the longest x4 3.74 us: scan_prefix(): lax.ppermute(packed, axis, perm=[(i, i + shift) for i in range(count - sh...]
    ppermute x4 -> x5, starting transfers between devices: 3.75 us -> 9.16 us  [pair_swap(): return lax.ppermute(x, axis, perm=[(0, 1), (1, 0)])]
    ppermute x4 -> x5, waiting for transfers between devices: 106 us -> 109 us  [pair_swap(): return lax.ppermute(x, axis, perm=[(0, 1), (1, 0)])]
  transfers between devices with their start and end apart: 8 -> 12, of which waited for: 8 -> 11; matrix products, arithmetic and copies ran while one was open for 3% -> 4% of each run, Pallas kernels for 0% -> 0%
where the time goes in v3:
time: 422 us
  waiting for transfers between devices  199 us (47%)
  blocking collectives  62.4 us (15%)
  other arithmetic  43.7 us (10%)
  starting transfers between devices  41.6 us (10%)
  local copies, waits for them, and re-layouts  38 us (9%)
  matrix products  22.7 us (5%)
  between operations  13.9 us (3%)
    ppermute x5, waiting for transfers between devices, pair_swap(): return lax.ppermute(x, axis, perm=[(0, 1), (1, 0)])  109 us
    all_to_all x1, blocking collectives, shards(): lax.all_to_all(outgoing, ('seq', 'eh'), split_axis=0, concat_axis=0, tile...  62.4 us
    all_to_all x1, waiting for transfers between devices, shards(): lax.all_to_all(piece_sum, ('seq', 'eh'), split_axis=0, concat_axis=0, til...  52.1 us
    reduce_scatter x1, waiting for transfers between devices, shards(): lax.psum_scatter(projected, ('eh', 'pz'), scatter_dimension=0, tiled=True)  31.9 us
    ppermute x4, starting transfers between devices, scan_prefix(): lax.ppermute(packed, axis, perm=[(i, i + shift) for i in range(count - sh...  22.6 us
    gather x2, local copies, waits for them, and re-layouts, shards(): results = summed.reshape(experts * capacity, -1)[target]  12 us
    ppermute x5, starting transfers between devices, pair_swap(): return lax.ppermute(x, axis, perm=[(0, 1), (1, 0)])  9.16 us
    convert_element_type x3, other arithmetic, pair_reduce(): (x[0].astype(jnp.float32) + pair_swap(x[1], axis).astype(jnp.float32)).as...  8.89 us
  transfers between devices with their start and end apart: 12, of which 11 were waited for; matrix products, arithmetic and copies ran while one was open for 4% of the time, Pallas kernels for 0%

profile of v3, /device:TPU:1, one launch (start us, length us, event | category | flops | bytes accessed | tf_op | source)
XLA Modules:
  0.0 421.5 jit_solution(15910396883360428991)
XLA Ops:
  6.5 0.9 reshape.224
  7.4 4.8 %reduce-window.14 = f32[4,4,2,128]{3,2,1,0:T(2,128)S(1)} reduce-window(f32[4,4,2,128]{3,2,1,0:T(2,128)S(1)} %reshape.224, f32[]{:T(128)} %constant.34.clone.1), window={size=1x1x1x128 pad=0_0x0_0x0_0x127_0}, to_apply=%region_0.0 | reduce-window | flops 520192 | bytes 32772 | tf_op jit(solution)/shard_map/reduce-window
  13.0 0.8 copy-done.10
  13.8 2.0 reshape.281
  16.4 0.9 fusion.50
  17.3 1.2 fusion.33
  18.5 3.1 while.13
  20.8 0.7 bitcast_dynamic-update-slice_fusion.2
  21.8 4.0 collective-permute-start
  25.9 2.2 collective-permute-done
  28.1 4.1 collective-permute-start.1
  32.2 1.9 collective-permute-done.1
  34.3 0.8 multiply_add_fusion.2
  35.1 5.4 %collective-permute-start.2 = (f32[4,8320]{1,0:T(4,128)S(1)}, f32[4,8320]{1,0:T(4,128)S(1)}, u32[]{:S(2)}, u32[]{:S(2)}) collective-permute-start(f32[4,8320]{1,0:T(4,128)S(1)} %pad_maximum_fusion.3), channel_id=1, source_target_pairs={{0,32},{16,48},{32,64},{48,80},{64,96},{80,112},{96,128},{112,144}... | collective-permute-start | bytes 399368 | tf_op jit(solution)/shard_map/ppermute | solution.py:43
  40.6 1.3 fusion.69
  43.3 0.7 pad_maximum_fusion.4
  44.0 9.4 %collective-permute-start.3 = (f32[4,8320]{1,0:T(4,128)}, f32[4,8320]{1,0:T(4,128)}, u32[]{:S(2)}, u32[]{:S(2)}) collective-permute-start(f32[4,8320]{1,0:T(4,128)} %pad_maximum_fusion.4), channel_id=1, source_target_pairs={{0,64},{16,80},{32,96},{48,112},{64,128},{80,144},{96,160},{112,17... | collective-permute-start | bytes 399368 | tf_op jit(solution)/shard_map/ppermute | solution.py:43
  53.4 2.6 fusion.18
  56.0 1.3 reduce_window_sum.46
  57.3 2.0 copy.88
  59.3 0.8 slice_reduce_fusion.1
  60.7 1.0 multiply_add_fusion
  61.8 3.7 collective-permute-start.4
  65.6 0.7 subtract_exponential_fusion
  66.3 1.2 collective-permute-done.4
  67.5 1.2 fusion.44
  68.7 1.8 fusion.21
  70.5 0.7 copy.87
  71.5 1.4 convolution_convert_fusion.1
  72.8 1.9 copy-done.3
  74.7 1.5 dynamic-slice_bitcast_fusion
  76.2 5.0 %collective-permute-start.5 = (bf16[8,64,2048]{2,1,0:T(8,128)(2,1)}, bf16[8,64,2048]{2,1,0:T(8,128)(2,1)}, u32[]{:S(2)}, u32[]{:S(2)}) collective-permute-start(bf16[8,64,2048]{2,1,0:T(8,128)(2,1)} %dynamic-slice_bitcast_fusion), channel_id=1, source_target_pairs={{0,1},{1,0},{2,3},{3,2},{4,5},{5,4},{6,7},{7,6},{8,9},{9,8},{10,11... | collective-permute-start | bytes 6291464 | tf_op jit(solution)/shard_map/ppermute | solution.py:50
  81.2 4.1 collective-permute-done.5
  85.3 4.5 %fusion.4 = bf16[8,64,2048]{2,1,0:T(8,128)(2,1)} fusion(bf16[8,64,2048]{2,1,0:T(8,128)(2,1)} %collective-permute-done.5, bf16[8,2,64,2048]{3,2,1,0:T(8,128)(2,1)} %bitcast.177, s32[]{:T(128)S(6)} %select_n.41), kind=kLoop, calls=%fused_computation.17 | loop fusion | flops 4194304 | bytes 6291460 | tf_op jit(solution)/shard_map/convert_element_type | solution.py:61
  90.2 0.9 reduce-window.16
  91.8 3.1 scatter_custom_fusion.1
  94.9 2.0 scatter_custom_fusion
  97.0 31.9 %reduce-scatter.2.cloned.1.call-done = bf16[1,64,2048]{2,1,0:T(8,128)(2,1)} async-done(((bf16[8,64,2048]{2,1,0:T(8,128)(2,1)}), bf16[1,64,2048]{2,1,0:T(8,128)(2,1)}) %reduce-scatter.2.cloned.1.call-update) | async-done | bytes 262160 | tf_op jit(solution)/shard_map/reduce_scatter | solution.py:185
  129.0 1.1 fusion.28
  130.1 1.1 fusion.30
  131.2 3.3 gather_fusion
  134.5 1.8 bitcast_select_fusion
  136.3 62.4 %all_to_all.10 = bf16[64,8,2048]{2,1,0:T(8,128)(2,1)S(1)} all-to-all(bf16[64,8,2048]{2,1,0:T(8,128)(2,1)S(1)} %bitcast_select_fusion), channel_id=1, replica_groups=mesh['seq'=16,'eh'=4,'pz'=2,'c'=2] {'seq','eh'}, dimensions={0} | all-to-all | bytes 4194304 | tf_op jit(solution)/shard_map/all_to_all | solution.py:222
  198.7 44.5 %collective-permute-done.6 = bf16[64,8,2048]{2,1,0:T(8,128)(2,1)S(1)} collective-permute-done((bf16[64,8,2048]{2,1,0:T(8,128)(2,1)S(1)}, bf16[64,8,2048]{2,1,0:T(8,128)(2,1)S(1)}, u32[]{:S(2)}, u32[]{:S(2)}) %collective-permute-start.6) | collective-permute-done | bytes 2097184 | tf_op jit(solution)/shard_map/ppermute | solution.py:50
  243.8 3.6 collective-permute-start.7
  247.4 6.8 %collective-permute-done.7 = bf16[2,64,8,2048]{3,2,1,0:T(8,128)(2,1)S(1)} collective-permute-done((bf16[2,64,8,2048]{3,2,1,0:T(8,128)(2,1)S(1)}, bf16[2,64,8,2048]{3,2,1,0:T(8,128)(2,1)S(1)}, u32[]{:S(2)}, u32[]{:S(2)}) %collective-permute-start.7) | collective-permute-done | bytes 4194336 | tf_op jit(solution)/shard_map/ppermute | solution.py:50
  254.2 2.0 copy-done.4
  256.2 6.2 %pad_maximum_fusion = bf16[2,2,64,8,2048]{4,3,2,1,0:T(8,128)(2,1)} fusion(bf16[1,2,64,8,2048]{4,3,2,1,0:T(8,128)(2,1)} %bitcast.179, bf16[1,2,64,8,2048]{4,3,2,1,0:T(8,128)(2,1)S(1)} %get-tuple-element.71), kind=kLoop, calls=%fused_computation.9 | loop fusion | flops 4194304 | bytes 16777216 | tf_op jit(solution)/shard_map/stack | solution.py:55
  262.4 6.4 %fusion.13 = f32[2048,352]{0,1:T(8,128)S(1)} fusion(bf16[2048,2048]{1,0:T(8,128)(2,1)} %bitcast.173, bf16[1,352,2048]{2,1,0:T(8,128)(2,1)} %param.30), kind=kOutput, calls=%fused_computation.35 | convolution fusion | flops 2952790016 | bytes 12713984 | tf_op jit(solution)/shard_map/dot_general | solution.py:234
  269.0 3.2 fusion.15
  272.2 4.9 %convolution_convert_fusion = bf16[2048,2048]{1,0:T(8,128)(2,1)S(1)} fusion(f32[2048,352]{0,1:T(8,128)S(1)} %fusion.13, f32[2048,352]{0,1:T(8,128)S(1)} %fusion.15, bf16[1,352,2048]{2,1,0:T(8,128)(2,1)S(1)} %copy-done), kind=kOutput, calls=%fused_computation.12 | convolution fusion | flops 2961309696 | bytes 15597568 | tf_op jit(solution)/shard_map/dot_general | solution.py:236
  277.1 0.9 fusion.68
  278.5 6.8 %collective-permute-done.8 = bf16[2,64,8,2048]{3,2,1,0:T(8,128)(2,1)S(1)} collective-permute-done((bf16[2,64,8,2048]{3,2,1,0:T(8,128)(2,1)S(1)}, bf16[2,64,8,2048]{3,2,1,0:T(8,128)(2,1)S(1)}, u32[]{:S(2)}, u32[]{:S(2)}) %collective-permute-start.8) | collective-permute-done | bytes 4194336 | tf_op jit(solution)/shard_map/ppermute | solution.py:50
  285.3 2.3 fusion.2
  288.0 46.8 %collective-permute-done.9 = bf16[64,8,2048]{2,1,0:T(8,128)(2,1)S(1)} collective-permute-done((bf16[64,8,2048]{2,1,0:T(8,128)(2,1)S(1)}, bf16[64,8,2048]{2,1,0:T(8,128)(2,1)S(1)}, u32[]{:S(2)}, u32[]{:S(2)}) %collective-permute-start.9) | collective-permute-done | bytes 2097184 | tf_op jit(solution)/shard_map/ppermute | solution.py:50
  334.8 2.1 fusion.3
  336.9 5.8 %all-to-all-start.1 = ((bf16[64,8,2048]{2,1,0:T(8,128)(2,1)}), bf16[64,8,2048]{2,1,0:T(8,128)(2,1)S(1)}, u32[]{:S(2)}, u32[]{:S(2)}) async-start(bf16[64,8,2048]{2,1,0:T(8,128)(2,1)} %fusion.3), calls=%async_computation.2 | async-start | bytes 4194304 | tf_op jit(solution)/shard_map/all_to_all | solution.py:243
  342.8 0.7 copy.94
  343.5 52.1 %all-to-all-done.1 = bf16[64,8,2048]{2,1,0:T(8,128)(2,1)S(1)} async-done(((bf16[64,8,2048]{2,1,0:T(8,128)(2,1)}), bf16[64,8,2048]{2,1,0:T(8,128)(2,1)S(1)}, u32[]{:S(2)}, u32[]{:S(2)}) %all-to-all-start.1) | async-done | bytes 2097184 | tf_op jit(solution)/shard_map/all_to_all | solution.py:243
  395.6 2.5 bitcast_convert_fusion
  398.0 7.3 %gather_fusion.1 = f32[384,2048]{1,0:T(8,128)} fusion(f32[512,2048]{1,0:T(8,128)} %bitcast_convert_fusion, s32[1024]{0:T(1024)S(1)} %pad_clamp_fusion), kind=kCustom, calls=%fused_computation.1 | custom fusion | bytes 6292992 | tf_op jit(solution)/shard_map/gather | solution.py:248
  405.3 4.7 %gather.13 = f32[64,6,2048]{2,1,0:T(8,128)} reshape(f32[384,2048]{1,0:T(8,128)} %gather_fusion.1) | data formatting | bytes 6291456 | tf_op jit(solution)/shard_map/gather | solution.py:248
  410.1 3.8 multiply_reduce_fusion
  413.9 0.8 fusion.31
  (112 shorter events, 9.3 us)
Async XLA Ops:
  6.5 265.6 %copy-start = (bf16[1,352,2048]{2,1,0:T(8,128)(2,1)S(1)}, bf16[1,352,2048]{2,1,0:T(8,128)(2,1)}, u32[]{:S(2)}) copy-start(bf16[1,352,2048]{2,1,0:T(8,128)(2,1)} %param.31) | copy-start | bytes 4325380
  6.5 122.4 %reduce-scatter.2.cloned.1.call-start = ((), (), s32[]{:S(2)}) async-start(), calls=%async_computation.3 | async-start | bytes 2359296 | tf_op jit(solution)/shard_map/reduce_scatter | solution.py:185
  13.0 0.8 copy-start.10
  15.8 24.7 %copy-start.8 = (bf16[1024,128]{1,0:T(8,128)(2,1)S(1)}, bf16[1024,128]{1,0:T(8,128)(2,1)}, u32[]{:S(2)}) copy-start(bf16[1024,128]{1,0:T(8,128)(2,1)} %param.20) | copy-start | bytes 786436
  16.4 24.2 %copy-start.9 = (bf16[1024,128]{1,0:T(8,128)(2,1)S(1)}, bf16[1024,128]{1,0:T(8,128)(2,1)}, u32[]{:S(2)}) copy-start(bf16[1024,128]{1,0:T(8,128)(2,1)} %param.19) | copy-start | bytes 786436
  16.4 25.5 %copy-start.13 = (f32[4,1024]{1,0:T(4,128)S(1)}, f32[4,1024]{1,0:T(4,128)}, u32[]{:S(2)}) copy-start(f32[4,1024]{1,0:T(4,128)} %param.21) | copy-start | bytes 49156
  21.6 21.5 %copy-start.14 = (f32[4,4]{1,0:T(4,128)}, f32[4,4]{1,0:T(4,128)S(1)}, u32[]{:S(2)}) copy-start(f32[4,4]{1,0:T(4,128)S(1)} %get-tuple-element.160) | copy-start | bytes 196
  21.8 6.2 %collective-permute-start = (f32[4,8320]{1,0:T(4,128)S(1)}, f32[4,8320]{1,0:T(4,128)S(1)}, u32[]{:S(2)}, u32[]{:S(2)}) collective-permute-start(f32[4,8320]{1,0:T(4,128)S(1)} %pad_maximum_fusion.2), channel_id=1, source_target_pairs={{0,16},{16,32},{32,48},{48,64},{64,80},{80,96},{96,112},{112,128},... | collective-permute-start | bytes 399368 | tf_op jit(solution)/shard_map/ppermute | solution.py:40
  28.1 6.0 %collective-permute-start.1 = (f32[4,8320]{1,0:T(4,128)S(1)}, f32[4,8320]{1,0:T(4,128)S(1)}, u32[]{:S(2)}, u32[]{:S(2)}) collective-permute-start(f32[4,8320]{1,0:T(4,128)S(1)} %collective-permute-done), channel_id=1, source_target_pairs={{0,16},{16,32},{32,48},{48,64},{64,80},{80,96},{96,112},{112,128},... | collective-permute-start | bytes 399368 | tf_op jit(solution)/shard_map/ppermute | solution.py:43
  34.3 0.8 copy-start.19
  35.1 7.4 %collective-permute-start.2 = (f32[4,8320]{1,0:T(4,128)S(1)}, f32[4,8320]{1,0:T(4,128)S(1)}, u32[]{:S(2)}, u32[]{:S(2)}) collective-permute-start(f32[4,8320]{1,0:T(4,128)S(1)} %pad_maximum_fusion.3), channel_id=1, source_target_pairs={{0,32},{16,48},{32,64},{48,80},{64,96},{80,112},{96,128},{112,144}... | collective-permute-start | bytes 399368 | tf_op jit(solution)/shard_map/ppermute | solution.py:43
  43.2 0.9 copy-start.17
  43.2 0.9 copy-start.18
  44.0 15.3 %collective-permute-start.3 = (f32[4,8320]{1,0:T(4,128)}, f32[4,8320]{1,0:T(4,128)}, u32[]{:S(2)}, u32[]{:S(2)}) collective-permute-start(f32[4,8320]{1,0:T(4,128)} %pad_maximum_fusion.4), channel_id=1, source_target_pairs={{0,64},{16,80},{32,96},{48,112},{64,128},{80,144},{96,160},{112,17... | collective-permute-start | bytes 399368 | tf_op jit(solution)/shard_map/ppermute | solution.py:43
  61.8 5.7 %collective-permute-start.4 = (f32[4,8320]{1,0:T(4,128)S(1)}, f32[4,8320]{1,0:T(4,128)S(1)}, u32[]{:S(2)}, u32[]{:S(2)}) collective-permute-start(f32[4,8320]{1,0:T(4,128)S(1)} %pad_maximum_fusion.5), channel_id=1, source_target_pairs={{0,128},{16,144},{32,160},{48,176},{64,192},{80,208},{96,224},{112... | collective-permute-start | bytes 399368 | tf_op jit(solution)/shard_map/ppermute | solution.py:43
  67.5 3.9 copy-start.11
  67.5 3.9 copy-start.22
  72.8 1.9 copy-start.3
  76.2 9.1 %collective-permute-start.5 = (bf16[8,64,2048]{2,1,0:T(8,128)(2,1)}, bf16[8,64,2048]{2,1,0:T(8,128)(2,1)}, u32[]{:S(2)}, u32[]{:S(2)}) collective-permute-start(bf16[8,64,2048]{2,1,0:T(8,128)(2,1)} %dynamic-slice_bitcast_fusion), channel_id=1, source_target_pairs={{0,1},{1,0},{2,3},{3,2},{4,5},{5,4},{6,7},{7,6},{8,9},{9,8},{10,11... | collective-permute-start | bytes 6291464 | tf_op jit(solution)/shard_map/ppermute | solution.py:50
  81.2 8.6 %copy-start.15 = (s32[64,6]{0,1:T(8,128)S(1)}, s32[64,6]{0,1:T(8,128)}, u32[]{:S(2)}) copy-start(s32[64,6]{0,1:T(8,128)} %param.27) | copy-start | bytes 4612
  81.2 47.7 %copy-start.5 = (bf16[64,2048]{1,0:T(8,128)(2,1)S(1)}, bf16[64,2048]{1,0:T(8,128)(2,1)}, u32[]{:S(2)}) copy-start(bf16[64,2048]{1,0:T(8,128)(2,1)} %param.25) | copy-start | bytes 786436
  81.2 48.9 %copy-start.16 = (f32[2048]{0:T(1024)S(1)}, f32[2048]{0:T(1024)}, u32[]{:S(2)}) copy-start(f32[2048]{0:T(1024)} %param.26) | copy-start | bytes 24580
  198.7 44.5 %collective-permute-start.6 = (bf16[64,8,2048]{2,1,0:T(8,128)(2,1)S(1)}, bf16[64,8,2048]{2,1,0:T(8,128)(2,1)S(1)}, u32[]{:S(2)}, u32[]{:S(2)}) collective-permute-start(bf16[64,8,2048]{2,1,0:T(8,128)(2,1)S(1)} %all_to_all.10), channel_id=1, source_target_pairs={{0,2},{2,0},{1,3},{3,1},{4,6},{6,4},{5,7},{7,5},{8,10},{10,8},{9,1... | collective-permute-start | bytes 6291464 | tf_op jit(solution)/shard_map/ppermute | solution.py:50
  243.8 10.4 %collective-permute-start.7 = (bf16[2,64,8,2048]{3,2,1,0:T(8,128)(2,1)S(1)}, bf16[2,64,8,2048]{3,2,1,0:T(8,128)(2,1)S(1)}, u32[]{:S(2)}, u32[]{:S(2)}) collective-permute-start(bf16[2,64,8,2048]{3,2,1,0:T(8,128)(2,1)S(1)} %get-tuple-element.72), channel_id=1, source_target_pairs={{0,1},{1,0},{2,3},{3,2},{4,5},{5,4},{6,7},{7,6},{8,9},{9,8},{10,11... | collective-permute-start | bytes 12582920 | tf_op jit(solution)/shard_map/ppermute | solution.py:50
  254.2 2.0 copy-start.4
  262.4 6.4 %copy-start.2 = (bf16[2,2,64,8,2048]{4,3,2,1,0:T(8,128)(2,1)S(1)}, bf16[2,2,64,8,2048]{4,3,2,1,0:T(8,128)(2,1)}, u32[]{:S(2)}) copy-start(bf16[2,2,64,8,2048]{4,3,2,1,0:T(8,128)(2,1)} %pad_maximum_fusion) | copy-start | bytes 25165828
  262.4 6.6 %copy-start.21 = (bf16[1,352,2048]{2,1,0:T(8,128)(2,1)S(1)}, bf16[1,352,2048]{2,1,0:T(8,128)(2,1)}, u32[]{:S(2)}) copy-start(bf16[1,352,2048]{2,1,0:T(8,128)(2,1)} %param.29) | copy-start | bytes 4325380
  278.1 7.2 %collective-permute-start.8 = (bf16[2,64,8,2048]{3,2,1,0:T(8,128)(2,1)S(1)}, bf16[2,64,8,2048]{3,2,1,0:T(8,128)(2,1)S(1)}, u32[]{:S(2)}, u32[]{:S(2)}) collective-permute-start(bf16[2,64,8,2048]{3,2,1,0:T(8,128)(2,1)S(1)} %bitcast.180), channel_id=1, source_target_pairs={{0,1},{1,0},{2,3},{3,2},{4,5},{5,4},{6,7},{7,6},{8,9},{9,8},{10,11... | collective-permute-start | bytes 12582920 | tf_op jit(solution)/shard_map/ppermute | solution.py:50
  287.8 54.9 %copy-start.20 = (f32[64,6]{0,1:T(8,128)S(1)}, f32[64,6]{0,1:T(8,128)}, u32[]{:S(2)}) copy-start(f32[64,6]{0,1:T(8,128)} %param.28) | copy-start | bytes 4612
  287.9 46.9 %collective-permute-start.9 = (bf16[64,8,2048]{2,1,0:T(8,128)(2,1)S(1)}, bf16[64,8,2048]{2,1,0:T(8,128)(2,1)S(1)}, u32[]{:S(2)}, u32[]{:S(2)}) collective-permute-start(bf16[64,8,2048]{2,1,0:T(8,128)(2,1)S(1)} %slice_bitcast_fusion), channel_id=1, source_target_pairs={{0,2},{2,0},{1,3},{3,1},{4,6},{6,4},{5,7},{7,5},{8,10},{10,8},{9,1... | collective-permute-start | bytes 6291464 | tf_op jit(solution)/shard_map/ppermute | solution.py:50
  336.9 58.7 %all-to-all-start.1 = ((bf16[64,8,2048]{2,1,0:T(8,128)(2,1)}), bf16[64,8,2048]{2,1,0:T(8,128)(2,1)S(1)}, u32[]{:S(2)}, u32[]{:S(2)}) async-start(bf16[64,8,2048]{2,1,0:T(8,128)(2,1)} %fusion.3), calls=%async_computation.2 | async-start | bytes 4194304 | tf_op jit(solution)/shard_map/all_to_all | solution.py:243
  405.3 4.7 %copy-start.12 = (f32[64,6]{1,0:T(8,128)S(1)}, f32[64,6]{1,0:T(8,128)}, u32[]{:S(2)}) copy-start(f32[64,6]{1,0:T(8,128)} %copy.94) | copy-start | bytes 4612
  405.3 9.3 %copy-start.1 = (bf16[1,352,2048]{2,1,0:T(8,128)(2,1)S(1)}, bf16[1,352,2048]{2,1,0:T(8,128)(2,1)}, u32[]{:S(2)}) copy-start(bf16[1,352,2048]{2,1,0:T(8,128)(2,1)} %param.31) | copy-start | bytes 4325380
  410.0 3.8 copy-start.6
  410.0 3.8 copy-start.7
Sparse Core Ops, SparseCore 0:
  90.0 38.9 reduce-scatter.1

commit v4 on v3

--- a/solution.py
+++ b/solution.py
@@ -9,12 +9,56 @@
 SPLIT = 4
 STRETCH = 256
 EXP = ("eh", "pz", "c")
-JOINT = True
 PZ_SWAP = True
 C_SWAP = True
 MIX_TWO = True
 MIX_SWAP = True
 PREFIX_SCAN = True
+CHUNKS = 1
+SCAN4 = True
+ONEHOT = True
+
+
+def radix_prefix(decay, state, axis):
+    heads = state.shape[0]
+    cut = state.shape[1] * state.shape[2]
+
+    def join(earlier, later):
+        total = earlier[:, cut] + later[:, cut]
+        carried = jnp.exp(later[:, cut])[:, None] * earlier[:, :cut] + later[:, :cut]
+        return jnp.concatenate([carried, jnp.broadcast_to(total[:, None], (heads, STATE))], axis=1)
+
+    def shifted(packed, shift):
+        count = lax.axis_size(axis)
+        return lax.ppermute(packed, axis, perm=[(i, i + shift) for i in range(count - shift)])
+
+    own = jnp.concatenate(
+        [state.reshape(heads, cut), jnp.broadcast_to(decay[:, None], (heads, STATE))], axis=1
+    )
+    window = join(shifted(own, 3), join(shifted(own, 2), shifted(own, 1)))
+    span = join(window, own)
+    result = join(shifted(span, 12), join(shifted(span, 8), join(shifted(span, 4), window)))
+    return result[:, cut], result[:, :cut].reshape(state.shape)
+
+
+def expert_round(outgoing, expert_gate, expert_up, expert_down):
+    arrived = lax.all_to_all(outgoing, ("seq", "eh"), split_axis=0, concat_axis=0, tiled=True)
+    block = pair_gather(arrived, "pz", PZ_SWAP)
+    block = pair_gather(block, "c", C_SWAP)
+    flat_rows = block.reshape(-1, block.shape[-1])
+    contract = (((1,), (1,)), ((), ()))
+    gate_val = lax.dot_general(
+        flat_rows, expert_gate[0], contract, preferred_element_type=jnp.float32
+    )
+    up_val = lax.dot_general(flat_rows, expert_up[0], contract, preferred_element_type=jnp.float32)
+    activated = (jax.nn.silu(gate_val) * up_val).astype(jnp.bfloat16)
+    piece_out = jnp.dot(activated, expert_down[0], preferred_element_type=jnp.float32).astype(
+        jnp.bfloat16
+    )
+    piece_out = piece_out.reshape(block.shape)
+    piece_sum = pair_reduce(piece_out, "c", C_SWAP)
+    piece_sum = pair_reduce(piece_sum, "pz", PZ_SWAP)
+    return lax.all_to_all(piece_sum, ("seq", "eh"), split_axis=0, concat_axis=0, tiled=True)
 
 
 def scan_prefix(decay, state, axis):
@@ -144,7 +188,9 @@
     zero_state = jnp.zeros((head_count, HEAD_DIM, STATE), jnp.float32)
     end_local, entering_local = lax.scan(advance, zero_state, (totals, block_state))
     device_decay = jnp.sum(totals, axis=0)
-    if PREFIX_SCAN:
+    if SCAN4 and lax.axis_size("seq") <= 16:
+        before = radix_prefix(device_decay, end_local, "seq")
+    elif PREFIX_SCAN:
         before = scan_prefix(device_decay, end_local, "seq")
     else:
         before = prefix(
@@ -205,50 +251,40 @@
     )
     earlier_count = jnp.cumsum(onehot, axis=0) - onehot
     slot_index = jnp.sum(earlier_count * onehot, axis=1)
-    if JOINT:
-        target = flat_routes * capacity + slot_index
-    else:
-        target = (
-            flat_routes % row_experts * (seq_count * capacity)
-            + flat_routes // row_experts * capacity
-            + slot_index
-        )
+    target = flat_routes * capacity + slot_index
     owner_row = jnp.arange(flat_routes.shape[0], dtype=jnp.int32) // TOP
     source = jnp.zeros((experts * capacity,), jnp.int32).at[target].set(owner_row)
     filled = jnp.zeros((experts * capacity,), jnp.bool_).at[target].set(True)
-    outgoing = jnp.where(filled[:, None], normed[source], jnp.zeros((), jnp.bfloat16))
-    if JOINT:
-        outgoing = outgoing.reshape(experts, capacity, -1)
-        arrived = lax.all_to_all(outgoing, ("seq", "eh"), split_axis=0, concat_axis=0, tiled=True)
+    slots = jnp.arange(experts * capacity, dtype=jnp.int32)
+    hits = target.reshape(row_count, TOP)[:, :, None] == slots[None, None, :]
+    if ONEHOT:
+        picks = jnp.any(hits, axis=1).T.astype(jnp.bfloat16)
+        outgoing = jnp.dot(picks, normed, preferred_element_type=jnp.float32).astype(jnp.bfloat16)
     else:
-        outgoing = outgoing.reshape(row_experts, seq_count, capacity, -1)
-        arrived = lax.all_to_all(outgoing, "seq", split_axis=1, concat_axis=1, tiled=True)
-        arrived = lax.all_to_all(arrived, "eh", split_axis=0, concat_axis=0, tiled=True)
-    block = pair_gather(arrived, "pz", PZ_SWAP)
-    block = pair_gather(block, "c", C_SWAP)
-    flat_rows = block.reshape(-1, block.shape[-1])
-    contract = (((1,), (1,)), ((), ()))
-    gate_val = lax.dot_general(
-        flat_rows, expert_gate[0], contract, preferred_element_type=jnp.float32
-    )
-    up_val = lax.dot_general(flat_rows, expert_up[0], contract, preferred_element_type=jnp.float32)
-    activated = (jax.nn.silu(gate_val) * up_val).astype(jnp.bfloat16)
-    piece_out = jnp.dot(activated, expert_down[0], preferred_element_type=jnp.float32).astype(
-        jnp.bfloat16
-    )
-    piece_out = piece_out.reshape(block.shape)
-    piece_sum = pair_reduce(piece_out, "c", C_SWAP)
-    piece_sum = pair_reduce(piece_sum, "pz", PZ_SWAP)
-    if JOINT:
-        returned = lax.all_to_all(piece_sum, ("seq", "eh"), split_axis=0, concat_axis=0, tiled=True)
+        outgoing = jnp.where(filled[:, None], normed[source], jnp.zeros((), jnp.bfloat16))
+    outgoing = outgoing.reshape(experts, capacity, -1)
+    step = capacity // CHUNKS
+    returned = jnp.concatenate(
+        [
+            expert_round(outgoing[:, part * step : (part + 1) * step], expert_gate, expert_up, expert_down)
+            for part in range(CHUNKS)
+        ],
+        axis=1,
+    )
+    if ONEHOT:
+        weights = jnp.sum(jnp.where(hits, route_weight[:, :, None], 0.0), axis=1)
+        expert_sum = jnp.dot(
+            weights,
+            returned.reshape(experts * capacity, -1).astype(jnp.float32),
+            precision=lax.Precision.HIGHEST,
+            preferred_element_type=jnp.float32,
+        )
     else:
-        returned = lax.all_to_all(piece_sum, "eh", split_axis=0, concat_axis=0, tiled=True)
-        returned = lax.all_to_all(returned, "seq", split_axis=1, concat_axis=1, tiled=True)
-    summed = returned.astype(jnp.float32)
-    results = summed.reshape(experts * capacity, -1)[target]
-    expert_sum = jnp.sum(
-        (results * route_weight.reshape(-1)[:, None]).reshape(row_count, TOP, -1), axis=1
-    )
+        summed = returned.astype(jnp.float32)
+        results = summed.reshape(experts * capacity, -1)[target]
+        expert_sum = jnp.sum(
+            (results * route_weight.reshape(-1)[:, None]).reshape(row_count, TOP, -1), axis=1
+        )
     return (stream.astype(jnp.float32) + expert_sum).astype(jnp.bfloat16)
 
 

time: 422 us -> 389 us (0.922)
  local copies, waits for them, and re-layouts: 38 us -> 15.7 us
  other arithmetic: 43.7 us -> 35.6 us
  starting transfers between devices: 41.6 us -> 35.4 us
    gather x3 -> x0, local copies, waits for them, and re-layouts: 15.3 us -> none  [the longest x2 12 us: shards(): results = summed.reshape(experts * capacity, -1)[target]]
    ppermute x5 -> x6, waiting for transfers between devices: 5.92 us -> 0.02 us  [shifted(): lax.ppermute(packed, axis, perm=[(i, i + shift) for i in range(count - sh...]
    reduce_scatter x1, waiting for transfers between devices: 31.9 us -> 37.1 us  [shards(): lax.psum_scatter(projected, ('eh', 'pz'), scatter_dimension=0, tiled=True)]
    scatter x2 -> x0, local copies, waits for them, and re-layouts: 5.06 us -> none  [the longest x1 3.09 us: shards(): jnp.zeros((experts * capacity,), jnp.int32).at[target].set(owner_row)]
    dot_general x3 -> x5, matrix products: 14.5 us -> 19.2 us  [the longest x1 6.35 us: expert_round(): lax.dot_general(flat_rows, expert_up[0], contract, preferred_element_type...]
    ppermute x5 -> x6, starting transfers between devices: 26.6 us -> 22.9 us  [shifted(): lax.ppermute(packed, axis, perm=[(i, i + shift) for i in range(count - sh...]
  transfers between devices with their start and end apart: 12 -> 13, of which waited for: 11 -> 7; matrix products, arithmetic and copies ran while one was open for 4% -> 2% of each run, Pallas kernels for 0% -> 0%
where the time goes in v4:
time: 389 us; the launch traced here: 388 us
  waiting for transfers between devices  199 us (51%)
  blocking collectives  63 us (16%)
  other arithmetic  35.6 us (9%)
  starting transfers between devices  35.4 us (9%)
  matrix products  25.3 us (7%)
  local copies, waits for them, and re-layouts  15.7 us (4%)
  between operations  13.8 us (4%)
    ppermute x5, waiting for transfers between devices, pair_swap(): return lax.ppermute(x, axis, perm=[(0, 1), (1, 0)])  110 us
    all_to_all x1, blocking collectives, expert_round(): lax.all_to_all(outgoing, ('seq', 'eh'), split_axis=0, concat_axis=0, tile...  63 us
    all_to_all x1, waiting for transfers between devices, expert_round(): lax.all_to_all(piece_sum, ('seq', 'eh'), split_axis=0, concat_axis=0, til...  52 us
    reduce_scatter x1, waiting for transfers between devices, shards(): lax.psum_scatter(projected, ('eh', 'pz'), scatter_dimension=0, tiled=True)  37.1 us
    ppermute x6, starting transfers between devices, shifted(): lax.ppermute(packed, axis, perm=[(i, i + shift) for i in range(count - sh...  22.9 us
    convert_element_type x3, other arithmetic, pair_reduce(): (x[0].astype(jnp.float32) + pair_swap(x[1], axis).astype(jnp.float32)).as...  8.89 us
  transfers between devices with their start and end apart: 13, of which 7 were waited for; matrix products, arithmetic and copies ran while one was open for 2% of the time, Pallas kernels for 0%

profile of v4, /device:TPU:1, one launch (start us, length us, event | category | flops | bytes accessed | tf_op | source)
XLA Modules:
  0.0 387.9 jit_solution(12932624976845895621)
XLA Ops:
  6.5 0.9 reshape.136
  7.4 4.8 %reduce-window.14 = f32[4,4,2,128]{3,2,1,0:T(2,128)S(1)} reduce-window(f32[4,4,2,128]{3,2,1,0:T(2,128)S(1)} %reshape.136, f32[]{:T(128)} %constant.33.clone.1), window={size=1x1x1x128 pad=0_0x0_0x0_0x127_0}, to_apply=%region_0.0 | reduce-window | flops 520192 | bytes 32772 | tf_op jit(solution)/shard_map/reduce-window
  12.7 0.3 copy.115
  13.0 0.8 copy-done.7
  13.8 2.1 reshape.153
  15.8 0.5 copy.120
  16.4 0.8 fusion.58
  17.2 1.2 fusion.36
  18.5 3.1 while.13
  18.5 0.7 bitcast_dynamic-update-slice_fusion.2
  19.3 0.7 bitcast_dynamic-update-slice_fusion.2
  20.0 0.7 bitcast_dynamic-update-slice_fusion.2
  20.8 0.7 bitcast_dynamic-update-slice_fusion.2
  21.8 0.7 pad_maximum_fusion.2
  22.5 6.3 %collective-permute-start = (f32[4,8320]{1,0:T(4,128)}, f32[4,8320]{1,0:T(4,128)}, u32[]{:S(2)}, u32[]{:S(2)}) collective-permute-start(f32[4,8320]{1,0:T(4,128)} %pad_maximum_fusion.2), channel_id=1, source_target_pairs={{0,32},{16,48},{32,64},{48,80},{64,96},{80,112},{96,128},{112,144}... | collective-permute-start | bytes 399368 | tf_op jit(solution)/shard_map/ppermute | solution.py:33
  28.8 2.9 collective-permute-start.1
  31.7 4.5 %collective-permute-start.2 = (f32[4,8320]{1,0:T(4,128)}, f32[4,8320]{1,0:T(4,128)}, u32[]{:S(2)}, u32[]{:S(2)}) collective-permute-start(f32[4,8320]{1,0:T(4,128)} %pad_maximum_fusion.2), channel_id=1, source_target_pairs={{0,48},{16,64},{32,80},{48,96},{64,112},{80,128},{96,144},{112,160... | collective-permute-start | bytes 399368 | tf_op jit(solution)/shard_map/ppermute | solution.py:33
  36.3 0.3 fusion.72
  36.7 1.4 fusion.21
  38.0 0.6 reduce_window_sum.46
  38.7 1.4 fusion.69
  40.1 1.2 multiply_add_fusion
  41.4 0.7 pad_maximum_fusion.3
  42.0 4.4 %collective-permute-start.3 = (f32[4,8320]{1,0:T(4,128)}, f32[4,8320]{1,0:T(4,128)}, u32[]{:S(2)}, u32[]{:S(2)}) collective-permute-start(f32[4,8320]{1,0:T(4,128)} %pad_maximum_fusion.3), channel_id=1, source_target_pairs={{0,128},{16,144},{32,160},{48,176},{64,192},{80,208},{96,224},{112... | collective-permute-start | bytes 399368 | tf_op jit(solution)/shard_map/ppermute | solution.py:33
  46.4 2.8 collective-permute-start.4
  49.2 1.9 collective-permute-start.5
  51.2 1.3 subtract_exponential_fusion
  52.4 2.0 copy.125
  54.5 0.9 fusion.62
  55.4 1.3 fusion.51
  56.6 1.8 fusion.24
  58.4 0.7 copy.124
  59.4 1.4 convolution_convert_fusion.1
  60.7 1.9 copy-done.2
  62.6 1.5 dynamic-slice_bitcast_fusion
  64.1 2.6 collective-permute-start.6
  66.8 4.1 %collective-permute-done.6 = bf16[8,64,2048]{2,1,0:T(8,128)(2,1)} collective-permute-done((bf16[8,64,2048]{2,1,0:T(8,128)(2,1)}, bf16[8,64,2048]{2,1,0:T(8,128)(2,1)}, u32[]{:S(2)}, u32[]{:S(2)}) %collective-permute-start.6) | collective-permute-done | bytes 2097184 | tf_op jit(solution)/shard_map/ppermute | solution.py:94
  70.9 4.5 %fusion.4 = bf16[8,64,2048]{2,1,0:T(8,128)(2,1)} fusion(bf16[8,64,2048]{2,1,0:T(8,128)(2,1)} %collective-permute-done.6, bf16[8,2,64,2048]{3,2,1,0:T(8,128)(2,1)} %bitcast.154, s32[]{:T(128)S(6)} %select_n.20), kind=kLoop, calls=%fused_computation.13 | loop fusion | flops 4194304 | bytes 6291460 | tf_op jit(solution)/shard_map/convert_element_type | solution.py:105
  75.8 0.9 reduce-window.16
  77.5 37.1 %reduce-scatter.2.cloned.1.call-done = bf16[1,64,2048]{2,1,0:T(8,128)(2,1)} async-done(((bf16[8,64,2048]{2,1,0:T(8,128)(2,1)}), bf16[1,64,2048]{2,1,0:T(8,128)(2,1)}) %reduce-scatter.2.cloned.1.call-update) | async-done | bytes 262160 | tf_op jit(solution)/shard_map/reduce_scatter | solution.py:231
  114.6 1.1 fusion.32
  115.8 1.7 fusion.5
  117.5 63.0 %all_to_all.10 = bf16[64,8,2048]{2,1,0:T(8,128)(2,1)S(1)} all-to-all(bf16[64,8,2048]{2,1,0:T(8,128)(2,1)S(1)} %fusion.5), channel_id=1, replica_groups=mesh['seq'=16,'eh'=4,'pz'=2,'c'=2] {'seq','eh'}, dimensions={0} | all-to-all | bytes 4194304 | tf_op jit(solution)/shard_map/all_to_all | solution.py:45
  180.6 45.3 %collective-permute-done.7 = bf16[64,8,2048]{2,1,0:T(8,128)(2,1)S(1)} collective-permute-done((bf16[64,8,2048]{2,1,0:T(8,128)(2,1)S(1)}, bf16[64,8,2048]{2,1,0:T(8,128)(2,1)S(1)}, u32[]{:S(2)}, u32[]{:S(2)}) %collective-permute-start.7) | collective-permute-done | bytes 2097184 | tf_op jit(solution)/shard_map/ppermute | solution.py:94
  225.8 0.6 fusion.67
  226.4 2.9 collective-permute-start.8
  229.3 6.8 %collective-permute-done.8 = bf16[2,64,8,2048]{3,2,1,0:T(8,128)(2,1)S(1)} collective-permute-done((bf16[2,64,8,2048]{3,2,1,0:T(8,128)(2,1)S(1)}, bf16[2,64,8,2048]{3,2,1,0:T(8,128)(2,1)S(1)}, u32[]{:S(2)}, u32[]{:S(2)}) %collective-permute-start.8) | collective-permute-done | bytes 4194336 | tf_op jit(solution)/shard_map/ppermute | solution.py:94
  236.1 2.0 copy-done.3
  238.0 6.2 %pad_maximum_fusion = bf16[2,2,64,8,2048]{4,3,2,1,0:T(8,128)(2,1)} fusion(bf16[1,2,64,8,2048]{4,3,2,1,0:T(8,128)(2,1)} %bitcast.156, bf16[1,2,64,8,2048]{4,3,2,1,0:T(8,128)(2,1)S(1)} %get-tuple-element.74), kind=kLoop, calls=%fused_computation.5 | loop fusion | flops 4194304 | bytes 16777216 | tf_op jit(solution)/shard_map/stack | solution.py:99
  244.2 6.4 %fusion.16 = f32[2048,352]{0,1:T(8,128)S(1)} fusion(bf16[2048,2048]{1,0:T(8,128)(2,1)} %bitcast.150, bf16[1,352,2048]{2,1,0:T(8,128)(2,1)} %param.30), kind=kOutput, calls=%fused_computation.33 | convolution fusion | flops 2952790016 | bytes 12713984 | tf_op jit(solution)/shard_map/dot_general | solution.py:53
  250.6 0.3 copy-done.17
  250.8 3.2 fusion.18
  254.0 4.9 %convolution_convert_fusion = bf16[2048,2048]{1,0:T(8,128)(2,1)S(1)} fusion(f32[2048,352]{0,1:T(8,128)S(1)} %fusion.16, f32[2048,352]{0,1:T(8,128)S(1)} %fusion.18, bf16[1,352,2048]{2,1,0:T(8,128)(2,1)S(1)} %copy-done), kind=kOutput, calls=%fused_computation.8 | convolution fusion | flops 2961309696 | bytes 15597568 | tf_op jit(solution)/shard_map/dot_general | solution.py:55
  259.0 0.9 fusion.70
  259.9 0.5 collective-permute-start.9
  260.4 6.8 %collective-permute-done.9 = bf16[2,64,8,2048]{3,2,1,0:T(8,128)(2,1)S(1)} collective-permute-done((bf16[2,64,8,2048]{3,2,1,0:T(8,128)(2,1)S(1)}, bf16[2,64,8,2048]{3,2,1,0:T(8,128)(2,1)S(1)}, u32[]{:S(2)}, u32[]{:S(2)}) %collective-permute-start.9) | collective-permute-done | bytes 4194336 | tf_op jit(solution)/shard_map/ppermute | solution.py:94
  267.2 2.3 fusion.2
  269.7 0.3 collective-permute-start.10
  270.0 46.8 %collective-permute-done.10 = bf16[64,8,2048]{2,1,0:T(8,128)(2,1)S(1)} collective-permute-done((bf16[64,8,2048]{2,1,0:T(8,128)(2,1)S(1)}, bf16[64,8,2048]{2,1,0:T(8,128)(2,1)S(1)}, u32[]{:S(2)}, u32[]{:S(2)}) %collective-permute-start.10) | collective-permute-done | bytes 2097184 | tf_op jit(solution)/shard_map/ppermute | solution.py:94
  316.9 2.1 fusion.3
  319.0 6.2 %all-to-all-start.1 = ((bf16[64,8,2048]{2,1,0:T(8,128)(2,1)}), bf16[64,8,2048]{2,1,0:T(8,128)(2,1)S(1)}, u32[]{:S(2)}, u32[]{:S(2)}) async-start(bf16[64,8,2048]{2,1,0:T(8,128)(2,1)} %fusion.3), calls=%async_computation.2 | async-start | bytes 4194304 | tf_op jit(solution)/shard_map/all_to_all | solution.py:61
  325.3 0.8 select_reduce_fusion
  326.1 52.0 %all-to-all-done.1 = bf16[64,8,2048]{2,1,0:T(8,128)(2,1)S(1)} async-done(((bf16[64,8,2048]{2,1,0:T(8,128)(2,1)}), bf16[64,8,2048]{2,1,0:T(8,128)(2,1)S(1)}, u32[]{:S(2)}, u32[]{:S(2)}) %all-to-all-start.1) | async-done | bytes 2097184 | tf_op jit(solution)/shard_map/all_to_all | solution.py:61
  378.1 3.0 fusion.6
  (84 shorter events, 2.9 us)
Async XLA Ops:
  6.5 247.5 %copy-start = (bf16[1,352,2048]{2,1,0:T(8,128)(2,1)S(1)}, bf16[1,352,2048]{2,1,0:T(8,128)(2,1)}, u32[]{:S(2)}) copy-start(bf16[1,352,2048]{2,1,0:T(8,128)(2,1)} %param.31) | copy-start | bytes 4325380
  6.5 108.1 %reduce-scatter.2.cloned.1.call-start = ((), (), s32[]{:S(2)}) async-start(), calls=%async_computation.3 | async-start | bytes 2359296 | tf_op jit(solution)/shard_map/reduce_scatter | solution.py:231
  13.0 0.8 copy-start.7
  13.7 8.7 %copy-start.14 = (f32[4]{0:T(128)}, f32[4]{0:T(128)S(1)}, u32[]{:S(2)}) copy-start(f32[4]{0:T(128)S(1)} %get-tuple-element.76) | copy-start | bytes 52
  13.7 22.5 %copy-start.9 = (f32[4,1024]{1,0:T(4,128)S(1)}, f32[4,1024]{1,0:T(4,128)}, u32[]{:S(2)}) copy-start(f32[4,1024]{1,0:T(4,128)} %param.21) | copy-start | bytes 49156
  13.8 22.6 %copy-start.5 = (bf16[1024,128]{1,0:T(8,128)(2,1)S(1)}, bf16[1024,128]{1,0:T(8,128)(2,1)}, u32[]{:S(2)}) copy-start(bf16[1024,128]{1,0:T(8,128)(2,1)} %param.20) | copy-start | bytes 786436
  16.4 19.9 %copy-start.6 = (bf16[1024,128]{1,0:T(8,128)(2,1)S(1)}, bf16[1024,128]{1,0:T(8,128)(2,1)}, u32[]{:S(2)}) copy-start(bf16[1024,128]{1,0:T(8,128)(2,1)} %param.19) | copy-start | bytes 786436
  21.6 10.1 %copy-start.10 = (f32[4,4]{1,0:T(4,128)}, f32[4,4]{1,0:T(4,128)S(1)}, u32[]{:S(2)}) copy-start(f32[4,4]{1,0:T(4,128)S(1)} %get-tuple-element.149) | copy-start | bytes 196
  22.5 16.2 %collective-permute-start = (f32[4,8320]{1,0:T(4,128)}, f32[4,8320]{1,0:T(4,128)}, u32[]{:S(2)}, u32[]{:S(2)}) collective-permute-start(f32[4,8320]{1,0:T(4,128)} %pad_maximum_fusion.2), channel_id=1, source_target_pairs={{0,32},{16,48},{32,64},{48,80},{64,96},{80,112},{96,128},{112,144}... | collective-permute-start | bytes 399368 | tf_op jit(solution)/shard_map/ppermute | solution.py:33
  28.8 9.9 %collective-permute-start.1 = (f32[4,8320]{1,0:T(4,128)}, f32[4,8320]{1,0:T(4,128)}, u32[]{:S(2)}, u32[]{:S(2)}) collective-permute-start(f32[4,8320]{1,0:T(4,128)} %pad_maximum_fusion.2), channel_id=1, source_target_pairs={{0,16},{16,32},{32,48},{48,64},{64,80},{80,96},{96,112},{112,128},... | collective-permute-start | bytes 399368 | tf_op jit(solution)/shard_map/ppermute | solution.py:33
  31.7 6.9 %collective-permute-start.2 = (f32[4,8320]{1,0:T(4,128)}, f32[4,8320]{1,0:T(4,128)}, u32[]{:S(2)}, u32[]{:S(2)}) collective-permute-start(f32[4,8320]{1,0:T(4,128)} %pad_maximum_fusion.2), channel_id=1, source_target_pairs={{0,48},{16,64},{32,80},{48,96},{64,112},{80,128},{96,144},{112,160... | collective-permute-start | bytes 399368 | tf_op jit(solution)/shard_map/ppermute | solution.py:33
  36.6 1.4 copy-start.11
  36.6 3.4 copy-start.15
  42.0 12.4 %collective-permute-start.3 = (f32[4,8320]{1,0:T(4,128)}, f32[4,8320]{1,0:T(4,128)}, u32[]{:S(2)}, u32[]{:S(2)}) collective-permute-start(f32[4,8320]{1,0:T(4,128)} %pad_maximum_fusion.3), channel_id=1, source_target_pairs={{0,128},{16,144},{32,160},{48,176},{64,192},{80,208},{96,224},{112... | collective-permute-start | bytes 399368 | tf_op jit(solution)/shard_map/ppermute | solution.py:33
  46.4 8.1 %collective-permute-start.4 = (f32[4,8320]{1,0:T(4,128)}, f32[4,8320]{1,0:T(4,128)}, u32[]{:S(2)}, u32[]{:S(2)}) collective-permute-start(f32[4,8320]{1,0:T(4,128)} %pad_maximum_fusion.3), channel_id=1, source_target_pairs={{0,64},{16,80},{32,96},{48,112},{64,128},{80,144},{96,160},{112,17... | collective-permute-start | bytes 399368 | tf_op jit(solution)/shard_map/ppermute | solution.py:33
  49.2 6.1 %collective-permute-start.5 = (f32[4,8320]{1,0:T(4,128)}, f32[4,8320]{1,0:T(4,128)}, u32[]{:S(2)}, u32[]{:S(2)}) collective-permute-start(f32[4,8320]{1,0:T(4,128)} %pad_maximum_fusion.3), channel_id=1, source_target_pairs={{0,192},{16,208},{32,224},{48,240},{1,193},{17,209},{33,225},{49,2... | collective-permute-start | bytes 399368 | tf_op jit(solution)/shard_map/ppermute | solution.py:33
  55.3 4.0 %copy-start.8 = (bf16[1024,256]{0,1:T(8,128)(2,1)S(1)}, bf16[1024,256]{0,1:T(8,128)(2,1)}, u32[]{:S(2)}) copy-start(bf16[1024,256]{0,1:T(8,128)(2,1)} %copy.125) | copy-start | bytes 1572868
  55.3 4.0 %copy-start.18 = (bf16[256,2048]{1,0:T(8,128)(2,1)S(1)}, bf16[256,2048]{1,0:T(8,128)(2,1)}, u32[]{:S(2)}) copy-start(bf16[256,2048]{1,0:T(8,128)(2,1)} %param.24) | copy-start | bytes 3145732
  60.7 1.9 copy-start.2
  64.1 6.8 %collective-permute-start.6 = (bf16[8,64,2048]{2,1,0:T(8,128)(2,1)}, bf16[8,64,2048]{2,1,0:T(8,128)(2,1)}, u32[]{:S(2)}, u32[]{:S(2)}) collective-permute-start(bf16[8,64,2048]{2,1,0:T(8,128)(2,1)} %dynamic-slice_bitcast_fusion), channel_id=1, source_target_pairs={{0,1},{1,0},{2,3},{3,2},{4,5},{5,4},{6,7},{7,6},{8,9},{9,8},{10,11... | collective-permute-start | bytes 6291464 | tf_op jit(solution)/shard_map/ppermute | solution.py:94
  66.8 8.6 %copy-start.12 = (s32[64,6]{0,1:T(8,128)S(1)}, s32[64,6]{0,1:T(8,128)}, u32[]{:S(2)}) copy-start(s32[64,6]{0,1:T(8,128)} %param.27) | copy-start | bytes 4612
  66.8 47.9 %copy-start.4 = (bf16[64,2048]{1,0:T(8,128)(2,1)S(1)}, bf16[64,2048]{1,0:T(8,128)(2,1)}, u32[]{:S(2)}) copy-start(bf16[64,2048]{1,0:T(8,128)(2,1)} %param.25) | copy-start | bytes 786436
  66.8 49.0 %copy-start.13 = (f32[2048]{0:T(1024)S(1)}, f32[2048]{0:T(1024)}, u32[]{:S(2)}) copy-start(f32[2048]{0:T(1024)} %param.26) | copy-start | bytes 24580
  180.6 45.3 %collective-permute-start.7 = (bf16[64,8,2048]{2,1,0:T(8,128)(2,1)S(1)}, bf16[64,8,2048]{2,1,0:T(8,128)(2,1)S(1)}, u32[]{:S(2)}, u32[]{:S(2)}) collective-permute-start(bf16[64,8,2048]{2,1,0:T(8,128)(2,1)S(1)} %all_to_all.10), channel_id=1, source_target_pairs={{0,2},{2,0},{1,3},{3,1},{4,6},{6,4},{5,7},{7,5},{8,10},{10,8},{9,1... | collective-permute-start | bytes 6291464 | tf_op jit(solution)/shard_map/ppermute | solution.py:94
  226.4 9.7 %collective-permute-start.8 = (bf16[2,64,8,2048]{3,2,1,0:T(8,128)(2,1)S(1)}, bf16[2,64,8,2048]{3,2,1,0:T(8,128)(2,1)S(1)}, u32[]{:S(2)}, u32[]{:S(2)}) collective-permute-start(bf16[2,64,8,2048]{3,2,1,0:T(8,128)(2,1)S(1)} %get-tuple-element.75), channel_id=1, source_target_pairs={{0,1},{1,0},{2,3},{3,2},{4,5},{5,4},{6,7},{7,6},{8,9},{9,8},{10,11... | collective-permute-start | bytes 12582920 | tf_op jit(solution)/shard_map/ppermute | solution.py:94
  236.1 2.0 copy-start.3
  244.2 6.4 %copy-start.1 = (bf16[2,2,64,8,2048]{4,3,2,1,0:T(8,128)(2,1)S(1)}, bf16[2,2,64,8,2048]{4,3,2,1,0:T(8,128)(2,1)}, u32[]{:S(2)}) copy-start(bf16[2,2,64,8,2048]{4,3,2,1,0:T(8,128)(2,1)} %pad_maximum_fusion) | copy-start | bytes 25165828
  244.2 6.6 %copy-start.17 = (bf16[1,352,2048]{2,1,0:T(8,128)(2,1)S(1)}, bf16[1,352,2048]{2,1,0:T(8,128)(2,1)}, u32[]{:S(2)}) copy-start(bf16[1,352,2048]{2,1,0:T(8,128)(2,1)} %param.29) | copy-start | bytes 4325380
  259.9 7.2 %collective-permute-start.9 = (bf16[2,64,8,2048]{3,2,1,0:T(8,128)(2,1)S(1)}, bf16[2,64,8,2048]{3,2,1,0:T(8,128)(2,1)S(1)}, u32[]{:S(2)}, u32[]{:S(2)}) collective-permute-start(bf16[2,64,8,2048]{3,2,1,0:T(8,128)(2,1)S(1)} %bitcast.157), channel_id=1, source_target_pairs={{0,1},{1,0},{2,3},{3,2},{4,5},{5,4},{6,7},{7,6},{8,9},{9,8},{10,11... | collective-permute-start | bytes 12582920 | tf_op jit(solution)/shard_map/ppermute | solution.py:94
  269.7 55.6 %copy-start.16 = (f32[64,6]{0,1:T(8,128)S(1)}, f32[64,6]{0,1:T(8,128)}, u32[]{:S(2)}) copy-start(f32[64,6]{0,1:T(8,128)} %param.28) | copy-start | bytes 4612
  269.7 47.2 %collective-permute-start.10 = (bf16[64,8,2048]{2,1,0:T(8,128)(2,1)S(1)}, bf16[64,8,2048]{2,1,0:T(8,128)(2,1)S(1)}, u32[]{:S(2)}, u32[]{:S(2)}) collective-permute-start(bf16[64,8,2048]{2,1,0:T(8,128)(2,1)S(1)} %slice_bitcast_fusion), channel_id=1, source_target_pairs={{0,2},{2,0},{1,3},{3,1},{4,6},{6,4},{5,7},{7,5},{8,10},{10,8},{9,1... | collective-permute-start | bytes 6291464 | tf_op jit(solution)/shard_map/ppermute | solution.py:94
  319.0 59.1 %all-to-all-start.1 = ((bf16[64,8,2048]{2,1,0:T(8,128)(2,1)}), bf16[64,8,2048]{2,1,0:T(8,128)(2,1)S(1)}, u32[]{:S(2)}, u32[]{:S(2)}) async-start(bf16[64,8,2048]{2,1,0:T(8,128)(2,1)} %fusion.3), calls=%async_computation.2 | async-start | bytes 4194304 | tf_op jit(solution)/shard_map/all_to_all | solution.py:61
Sparse Core Ops, SparseCore 0:
  75.5 39.0 reduce-scatter.1

commit v5 on v4

--- a/solution.py
+++ b/solution.py
@@ -17,6 +17,8 @@
 CHUNKS = 1
 SCAN4 = True
 ONEHOT = True
+CUM_DOT = True
+MIX_PAIR = False
 
 
 def radix_prefix(decay, state, axis):
@@ -162,9 +164,19 @@
     key_rows = write_keys.reshape(blocks, STRETCH, STATE)
     queries = read_queries.reshape(blocks, STRETCH, STATE)
     step_rows = step_size.reshape(head_count, blocks, STRETCH).transpose(1, 0, 2)
-    cumulative = jnp.cumsum(log_decay.reshape(head_count, blocks, STRETCH), axis=2).transpose(
-        1, 0, 2
-    )
+    if CUM_DOT:
+        spots = jnp.arange(STRETCH, dtype=jnp.int32)
+        upper = (spots[:, None] <= spots[None, :]).astype(jnp.float32)
+        cumulative = jnp.dot(
+            log_decay.reshape(head_count * blocks, STRETCH),
+            upper,
+            precision=lax.Precision.HIGHEST,
+            preferred_element_type=jnp.float32,
+        ).reshape(head_count, blocks, STRETCH).transpose(1, 0, 2)
+    else:
+        cumulative = jnp.cumsum(log_decay.reshape(head_count, blocks, STRETCH), axis=2).transpose(
+            1, 0, 2
+        )
     location_values = jnp.arange(STRETCH, dtype=jnp.int32)
     causal = location_values[:, None] >= location_values[None, :]
     scores = jnp.einsum("cin,cjn->cij", queries, key_rows, preferred_element_type=jnp.float32)
@@ -228,9 +240,27 @@
             )
         else:
             projected = lax.psum_scatter(projected, "c", scatter_dimension=0, tiled=True)[0]
-        mixer_out = lax.psum_scatter(
-            projected, ("eh", "pz"), scatter_dimension=0, tiled=True
-        )[0].astype(jnp.float32)
+        if MIX_PAIR:
+            pairs = lax.axis_size("pz")
+            projected = projected.reshape(-1, pairs, row_count, projected.shape[-1]).transpose(1, 0, 2, 3)
+            side = lax.axis_index("pz")
+            projected = pair_reduce(
+                jnp.stack(
+                    [
+                        lax.dynamic_index_in_dim(projected, side, 0, False),
+                        lax.dynamic_index_in_dim(projected, 1 - side, 0, False),
+                    ]
+                ),
+                "pz",
+                True,
+            )
+            mixer_out = lax.psum_scatter(projected, "eh", scatter_dimension=0, tiled=True)[0].astype(
+                jnp.float32
+            )
+        else:
+            mixer_out = lax.psum_scatter(
+                projected, ("eh", "pz"), scatter_dimension=0, tiled=True
+            )[0].astype(jnp.float32)
     else:
         mixer_out = lax.psum_scatter(projected, EXP, scatter_dimension=0, tiled=True).astype(
             jnp.float32

time: 389 us -> 383 us (0.985)
  other arithmetic: 35.6 us -> 29.9 us
    another operation x5 -> x2, other arithmetic: 5.88 us -> 0.95 us
where the time goes in v5:
time: 383 us; the launch traced here: 382 us
  waiting for transfers between devices  198 us (52%)
  blocking collectives  62.5 us (16%)
  starting transfers between devices  36.5 us (10%)
  other arithmetic  29.9 us (8%)
  matrix products  25.5 us (7%)
  local copies, waits for them, and re-layouts  16.2 us (4%)
  between operations  13.8 us (4%)
    ppermute x5, waiting for transfers between devices, pair_swap(): return lax.ppermute(x, axis, perm=[(0, 1), (1, 0)])  109 us
    all_to_all x1, blocking collectives, expert_round(): lax.all_to_all(outgoing, ('seq', 'eh'), split_axis=0, concat_axis=0, tile...  62.5 us
    all_to_all x1, waiting for transfers between devices, expert_round(): lax.all_to_all(piece_sum, ('seq', 'eh'), split_axis=0, concat_axis=0, til...  52.1 us
    reduce_scatter x1, waiting for transfers between devices, shards(): lax.psum_scatter(projected, ('eh', 'pz'), scatter_dimension=0, tiled=True)  36.5 us
    ppermute x6, starting transfers between devices, shifted(): lax.ppermute(packed, axis, perm=[(i, i + shift) for i in range(count - sh...  23.5 us
    convert_element_type x3, other arithmetic, pair_reduce(): (x[0].astype(jnp.float32) + pair_swap(x[1], axis).astype(jnp.float32)).as...  8.89 us
  transfers between devices with their start and end apart: 13, of which 7 were waited for; matrix products, arithmetic and copies ran while one was open for 2% of the time, Pallas kernels for 0%

profile of v5, /device:TPU:1, one launch (start us, length us, event | category | flops | bytes accessed | tf_op | source)
XLA Modules:
  0.0 381.9 jit_solution(2036198029004533113)
XLA Ops:
  6.5 0.8 reshape.130
  7.6 0.3 copy.108
  8.0 0.8 reshape.132
  8.7 0.6 bitcast_multiply_fusion
  9.4 2.1 reshape.147
  11.5 0.5 copy.113
  12.0 1.3 fusion.36
  13.3 3.1 while.13
  13.3 0.7 bitcast_dynamic-update-slice_fusion.2
  14.1 0.7 bitcast_dynamic-update-slice_fusion.2
  14.9 0.7 bitcast_dynamic-update-slice_fusion.2
  15.7 0.7 bitcast_dynamic-update-slice_fusion.2
  16.6 0.7 pad_maximum_fusion.2
  17.3 6.3 %collective-permute-start = (f32[4,8320]{1,0:T(4,128)}, f32[4,8320]{1,0:T(4,128)}, u32[]{:S(2)}, u32[]{:S(2)}) collective-permute-start(f32[4,8320]{1,0:T(4,128)} %pad_maximum_fusion.2), channel_id=1, source_target_pairs={{0,32},{16,48},{32,64},{48,80},{64,96},{80,112},{96,128},{112,144}... | collective-permute-start | bytes 399368 | tf_op jit(solution)/shard_map/ppermute | solution.py:35
  23.6 2.9 collective-permute-start.1
  26.6 4.5 %collective-permute-start.2 = (f32[4,8320]{1,0:T(4,128)}, f32[4,8320]{1,0:T(4,128)}, u32[]{:S(2)}, u32[]{:S(2)}) collective-permute-start(f32[4,8320]{1,0:T(4,128)} %pad_maximum_fusion.2), channel_id=1, source_target_pairs={{0,48},{16,64},{32,80},{48,96},{64,112},{80,128},{96,144},{112,160... | collective-permute-start | bytes 399368 | tf_op jit(solution)/shard_map/ppermute | solution.py:35
  31.1 0.3 fusion.69
  31.4 1.4 fusion.21
  32.9 1.4 fusion.66
  34.3 1.2 multiply_add_fusion
  35.5 0.7 pad_maximum_fusion.3
  36.2 5.0 %collective-permute-start.3 = (f32[4,8320]{1,0:T(4,128)}, f32[4,8320]{1,0:T(4,128)}, u32[]{:S(2)}, u32[]{:S(2)}) collective-permute-start(f32[4,8320]{1,0:T(4,128)} %pad_maximum_fusion.3), channel_id=1, source_target_pairs={{0,128},{16,144},{32,160},{48,176},{64,192},{80,208},{96,224},{112... | collective-permute-start | bytes 399368 | tf_op jit(solution)/shard_map/ppermute | solution.py:35
  41.2 2.9 collective-permute-start.4
  44.0 1.9 collective-permute-start.5
  46.0 1.2 subtract_exponential_fusion
  47.2 0.7 copy.117
  47.9 2.0 copy.119
  50.0 0.8 fusion.59
  50.9 1.3 fusion.51
  52.1 1.8 fusion.24
  53.9 0.7 copy.118
  54.9 1.4 convolution_convert_fusion.1
  56.2 1.9 copy-done.2
  58.2 1.5 dynamic-slice_bitcast_fusion
  59.6 2.6 collective-permute-start.6
  62.3 4.1 %collective-permute-done.6 = bf16[8,64,2048]{2,1,0:T(8,128)(2,1)} collective-permute-done((bf16[8,64,2048]{2,1,0:T(8,128)(2,1)}, bf16[8,64,2048]{2,1,0:T(8,128)(2,1)}, u32[]{:S(2)}, u32[]{:S(2)}) %collective-permute-start.6) | collective-permute-done | bytes 2097184 | tf_op jit(solution)/shard_map/ppermute | solution.py:96
  66.4 4.5 %fusion.4 = bf16[8,64,2048]{2,1,0:T(8,128)(2,1)} fusion(bf16[8,64,2048]{2,1,0:T(8,128)(2,1)} %collective-permute-done.6, bf16[8,2,64,2048]{3,2,1,0:T(8,128)(2,1)} %bitcast.153, s32[]{:T(128)S(6)} %select_n.20), kind=kLoop, calls=%fused_computation.13 | loop fusion | flops 4194304 | bytes 6291460 | tf_op jit(solution)/shard_map/convert_element_type | solution.py:107
  71.3 0.9 reduce-window.6
  73.0 36.5 %reduce-scatter.2.cloned.1.call-done = bf16[1,64,2048]{2,1,0:T(8,128)(2,1)} async-done(((bf16[8,64,2048]{2,1,0:T(8,128)(2,1)}), bf16[1,64,2048]{2,1,0:T(8,128)(2,1)}) %reduce-scatter.2.cloned.1.call-update) | async-done | bytes 262160 | tf_op jit(solution)/shard_map/reduce_scatter | solution.py:261
  109.5 1.1 fusion.32
  110.6 1.7 fusion.5
  112.4 62.5 %all_to_all.10 = bf16[64,8,2048]{2,1,0:T(8,128)(2,1)S(1)} all-to-all(bf16[64,8,2048]{2,1,0:T(8,128)(2,1)S(1)} %fusion.5), channel_id=1, replica_groups=mesh['seq'=16,'eh'=4,'pz'=2,'c'=2] {'seq','eh'}, dimensions={0} | all-to-all | bytes 4194304 | tf_op jit(solution)/shard_map/all_to_all | solution.py:47
  174.8 44.5 %collective-permute-done.7 = bf16[64,8,2048]{2,1,0:T(8,128)(2,1)S(1)} collective-permute-done((bf16[64,8,2048]{2,1,0:T(8,128)(2,1)S(1)}, bf16[64,8,2048]{2,1,0:T(8,128)(2,1)S(1)}, u32[]{:S(2)}, u32[]{:S(2)}) %collective-permute-start.7) | collective-permute-done | bytes 2097184 | tf_op jit(solution)/shard_map/ppermute | solution.py:96
  219.3 0.6 fusion.64
  219.9 3.6 collective-permute-start.8
  223.5 6.8 %collective-permute-done.8 = bf16[2,64,8,2048]{3,2,1,0:T(8,128)(2,1)S(1)} collective-permute-done((bf16[2,64,8,2048]{3,2,1,0:T(8,128)(2,1)S(1)}, bf16[2,64,8,2048]{3,2,1,0:T(8,128)(2,1)S(1)}, u32[]{:S(2)}, u32[]{:S(2)}) %collective-permute-start.8) | collective-permute-done | bytes 4194336 | tf_op jit(solution)/shard_map/ppermute | solution.py:96
  230.3 2.0 copy-done.3
  232.3 6.2 %pad_maximum_fusion = bf16[2,2,64,8,2048]{4,3,2,1,0:T(8,128)(2,1)} fusion(bf16[1,2,64,8,2048]{4,3,2,1,0:T(8,128)(2,1)} %bitcast.155, bf16[1,2,64,8,2048]{4,3,2,1,0:T(8,128)(2,1)S(1)} %get-tuple-element.74), kind=kLoop, calls=%fused_computation.5 | loop fusion | flops 4194304 | bytes 16777216 | tf_op jit(solution)/shard_map/stack | solution.py:101
  238.5 6.4 %fusion.16 = f32[2048,352]{0,1:T(8,128)S(1)} fusion(bf16[2048,2048]{1,0:T(8,128)(2,1)} %bitcast.149, bf16[1,352,2048]{2,1,0:T(8,128)(2,1)} %param.30), kind=kOutput, calls=%fused_computation.33 | convolution fusion | flops 2952790016 | bytes 12713984 | tf_op jit(solution)/shard_map/dot_general | solution.py:55
  244.8 0.3 copy-done.12
  245.1 3.2 fusion.18
  248.3 4.9 %convolution_convert_fusion = bf16[2048,2048]{1,0:T(8,128)(2,1)S(1)} fusion(f32[2048,352]{0,1:T(8,128)S(1)} %fusion.16, f32[2048,352]{0,1:T(8,128)S(1)} %fusion.18, bf16[1,352,2048]{2,1,0:T(8,128)(2,1)S(1)} %copy-done), kind=kOutput, calls=%fused_computation.8 | convolution fusion | flops 2961309696 | bytes 15597568 | tf_op jit(solution)/shard_map/dot_general | solution.py:57
  253.2 0.9 fusion.67
  254.2 0.5 collective-permute-start.9
  254.6 6.8 %collective-permute-done.9 = bf16[2,64,8,2048]{3,2,1,0:T(8,128)(2,1)S(1)} collective-permute-done((bf16[2,64,8,2048]{3,2,1,0:T(8,128)(2,1)S(1)}, bf16[2,64,8,2048]{3,2,1,0:T(8,128)(2,1)S(1)}, u32[]{:S(2)}, u32[]{:S(2)}) %collective-permute-start.9) | collective-permute-done | bytes 4194336 | tf_op jit(solution)/shard_map/ppermute | solution.py:96
  261.4 2.3 fusion.2
  263.7 0.2 slice_bitcast_fusion
  264.0 0.3 collective-permute-start.10
  264.3 46.8 %collective-permute-done.10 = bf16[64,8,2048]{2,1,0:T(8,128)(2,1)S(1)} collective-permute-done((bf16[64,8,2048]{2,1,0:T(8,128)(2,1)S(1)}, bf16[64,8,2048]{2,1,0:T(8,128)(2,1)S(1)}, u32[]{:S(2)}, u32[]{:S(2)}) %collective-permute-start.10) | collective-permute-done | bytes 2097184 | tf_op jit(solution)/shard_map/ppermute | solution.py:96
  311.1 2.1 fusion.3
  313.3 5.9 %all-to-all-start.1 = ((bf16[64,8,2048]{2,1,0:T(8,128)(2,1)}), bf16[64,8,2048]{2,1,0:T(8,128)(2,1)S(1)}, u32[]{:S(2)}, u32[]{:S(2)}) async-start(bf16[64,8,2048]{2,1,0:T(8,128)(2,1)} %fusion.3), calls=%async_computation.2 | async-start | bytes 4194304 | tf_op jit(solution)/shard_map/all_to_all | solution.py:63
  319.2 0.8 select_reduce_fusion
  320.0 52.1 %all-to-all-done.1 = bf16[64,8,2048]{2,1,0:T(8,128)(2,1)S(1)} async-done(((bf16[64,8,2048]{2,1,0:T(8,128)(2,1)}), bf16[64,8,2048]{2,1,0:T(8,128)(2,1)S(1)}, u32[]{:S(2)}, u32[]{:S(2)}) %all-to-all-start.1) | async-done | bytes 2097184 | tf_op jit(solution)/shard_map/all_to_all | solution.py:63
  372.1 3.0 fusion.6
  (71 shorter events, 2.5 us)
Async XLA Ops:
  6.5 241.7 %copy-start = (bf16[1,352,2048]{2,1,0:T(8,128)(2,1)S(1)}, bf16[1,352,2048]{2,1,0:T(8,128)(2,1)}, u32[]{:S(2)}) copy-start(bf16[1,352,2048]{2,1,0:T(8,128)(2,1)} %param.31) | copy-start | bytes 4325380
  6.5 102.9 %reduce-scatter.2.cloned.1.call-start = ((), (), s32[]{:S(2)}) async-start(), calls=%async_computation.3 | async-start | bytes 2359296 | tf_op jit(solution)/shard_map/reduce_scatter | solution.py:261
  7.9 1.5 copy-start.7
  9.4 21.7 %copy-start.5 = (bf16[1024,128]{1,0:T(8,128)(2,1)S(1)}, bf16[1024,128]{1,0:T(8,128)(2,1)}, u32[]{:S(2)}) copy-start(bf16[1024,128]{1,0:T(8,128)(2,1)} %param.20) | copy-start | bytes 786436
  12.0 19.1 %copy-start.6 = (bf16[1024,128]{1,0:T(8,128)(2,1)S(1)}, bf16[1024,128]{1,0:T(8,128)(2,1)}, u32[]{:S(2)}) copy-start(bf16[1024,128]{1,0:T(8,128)(2,1)} %param.19) | copy-start | bytes 786436
  17.3 15.5 %collective-permute-start = (f32[4,8320]{1,0:T(4,128)}, f32[4,8320]{1,0:T(4,128)}, u32[]{:S(2)}, u32[]{:S(2)}) collective-permute-start(f32[4,8320]{1,0:T(4,128)} %pad_maximum_fusion.2), channel_id=1, source_target_pairs={{0,32},{16,48},{32,64},{48,80},{64,96},{80,112},{96,128},{112,144}... | collective-permute-start | bytes 399368 | tf_op jit(solution)/shard_map/ppermute | solution.py:35
  23.6 9.2 %collective-permute-start.1 = (f32[4,8320]{1,0:T(4,128)}, f32[4,8320]{1,0:T(4,128)}, u32[]{:S(2)}, u32[]{:S(2)}) collective-permute-start(f32[4,8320]{1,0:T(4,128)} %pad_maximum_fusion.2), channel_id=1, source_target_pairs={{0,16},{16,32},{32,48},{48,64},{64,80},{80,96},{96,112},{112,128},... | collective-permute-start | bytes 399368 | tf_op jit(solution)/shard_map/ppermute | solution.py:35
  26.6 6.3 %collective-permute-start.2 = (f32[4,8320]{1,0:T(4,128)}, f32[4,8320]{1,0:T(4,128)}, u32[]{:S(2)}, u32[]{:S(2)}) collective-permute-start(f32[4,8320]{1,0:T(4,128)} %pad_maximum_fusion.2), channel_id=1, source_target_pairs={{0,48},{16,64},{32,80},{48,96},{64,112},{80,128},{96,144},{112,160... | collective-permute-start | bytes 399368 | tf_op jit(solution)/shard_map/ppermute | solution.py:35
  36.2 13.8 %collective-permute-start.3 = (f32[4,8320]{1,0:T(4,128)}, f32[4,8320]{1,0:T(4,128)}, u32[]{:S(2)}, u32[]{:S(2)}) collective-permute-start(f32[4,8320]{1,0:T(4,128)} %pad_maximum_fusion.3), channel_id=1, source_target_pairs={{0,128},{16,144},{32,160},{48,176},{64,192},{80,208},{96,224},{112... | collective-permute-start | bytes 399368 | tf_op jit(solution)/shard_map/ppermute | solution.py:35
  41.2 8.8 %collective-permute-start.4 = (f32[4,8320]{1,0:T(4,128)}, f32[4,8320]{1,0:T(4,128)}, u32[]{:S(2)}, u32[]{:S(2)}) collective-permute-start(f32[4,8320]{1,0:T(4,128)} %pad_maximum_fusion.3), channel_id=1, source_target_pairs={{0,64},{16,80},{32,96},{48,112},{64,128},{80,144},{96,160},{112,17... | collective-permute-start | bytes 399368 | tf_op jit(solution)/shard_map/ppermute | solution.py:35
  44.0 6.8 %collective-permute-start.5 = (f32[4,8320]{1,0:T(4,128)}, f32[4,8320]{1,0:T(4,128)}, u32[]{:S(2)}, u32[]{:S(2)}) collective-permute-start(f32[4,8320]{1,0:T(4,128)} %pad_maximum_fusion.3), channel_id=1, source_target_pairs={{0,192},{16,208},{32,224},{48,240},{1,193},{17,209},{33,225},{49,2... | collective-permute-start | bytes 399368 | tf_op jit(solution)/shard_map/ppermute | solution.py:35
  50.8 4.0 %copy-start.8 = (bf16[1024,256]{0,1:T(8,128)(2,1)S(1)}, bf16[1024,256]{0,1:T(8,128)(2,1)}, u32[]{:S(2)}) copy-start(bf16[1024,256]{0,1:T(8,128)(2,1)} %copy.119) | copy-start | bytes 1572868
  50.8 4.0 %copy-start.13 = (bf16[256,2048]{1,0:T(8,128)(2,1)S(1)}, bf16[256,2048]{1,0:T(8,128)(2,1)}, u32[]{:S(2)}) copy-start(bf16[256,2048]{1,0:T(8,128)(2,1)} %param.24) | copy-start | bytes 3145732
  56.2 1.9 copy-start.2
  59.6 6.8 %collective-permute-start.6 = (bf16[8,64,2048]{2,1,0:T(8,128)(2,1)}, bf16[8,64,2048]{2,1,0:T(8,128)(2,1)}, u32[]{:S(2)}, u32[]{:S(2)}) collective-permute-start(bf16[8,64,2048]{2,1,0:T(8,128)(2,1)} %dynamic-slice_bitcast_fusion), channel_id=1, source_target_pairs={{0,1},{1,0},{2,3},{3,2},{4,5},{5,4},{6,7},{7,6},{8,9},{9,8},{10,11... | collective-permute-start | bytes 6291464 | tf_op jit(solution)/shard_map/ppermute | solution.py:96
  62.3 8.6 %copy-start.9 = (s32[64,6]{0,1:T(8,128)S(1)}, s32[64,6]{0,1:T(8,128)}, u32[]{:S(2)}) copy-start(s32[64,6]{0,1:T(8,128)} %param.27) | copy-start | bytes 4612
  62.3 47.2 %copy-start.4 = (bf16[64,2048]{1,0:T(8,128)(2,1)S(1)}, bf16[64,2048]{1,0:T(8,128)(2,1)}, u32[]{:S(2)}) copy-start(bf16[64,2048]{1,0:T(8,128)(2,1)} %param.25) | copy-start | bytes 786436
  62.3 48.3 %copy-start.10 = (f32[2048]{0:T(1024)S(1)}, f32[2048]{0:T(1024)}, u32[]{:S(2)}) copy-start(f32[2048]{0:T(1024)} %param.26) | copy-start | bytes 24580
  174.8 44.5 %collective-permute-start.7 = (bf16[64,8,2048]{2,1,0:T(8,128)(2,1)S(1)}, bf16[64,8,2048]{2,1,0:T(8,128)(2,1)S(1)}, u32[]{:S(2)}, u32[]{:S(2)}) collective-permute-start(bf16[64,8,2048]{2,1,0:T(8,128)(2,1)S(1)} %all_to_all.10), channel_id=1, source_target_pairs={{0,2},{2,0},{1,3},{3,1},{4,6},{6,4},{5,7},{7,5},{8,10},{10,8},{9,1... | collective-permute-start | bytes 6291464 | tf_op jit(solution)/shard_map/ppermute | solution.py:96
  219.9 10.4 %collective-permute-start.8 = (bf16[2,64,8,2048]{3,2,1,0:T(8,128)(2,1)S(1)}, bf16[2,64,8,2048]{3,2,1,0:T(8,128)(2,1)S(1)}, u32[]{:S(2)}, u32[]{:S(2)}) collective-permute-start(bf16[2,64,8,2048]{3,2,1,0:T(8,128)(2,1)S(1)} %get-tuple-element.75), channel_id=1, source_target_pairs={{0,1},{1,0},{2,3},{3,2},{4,5},{5,4},{6,7},{7,6},{8,9},{9,8},{10,11... | collective-permute-start | bytes 12582920 | tf_op jit(solution)/shard_map/ppermute | solution.py:96
  230.3 2.0 copy-start.3
  238.5 6.4 %copy-start.1 = (bf16[2,2,64,8,2048]{4,3,2,1,0:T(8,128)(2,1)S(1)}, bf16[2,2,64,8,2048]{4,3,2,1,0:T(8,128)(2,1)}, u32[]{:S(2)}) copy-start(bf16[2,2,64,8,2048]{4,3,2,1,0:T(8,128)(2,1)} %pad_maximum_fusion) | copy-start | bytes 25165828
  238.5 6.6 %copy-start.12 = (bf16[1,352,2048]{2,1,0:T(8,128)(2,1)S(1)}, bf16[1,352,2048]{2,1,0:T(8,128)(2,1)}, u32[]{:S(2)}) copy-start(bf16[1,352,2048]{2,1,0:T(8,128)(2,1)} %param.29) | copy-start | bytes 4325380
  254.2 7.2 %collective-permute-start.9 = (bf16[2,64,8,2048]{3,2,1,0:T(8,128)(2,1)S(1)}, bf16[2,64,8,2048]{3,2,1,0:T(8,128)(2,1)S(1)}, u32[]{:S(2)}, u32[]{:S(2)}) collective-permute-start(bf16[2,64,8,2048]{3,2,1,0:T(8,128)(2,1)S(1)} %bitcast.156), channel_id=1, source_target_pairs={{0,1},{1,0},{2,3},{3,2},{4,5},{5,4},{6,7},{7,6},{8,9},{9,8},{10,11... | collective-permute-start | bytes 12582920 | tf_op jit(solution)/shard_map/ppermute | solution.py:96
  264.0 55.2 %copy-start.11 = (f32[64,6]{0,1:T(8,128)S(1)}, f32[64,6]{0,1:T(8,128)}, u32[]{:S(2)}) copy-start(f32[64,6]{0,1:T(8,128)} %param.28) | copy-start | bytes 4612
  264.0 47.2 %collective-permute-start.10 = (bf16[64,8,2048]{2,1,0:T(8,128)(2,1)S(1)}, bf16[64,8,2048]{2,1,0:T(8,128)(2,1)S(1)}, u32[]{:S(2)}, u32[]{:S(2)}) collective-permute-start(bf16[64,8,2048]{2,1,0:T(8,128)(2,1)S(1)} %slice_bitcast_fusion), channel_id=1, source_target_pairs={{0,2},{2,0},{1,3},{3,1},{4,6},{6,4},{5,7},{7,5},{8,10},{10,8},{9,1... | collective-permute-start | bytes 6291464 | tf_op jit(solution)/shard_map/ppermute | solution.py:96
  313.3 58.8 %all-to-all-start.1 = ((bf16[64,8,2048]{2,1,0:T(8,128)(2,1)}), bf16[64,8,2048]{2,1,0:T(8,128)(2,1)S(1)}, u32[]{:S(2)}, u32[]{:S(2)}) async-start(bf16[64,8,2048]{2,1,0:T(8,128)(2,1)} %fusion.3), calls=%async_computation.2 | async-start | bytes 4194304 | tf_op jit(solution)/shard_map/all_to_all | solution.py:63
Sparse Core Ops, SparseCore 0:
  71.0 38.3 reduce-scatter.1

commit v6 on v5

--- a/solution.py
+++ b/solution.py
@@ -19,6 +19,8 @@
 ONEHOT = True
 CUM_DOT = True
 MIX_PAIR = False
+C_EARLY = True
+UNROLL = False
 
 
 def radix_prefix(decay, state, axis):
@@ -45,8 +47,14 @@
 
 def expert_round(outgoing, expert_gate, expert_up, expert_down):
     arrived = lax.all_to_all(outgoing, ("seq", "eh"), split_axis=0, concat_axis=0, tiled=True)
-    block = pair_gather(arrived, "pz", PZ_SWAP)
-    block = pair_gather(block, "c", C_SWAP)
+    if C_EARLY:
+        partner = pair_swap(arrived, "pz")
+        block = jnp.stack(
+            [jnp.stack([arrived, partner]), jnp.stack([pair_swap(arrived, "c"), pair_swap(partner, "c")])]
+        )
+    else:
+        block = pair_gather(arrived, "pz", PZ_SWAP)
+        block = pair_gather(block, "c", C_SWAP)
     flat_rows = block.reshape(-1, block.shape[-1])
     contract = (((1,), (1,)), ((), ()))
     gate_val = lax.dot_general(
@@ -198,7 +206,7 @@
         return (jnp.exp(block_total)[:, None, None] * carry_state + fresh_state, carry_state)
 
     zero_state = jnp.zeros((head_count, HEAD_DIM, STATE), jnp.float32)
-    end_local, entering_local = lax.scan(advance, zero_state, (totals, block_state))
+    end_local, entering_local = lax.scan(advance, zero_state, (totals, block_state), unroll=UNROLL)
     device_decay = jnp.sum(totals, axis=0)
     if SCAN4 and lax.axis_size("seq") <= 16:
         before = radix_prefix(device_decay, end_local, "seq")

time: 383 us -> 380 us (level)
  waiting for transfers between devices: 198 us -> 192 us
    ppermute x5 -> x6, waiting for transfers between devices: 109 us -> 103 us  [pair_swap(): return lax.ppermute(x, axis, perm=[(0, 1), (1, 0)])]
    ppermute x5 -> x6, starting transfers between devices: 7.05 us -> 9.58 us  [pair_swap(): return lax.ppermute(x, axis, perm=[(0, 1), (1, 0)])]
    another operation x4 -> x5, other arithmetic: 7.69 us -> 9.84 us  [the longest x3 8.89 us: expert_round(): jnp.stack([jnp.stack([arrived, partner]), jnp.stack([pair_swap(arrived, '...]
  transfers between devices with their start and end apart: 13 -> 14, of which waited for: 7 -> 7; matrix products, arithmetic and copies ran while one was open for 2% -> 3% of each run, Pallas kernels for 0% -> 0%
where the time goes in v6:
time: 380 us; the launch traced here: 379 us
  waiting for transfers between devices  192 us (51%)
  blocking collectives  62.5 us (16%)
  starting transfers between devices  39 us (10%)
  other arithmetic  32 us (8%)
  matrix products  25.7 us (7%)
  local copies, waits for them, and re-layouts  14.2 us (4%)
  between operations  13.8 us (4%)
    ppermute x6, waiting for transfers between devices, pair_swap(): return lax.ppermute(x, axis, perm=[(0, 1), (1, 0)])  103 us
    all_to_all x1, blocking collectives, expert_round(): lax.all_to_all(outgoing, ('seq', 'eh'), split_axis=0, concat_axis=0, tile...  62.5 us
    all_to_all x1, waiting for transfers between devices, expert_round(): lax.all_to_all(piece_sum, ('seq', 'eh'), split_axis=0, concat_axis=0, til...  52 us
    reduce_scatter x1, waiting for transfers between devices, shards(): lax.psum_scatter(projected, ('eh', 'pz'), scatter_dimension=0, tiled=True)  36.5 us
    ppermute x6, starting transfers between devices, shifted(): lax.ppermute(packed, axis, perm=[(i, i + shift) for i in range(count - sh...  23.5 us
    ppermute x6, starting transfers between devices, pair_swap(): return lax.ppermute(x, axis, perm=[(0, 1), (1, 0)])  9.58 us
    another operation x3, other arithmetic, expert_round(): jnp.stack([jnp.stack([arrived, partner]), jnp.stack([pair_swap(arrived, '...  8.89 us
    convert_element_type x3, other arithmetic, pair_reduce(): (x[0].astype(jnp.float32) + pair_swap(x[1], axis).astype(jnp.float32)).as...  8.89 us
  transfers between devices with their start and end apart: 14, of which 7 were waited for; matrix products, arithmetic and copies ran while one was open for 3% of the time, Pallas kernels for 0%

profile of v6, /device:TPU:1, one launch (start us, length us, event | category | flops | bytes accessed | tf_op | source)
XLA Modules:
  0.0 378.8 jit_solution(5184521239784837130)
XLA Ops:
  6.5 0.8 reshape.130
  7.6 0.3 copy.108
  8.0 0.8 reshape.132
  8.7 0.6 bitcast_multiply_fusion
  9.4 2.1 reshape.147
  11.5 0.5 copy.113
  12.0 1.3 fusion.35
  13.3 3.1 while.13
  13.3 0.7 bitcast_dynamic-update-slice_fusion.2
  14.1 0.7 bitcast_dynamic-update-slice_fusion.2
  14.9 0.7 bitcast_dynamic-update-slice_fusion.2
  15.7 0.7 bitcast_dynamic-update-slice_fusion.2
  16.6 0.7 pad_maximum_fusion.1
  17.3 6.3 %collective-permute-start = (f32[4,8320]{1,0:T(4,128)}, f32[4,8320]{1,0:T(4,128)}, u32[]{:S(2)}, u32[]{:S(2)}) collective-permute-start(f32[4,8320]{1,0:T(4,128)} %pad_maximum_fusion.1), channel_id=1, source_target_pairs={{0,32},{16,48},{32,64},{48,80},{64,96},{80,112},{96,128},{112,144}... | collective-permute-start | bytes 399368 | tf_op jit(solution)/shard_map/ppermute | solution.py:37
  23.6 2.9 collective-permute-start.1
  26.6 4.5 %collective-permute-start.2 = (f32[4,8320]{1,0:T(4,128)}, f32[4,8320]{1,0:T(4,128)}, u32[]{:S(2)}, u32[]{:S(2)}) collective-permute-start(f32[4,8320]{1,0:T(4,128)} %pad_maximum_fusion.1), channel_id=1, source_target_pairs={{0,48},{16,64},{32,80},{48,96},{64,112},{80,128},{96,144},{112,160... | collective-permute-start | bytes 399368 | tf_op jit(solution)/shard_map/ppermute | solution.py:37
  31.1 0.3 fusion.66
  31.4 1.4 fusion.20
  32.9 1.4 fusion.63
  34.3 1.2 multiply_add_fusion
  35.5 0.7 pad_maximum_fusion.2
  36.2 5.0 %collective-permute-start.3 = (f32[4,8320]{1,0:T(4,128)}, f32[4,8320]{1,0:T(4,128)}, u32[]{:S(2)}, u32[]{:S(2)}) collective-permute-start(f32[4,8320]{1,0:T(4,128)} %pad_maximum_fusion.2), channel_id=1, source_target_pairs={{0,128},{16,144},{32,160},{48,176},{64,192},{80,208},{96,224},{112... | collective-permute-start | bytes 399368 | tf_op jit(solution)/shard_map/ppermute | solution.py:37
  41.2 2.9 collective-permute-start.4
  44.0 1.9 collective-permute-start.5
  46.0 1.2 subtract_exponential_fusion
  47.2 0.7 copy.117
  47.9 2.0 copy.119
  50.0 0.8 fusion.58
  50.9 1.3 fusion.50
  52.1 1.8 fusion.23
  53.9 0.7 copy.118
  54.9 1.4 convolution_convert_fusion.1
  56.2 1.9 copy-done.2
  58.2 1.5 dynamic-slice_bitcast_fusion
  59.6 2.6 collective-permute-start.6
  62.3 4.1 %collective-permute-done.6 = bf16[8,64,2048]{2,1,0:T(8,128)(2,1)} collective-permute-done((bf16[8,64,2048]{2,1,0:T(8,128)(2,1)}, bf16[8,64,2048]{2,1,0:T(8,128)(2,1)}, u32[]{:S(2)}, u32[]{:S(2)}) %collective-permute-start.6) | collective-permute-done | bytes 2097184 | tf_op jit(solution)/shard_map/ppermute | solution.py:104
  66.4 4.5 %fusion.4 = bf16[8,64,2048]{2,1,0:T(8,128)(2,1)} fusion(bf16[8,64,2048]{2,1,0:T(8,128)(2,1)} %collective-permute-done.6, bf16[8,2,64,2048]{3,2,1,0:T(8,128)(2,1)} %bitcast.157, s32[]{:T(128)S(6)} %select_n.20), kind=kLoop, calls=%fused_computation.14 | loop fusion | flops 4194304 | bytes 6291460 | tf_op jit(solution)/shard_map/convert_element_type | solution.py:115
  71.3 0.9 reduce-window.6
  73.0 36.5 %reduce-scatter.2.cloned.1.call-done = bf16[1,64,2048]{2,1,0:T(8,128)(2,1)} async-done(((bf16[8,64,2048]{2,1,0:T(8,128)(2,1)}), bf16[1,64,2048]{2,1,0:T(8,128)(2,1)}) %reduce-scatter.2.cloned.1.call-update) | async-done | bytes 262160 | tf_op jit(solution)/shard_map/reduce_scatter | solution.py:269
  109.5 1.1 fusion.31
  110.6 1.7 fusion.6
  112.4 62.5 %all_to_all.10 = bf16[64,8,2048]{2,1,0:T(8,128)(2,1)S(1)} all-to-all(bf16[64,8,2048]{2,1,0:T(8,128)(2,1)S(1)} %fusion.6), channel_id=1, replica_groups=mesh['seq'=16,'eh'=4,'pz'=2,'c'=2] {'seq','eh'}, dimensions={0} | all-to-all | bytes 4194304 | tf_op jit(solution)/shard_map/all_to_all | solution.py:49
  174.8 2.6 collective-permute-start.8
  177.4 41.9 %collective-permute-done.7 = bf16[64,8,2048]{2,1,0:T(8,128)(2,1)S(1)} collective-permute-done((bf16[64,8,2048]{2,1,0:T(8,128)(2,1)S(1)}, bf16[64,8,2048]{2,1,0:T(8,128)(2,1)S(1)}, u32[]{:S(2)}, u32[]{:S(2)}) %collective-permute-start.7) | collective-permute-done | bytes 2097184 | tf_op jit(solution)/shard_map/ppermute | solution.py:104
  219.3 3.5 collective-permute-start.9
  222.9 0.4 maximum_bitcast_fusion
  223.3 3.4 collective-permute-done.9
  226.6 2.3 maximum_bitcast_fusion.1
  229.0 6.2 %pad_maximum_fusion = bf16[2,2,64,8,2048]{4,3,2,1,0:T(8,128)(2,1)} fusion(bf16[1,2,64,8,2048]{4,3,2,1,0:T(8,128)(2,1)} %maximum_bitcast_fusion.1, bf16[1,2,64,8,2048]{4,3,2,1,0:T(8,128)(2,1)S(1)} %maximum_bitcast_fusion), kind=kLoop, calls=%fused_computation.5 | loop fusion | flops 4194304 | bytes 16777216 | tf_op jit(solution)/shard_map/stack | solution.py:52
  235.2 6.4 %fusion.18 = f32[2048,352]{0,1:T(8,128)S(1)} fusion(bf16[2048,2048]{1,0:T(8,128)(2,1)} %bitcast.153, bf16[1,352,2048]{2,1,0:T(8,128)(2,1)} %param.29), kind=kOutput, calls=%fused_computation.36 | convolution fusion | flops 2952790016 | bytes 12713984 | tf_op jit(solution)/shard_map/dot_general | solution.py:60
  241.5 0.3 copy-done.11
  241.8 3.5 fusion.5
  245.3 4.8 %convolution_convert_fusion = bf16[2048,2048]{1,0:T(8,128)(2,1)S(1)} fusion(bf16[2048,352]{0,1:T(8,128)(2,1)S(1)} %fusion.5, bf16[1,352,2048]{2,1,0:T(8,128)(2,1)S(1)} %copy-done), kind=kOutput, calls=%fused_computation.8 | convolution fusion | flops 2956984320 | bytes 11272192 | tf_op jit(solution)/shard_map/dot_general | solution.py:65
  250.1 0.9 fusion.64
  251.1 0.7 collective-permute-start.10
  251.8 6.8 %collective-permute-done.10 = bf16[2,64,8,2048]{3,2,1,0:T(8,128)(2,1)S(1)} collective-permute-done((bf16[2,64,8,2048]{3,2,1,0:T(8,128)(2,1)S(1)}, bf16[2,64,8,2048]{3,2,1,0:T(8,128)(2,1)S(1)}, u32[]{:S(2)}, u32[]{:S(2)}) %collective-permute-start.10) | collective-permute-done | bytes 4194336 | tf_op jit(solution)/shard_map/ppermute | solution.py:104
  258.5 2.3 fusion.2
  260.8 0.2 slice_bitcast_fusion
  261.2 46.8 %collective-permute-done.11 = bf16[64,8,2048]{2,1,0:T(8,128)(2,1)S(1)} collective-permute-done((bf16[64,8,2048]{2,1,0:T(8,128)(2,1)S(1)}, bf16[64,8,2048]{2,1,0:T(8,128)(2,1)S(1)}, u32[]{:S(2)}, u32[]{:S(2)}) %collective-permute-start.11) | collective-permute-done | bytes 2097184 | tf_op jit(solution)/shard_map/ppermute | solution.py:104
  308.0 2.1 fusion.3
  310.2 5.9 %all-to-all-start.1 = ((bf16[64,8,2048]{2,1,0:T(8,128)(2,1)}), bf16[64,8,2048]{2,1,0:T(8,128)(2,1)S(1)}, u32[]{:S(2)}, u32[]{:S(2)}) async-start(bf16[64,8,2048]{2,1,0:T(8,128)(2,1)} %fusion.3), calls=%async_computation.2 | async-start | bytes 4194304 | tf_op jit(solution)/shard_map/all_to_all | solution.py:71
  316.1 0.8 select_reduce_fusion
  316.9 52.0 %all-to-all-done.1 = bf16[64,8,2048]{2,1,0:T(8,128)(2,1)S(1)} async-done(((bf16[64,8,2048]{2,1,0:T(8,128)(2,1)}), bf16[64,8,2048]{2,1,0:T(8,128)(2,1)S(1)}, u32[]{:S(2)}, u32[]{:S(2)}) %all-to-all-start.1) | async-done | bytes 2097184 | tf_op jit(solution)/shard_map/all_to_all | solution.py:71
  368.9 3.0 fusion.7
  (72 shorter events, 2.5 us)
Async XLA Ops:
  6.5 238.8 %copy-start = (bf16[1,352,2048]{2,1,0:T(8,128)(2,1)S(1)}, bf16[1,352,2048]{2,1,0:T(8,128)(2,1)}, u32[]{:S(2)}) copy-start(bf16[1,352,2048]{2,1,0:T(8,128)(2,1)} %param.31) | copy-start | bytes 4325380
  6.5 102.9 %reduce-scatter.2.cloned.1.call-start = ((), (), s32[]{:S(2)}) async-start(), calls=%async_computation.3 | async-start | bytes 2359296 | tf_op jit(solution)/shard_map/reduce_scatter | solution.py:269
  7.9 1.5 copy-start.6
  9.4 21.7 %copy-start.4 = (bf16[1024,128]{1,0:T(8,128)(2,1)S(1)}, bf16[1024,128]{1,0:T(8,128)(2,1)}, u32[]{:S(2)}) copy-start(bf16[1024,128]{1,0:T(8,128)(2,1)} %param.20) | copy-start | bytes 786436
  12.0 19.1 %copy-start.5 = (bf16[1024,128]{1,0:T(8,128)(2,1)S(1)}, bf16[1024,128]{1,0:T(8,128)(2,1)}, u32[]{:S(2)}) copy-start(bf16[1024,128]{1,0:T(8,128)(2,1)} %param.19) | copy-start | bytes 786436
  17.3 15.5 %collective-permute-start = (f32[4,8320]{1,0:T(4,128)}, f32[4,8320]{1,0:T(4,128)}, u32[]{:S(2)}, u32[]{:S(2)}) collective-permute-start(f32[4,8320]{1,0:T(4,128)} %pad_maximum_fusion.1), channel_id=1, source_target_pairs={{0,32},{16,48},{32,64},{48,80},{64,96},{80,112},{96,128},{112,144}... | collective-permute-start | bytes 399368 | tf_op jit(solution)/shard_map/ppermute | solution.py:37
  23.6 9.2 %collective-permute-start.1 = (f32[4,8320]{1,0:T(4,128)}, f32[4,8320]{1,0:T(4,128)}, u32[]{:S(2)}, u32[]{:S(2)}) collective-permute-start(f32[4,8320]{1,0:T(4,128)} %pad_maximum_fusion.1), channel_id=1, source_target_pairs={{0,16},{16,32},{32,48},{48,64},{64,80},{80,96},{96,112},{112,128},... | collective-permute-start | bytes 399368 | tf_op jit(solution)/shard_map/ppermute | solution.py:37
  26.6 6.3 %collective-permute-start.2 = (f32[4,8320]{1,0:T(4,128)}, f32[4,8320]{1,0:T(4,128)}, u32[]{:S(2)}, u32[]{:S(2)}) collective-permute-start(f32[4,8320]{1,0:T(4,128)} %pad_maximum_fusion.1), channel_id=1, source_target_pairs={{0,48},{16,64},{32,80},{48,96},{64,112},{80,128},{96,144},{112,160... | collective-permute-start | bytes 399368 | tf_op jit(solution)/shard_map/ppermute | solution.py:37
  36.2 13.8 %collective-permute-start.3 = (f32[4,8320]{1,0:T(4,128)}, f32[4,8320]{1,0:T(4,128)}, u32[]{:S(2)}, u32[]{:S(2)}) collective-permute-start(f32[4,8320]{1,0:T(4,128)} %pad_maximum_fusion.2), channel_id=1, source_target_pairs={{0,128},{16,144},{32,160},{48,176},{64,192},{80,208},{96,224},{112... | collective-permute-start | bytes 399368 | tf_op jit(solution)/shard_map/ppermute | solution.py:37
  41.2 8.8 %collective-permute-start.4 = (f32[4,8320]{1,0:T(4,128)}, f32[4,8320]{1,0:T(4,128)}, u32[]{:S(2)}, u32[]{:S(2)}) collective-permute-start(f32[4,8320]{1,0:T(4,128)} %pad_maximum_fusion.2), channel_id=1, source_target_pairs={{0,64},{16,80},{32,96},{48,112},{64,128},{80,144},{96,160},{112,17... | collective-permute-start | bytes 399368 | tf_op jit(solution)/shard_map/ppermute | solution.py:37
  44.0 6.8 %collective-permute-start.5 = (f32[4,8320]{1,0:T(4,128)}, f32[4,8320]{1,0:T(4,128)}, u32[]{:S(2)}, u32[]{:S(2)}) collective-permute-start(f32[4,8320]{1,0:T(4,128)} %pad_maximum_fusion.2), channel_id=1, source_target_pairs={{0,192},{16,208},{32,224},{48,240},{1,193},{17,209},{33,225},{49,2... | collective-permute-start | bytes 399368 | tf_op jit(solution)/shard_map/ppermute | solution.py:37
  50.8 4.0 %copy-start.7 = (bf16[1024,256]{0,1:T(8,128)(2,1)S(1)}, bf16[1024,256]{0,1:T(8,128)(2,1)}, u32[]{:S(2)}) copy-start(bf16[1024,256]{0,1:T(8,128)(2,1)} %copy.119) | copy-start | bytes 1572868
  50.8 4.0 %copy-start.12 = (bf16[256,2048]{1,0:T(8,128)(2,1)S(1)}, bf16[256,2048]{1,0:T(8,128)(2,1)}, u32[]{:S(2)}) copy-start(bf16[256,2048]{1,0:T(8,128)(2,1)} %param.24) | copy-start | bytes 3145732
  56.2 1.9 copy-start.2
  59.6 6.8 %collective-permute-start.6 = (bf16[8,64,2048]{2,1,0:T(8,128)(2,1)}, bf16[8,64,2048]{2,1,0:T(8,128)(2,1)}, u32[]{:S(2)}, u32[]{:S(2)}) collective-permute-start(bf16[8,64,2048]{2,1,0:T(8,128)(2,1)} %dynamic-slice_bitcast_fusion), channel_id=1, source_target_pairs={{0,1},{1,0},{2,3},{3,2},{4,5},{5,4},{6,7},{7,6},{8,9},{9,8},{10,11... | collective-permute-start | bytes 6291464 | tf_op jit(solution)/shard_map/ppermute | solution.py:104
  62.3 8.6 %copy-start.8 = (s32[64,6]{0,1:T(8,128)S(1)}, s32[64,6]{0,1:T(8,128)}, u32[]{:S(2)}) copy-start(s32[64,6]{0,1:T(8,128)} %param.27) | copy-start | bytes 4612
  62.3 47.2 %copy-start.3 = (bf16[64,2048]{1,0:T(8,128)(2,1)S(1)}, bf16[64,2048]{1,0:T(8,128)(2,1)}, u32[]{:S(2)}) copy-start(bf16[64,2048]{1,0:T(8,128)(2,1)} %param.25) | copy-start | bytes 786436
  62.3 48.3 %copy-start.9 = (f32[2048]{0:T(1024)S(1)}, f32[2048]{0:T(1024)}, u32[]{:S(2)}) copy-start(f32[2048]{0:T(1024)} %param.26) | copy-start | bytes 24580
  174.8 44.5 %collective-permute-start.7 = (bf16[64,8,2048]{2,1,0:T(8,128)(2,1)S(1)}, bf16[64,8,2048]{2,1,0:T(8,128)(2,1)S(1)}, u32[]{:S(2)}, u32[]{:S(2)}) collective-permute-start(bf16[64,8,2048]{2,1,0:T(8,128)(2,1)S(1)} %all_to_all.10), channel_id=1, source_target_pairs={{0,2},{2,0},{1,3},{3,1},{4,6},{6,4},{5,7},{7,5},{8,10},{10,8},{9,1... | collective-permute-start | bytes 6291464 | tf_op jit(solution)/shard_map/ppermute | solution.py:104
  174.8 48.4 %collective-permute-start.8 = (bf16[64,8,2048]{2,1,0:T(8,128)(2,1)S(1)}, bf16[64,8,2048]{2,1,0:T(8,128)(2,1)S(1)}, u32[]{:S(2)}, u32[]{:S(2)}) collective-permute-start(bf16[64,8,2048]{2,1,0:T(8,128)(2,1)S(1)} %all_to_all.10), channel_id=1, source_target_pairs={{0,1},{1,0},{2,3},{3,2},{4,5},{5,4},{6,7},{7,6},{8,9},{9,8},{10,11... | collective-permute-start | bytes 6291464 | tf_op jit(solution)/shard_map/ppermute | solution.py:104
  219.3 7.3 %collective-permute-start.9 = (bf16[64,8,2048]{2,1,0:T(8,128)(2,1)S(1)}, bf16[64,8,2048]{2,1,0:T(8,128)(2,1)S(1)}, u32[]{:S(2)}, u32[]{:S(2)}) collective-permute-start(bf16[64,8,2048]{2,1,0:T(8,128)(2,1)S(1)} %collective-permute-done.7), channel_id=1, source_target_pairs={{0,1},{1,0},{2,3},{3,2},{4,5},{5,4},{6,7},{7,6},{8,9},{9,8},{10,11... | collective-permute-start | bytes 6291464 | tf_op jit(solution)/shard_map/ppermute | solution.py:104
  235.2 6.4 %copy-start.1 = (bf16[2,2,64,8,2048]{4,3,2,1,0:T(8,128)(2,1)S(1)}, bf16[2,2,64,8,2048]{4,3,2,1,0:T(8,128)(2,1)}, u32[]{:S(2)}) copy-start(bf16[2,2,64,8,2048]{4,3,2,1,0:T(8,128)(2,1)} %pad_maximum_fusion) | copy-start | bytes 25165828
  235.2 6.6 %copy-start.11 = (bf16[1,352,2048]{2,1,0:T(8,128)(2,1)S(1)}, bf16[1,352,2048]{2,1,0:T(8,128)(2,1)}, u32[]{:S(2)}) copy-start(bf16[1,352,2048]{2,1,0:T(8,128)(2,1)} %param.30) | copy-start | bytes 4325380
  251.1 7.5 %collective-permute-start.10 = (bf16[2,64,8,2048]{3,2,1,0:T(8,128)(2,1)S(1)}, bf16[2,64,8,2048]{3,2,1,0:T(8,128)(2,1)S(1)}, u32[]{:S(2)}, u32[]{:S(2)}) collective-permute-start(bf16[2,64,8,2048]{3,2,1,0:T(8,128)(2,1)S(1)} %bitcast.159), channel_id=1, source_target_pairs={{0,1},{1,0},{2,3},{3,2},{4,5},{5,4},{6,7},{7,6},{8,9},{9,8},{10,11... | collective-permute-start | bytes 12582920 | tf_op jit(solution)/shard_map/ppermute | solution.py:104
  261.1 55.0 %copy-start.10 = (f32[64,6]{0,1:T(8,128)S(1)}, f32[64,6]{0,1:T(8,128)}, u32[]{:S(2)}) copy-start(f32[64,6]{0,1:T(8,128)} %param.28) | copy-start | bytes 4612
  261.1 46.9 %collective-permute-start.11 = (bf16[64,8,2048]{2,1,0:T(8,128)(2,1)S(1)}, bf16[64,8,2048]{2,1,0:T(8,128)(2,1)S(1)}, u32[]{:S(2)}, u32[]{:S(2)}) collective-permute-start(bf16[64,8,2048]{2,1,0:T(8,128)(2,1)S(1)} %slice_bitcast_fusion), channel_id=1, source_target_pairs={{0,2},{2,0},{1,3},{3,1},{4,6},{6,4},{5,7},{7,5},{8,10},{10,8},{9,1... | collective-permute-start | bytes 6291464 | tf_op jit(solution)/shard_map/ppermute | solution.py:104
  310.2 58.8 %all-to-all-start.1 = ((bf16[64,8,2048]{2,1,0:T(8,128)(2,1)}), bf16[64,8,2048]{2,1,0:T(8,128)(2,1)S(1)}, u32[]{:S(2)}, u32[]{:S(2)}) async-start(bf16[64,8,2048]{2,1,0:T(8,128)(2,1)} %fusion.3), calls=%async_computation.2 | async-start | bytes 4194304 | tf_op jit(solution)/shard_map/all_to_all | solution.py:71
Sparse Core Ops, SparseCore 0:
  71.0 38.3 reduce-scatter.1

commit v7 on v6

--- a/solution.py
+++ b/solution.py
@@ -20,6 +20,7 @@
 CUM_DOT = True
 MIX_PAIR = False
 C_EARLY = True
+R_EARLY = True
 UNROLL = False
 
 
@@ -66,8 +67,14 @@
         jnp.bfloat16
     )
     piece_out = piece_out.reshape(block.shape)
-    piece_sum = pair_reduce(piece_out, "c", C_SWAP)
-    piece_sum = pair_reduce(piece_sum, "pz", PZ_SWAP)
+    if R_EARLY:
+        crossing = pair_reduce(piece_out[:, 1], "c", True)
+        arriving = pair_swap(crossing, "pz")
+        staying = pair_reduce(piece_out[:, 0], "c", True)
+        piece_sum = (staying.astype(jnp.float32) + arriving.astype(jnp.float32)).astype(jnp.bfloat16)
+    else:
+        piece_sum = pair_reduce(piece_out, "c", C_SWAP)
+        piece_sum = pair_reduce(piece_sum, "pz", PZ_SWAP)
     return lax.all_to_all(piece_sum, ("seq", "eh"), split_axis=0, concat_axis=0, tiled=True)
 
 

time: 380 us -> 374 us (0.984)
    convert_element_type x3 -> x2, other arithmetic: 8.89 us -> 4.47 us  [pair_reduce(): (x[0].astype(jnp.float32) + pair_swap(x[1], axis).astype(jnp.float32)).as...]
    ppermute x6 -> x7, waiting for transfers between devices: 103 us -> 99.1 us  [pair_swap(): return lax.ppermute(x, axis, perm=[(0, 1), (1, 0)])]
    ppermute x6 -> x7, starting transfers between devices: 9.58 us -> 10.4 us  [pair_swap(): return lax.ppermute(x, axis, perm=[(0, 1), (1, 0)])]
  transfers between devices with their start and end apart: 14 -> 15, of which waited for: 7 -> 8; matrix products, arithmetic and copies ran while one was open for 3% -> 3% of each run, Pallas kernels for 0% -> 0%
where the time goes in v7:
time: 374 us; the launch traced here: 373 us
  waiting for transfers between devices  189 us (51%)
  blocking collectives  61.8 us (17%)
  starting transfers between devices  39.8 us (11%)
  other arithmetic  29.6 us (8%)
  matrix products  25.7 us (7%)
  between operations  13.8 us (4%)
  local copies, waits for them, and re-layouts  13.3 us (4%)
    ppermute x7, waiting for transfers between devices, pair_swap(): return lax.ppermute(x, axis, perm=[(0, 1), (1, 0)])  99.1 us
    all_to_all x1, blocking collectives, expert_round(): lax.all_to_all(outgoing, ('seq', 'eh'), split_axis=0, concat_axis=0, tile...  61.8 us
    all_to_all x1, waiting for transfers between devices, expert_round(): lax.all_to_all(piece_sum, ('seq', 'eh'), split_axis=0, concat_axis=0, til...  52.1 us
    reduce_scatter x1, waiting for transfers between devices, shards(): lax.psum_scatter(projected, ('eh', 'pz'), scatter_dimension=0, tiled=True)  37.7 us
    ppermute x6, starting transfers between devices, shifted(): lax.ppermute(packed, axis, perm=[(i, i + shift) for i in range(count - sh...  22.9 us
    ppermute x7, starting transfers between devices, pair_swap(): return lax.ppermute(x, axis, perm=[(0, 1), (1, 0)])  10.4 us
    another operation x3, other arithmetic, expert_round(): jnp.stack([jnp.stack([arrived, partner]), jnp.stack([pair_swap(arrived, '...  8.89 us
  transfers between devices with their start and end apart: 15, of which 8 were waited for; matrix products, arithmetic and copies ran while one was open for 3% of the time, Pallas kernels for 0%

profile of v7, /device:TPU:1, one launch (start us, length us, event | category | flops | bytes accessed | tf_op | source)
XLA Modules:
  0.0 372.9 jit_solution(17902676048922680312)
XLA Ops:
  6.5 0.8 reshape.136
  7.6 0.3 copy.108
  8.0 0.8 reshape.138
  8.9 2.0 reshape.154
  10.9 0.5 copy.113
  11.5 1.3 fusion.35
  12.8 3.1 while.13
  12.8 0.7 bitcast_dynamic-update-slice_fusion.2
  13.6 0.7 bitcast_dynamic-update-slice_fusion.2
  14.3 0.7 bitcast_dynamic-update-slice_fusion.2
  15.1 0.7 bitcast_dynamic-update-slice_fusion.2
  16.1 0.7 pad_maximum_fusion.1
  16.8 6.3 %collective-permute-start = (f32[4,8320]{1,0:T(4,128)}, f32[4,8320]{1,0:T(4,128)}, u32[]{:S(2)}, u32[]{:S(2)}) collective-permute-start(f32[4,8320]{1,0:T(4,128)} %pad_maximum_fusion.1), channel_id=1, source_target_pairs={{0,32},{16,48},{32,64},{48,80},{64,96},{80,112},{96,128},{112,144}... | collective-permute-start | bytes 399368 | tf_op jit(solution)/shard_map/ppermute | solution.py:38
  23.1 2.9 collective-permute-start.1
  26.0 4.5 %collective-permute-start.2 = (f32[4,8320]{1,0:T(4,128)}, f32[4,8320]{1,0:T(4,128)}, u32[]{:S(2)}, u32[]{:S(2)}) collective-permute-start(f32[4,8320]{1,0:T(4,128)} %pad_maximum_fusion.1), channel_id=1, source_target_pairs={{0,48},{16,64},{32,80},{48,96},{64,112},{80,128},{96,144},{112,160... | collective-permute-start | bytes 399368 | tf_op jit(solution)/shard_map/ppermute | solution.py:38
  30.6 0.3 fusion.65
  30.9 1.4 fusion.20
  32.3 0.6 reduce_window_sum.29
  32.9 1.4 fusion.63
  34.3 1.2 multiply_add_fusion
  35.6 0.7 pad_maximum_fusion.2
  36.2 4.4 %collective-permute-start.3 = (f32[4,8320]{1,0:T(4,128)}, f32[4,8320]{1,0:T(4,128)}, u32[]{:S(2)}, u32[]{:S(2)}) collective-permute-start(f32[4,8320]{1,0:T(4,128)} %pad_maximum_fusion.2), channel_id=1, source_target_pairs={{0,128},{16,144},{32,160},{48,176},{64,192},{80,208},{96,224},{112... | collective-permute-start | bytes 399368 | tf_op jit(solution)/shard_map/ppermute | solution.py:38
  40.6 2.9 collective-permute-start.4
  43.5 1.9 collective-permute-start.5
  45.4 0.7 subtract_exponential_fusion
  46.1 2.0 copy.119
  48.2 0.9 fusion.58
  49.0 1.2 fusion.50
  50.2 1.8 fusion.23
  52.0 0.7 copy.118
  53.0 0.3 copy-done.12
  53.4 1.4 convolution_convert_fusion.1
  54.8 1.9 copy-done.2
  56.7 1.5 dynamic-slice_bitcast_fusion
  58.1 2.7 collective-permute-start.6
  60.8 4.0 %collective-permute-done.6 = bf16[8,64,2048]{2,1,0:T(8,128)(2,1)S(1)} collective-permute-done((bf16[8,64,2048]{2,1,0:T(8,128)(2,1)}, bf16[8,64,2048]{2,1,0:T(8,128)(2,1)S(1)}, u32[]{:S(2)}, u32[]{:S(2)}) %collective-permute-start.6) | collective-permute-done | bytes 2097184 | tf_op jit(solution)/shard_map/ppermute | solution.py:111
  64.8 3.7 fusion.4
  68.9 0.9 reduce-window.6
  70.6 37.7 %reduce-scatter.2.cloned.1.call-done = bf16[1,64,2048]{2,1,0:T(8,128)(2,1)} async-done(((bf16[8,64,2048]{2,1,0:T(8,128)(2,1)}), bf16[1,64,2048]{2,1,0:T(8,128)(2,1)}) %reduce-scatter.2.cloned.1.call-update) | async-done | bytes 262160 | tf_op jit(solution)/shard_map/reduce_scatter | solution.py:276
  108.3 1.1 fusion.31
  109.5 1.7 fusion.6
  111.2 61.8 %all_to_all.10 = bf16[64,8,2048]{2,1,0:T(8,128)(2,1)S(1)} all-to-all(bf16[64,8,2048]{2,1,0:T(8,128)(2,1)S(1)} %fusion.6), channel_id=1, replica_groups=mesh['seq'=16,'eh'=4,'pz'=2,'c'=2] {'seq','eh'}, dimensions={0} | all-to-all | bytes 4194304 | tf_op jit(solution)/shard_map/all_to_all | solution.py:50
  173.0 2.9 collective-permute-start.8
  175.9 41.3 %collective-permute-done.7 = bf16[64,8,2048]{2,1,0:T(8,128)(2,1)S(1)} collective-permute-done((bf16[64,8,2048]{2,1,0:T(8,128)(2,1)S(1)}, bf16[64,8,2048]{2,1,0:T(8,128)(2,1)S(1)}, u32[]{:S(2)}, u32[]{:S(2)}) %collective-permute-start.7) | collective-permute-done | bytes 2097184 | tf_op jit(solution)/shard_map/ppermute | solution.py:111
  217.2 3.9 %collective-permute-start.9 = (bf16[64,8,2048]{2,1,0:T(8,128)(2,1)S(1)}, bf16[64,8,2048]{2,1,0:T(8,128)(2,1)S(1)}, u32[]{:S(2)}, u32[]{:S(2)}) collective-permute-start(bf16[64,8,2048]{2,1,0:T(8,128)(2,1)S(1)} %collective-permute-done.7), channel_id=1, source_target_pairs={{0,1},{1,0},{2,3},{3,2},{4,5},{5,4},{6,7},{7,6},{8,9},{9,8},{10,11... | collective-permute-start | bytes 6291464 | tf_op jit(solution)/shard_map/ppermute | solution.py:111
  221.1 0.4 maximum_bitcast_fusion
  221.5 3.4 collective-permute-done.9
  224.8 2.3 maximum_bitcast_fusion.1
  227.2 6.2 %pad_maximum_fusion = bf16[2,2,64,8,2048]{4,3,2,1,0:T(8,128)(2,1)} fusion(bf16[1,2,64,8,2048]{4,3,2,1,0:T(8,128)(2,1)} %maximum_bitcast_fusion.1, bf16[1,2,64,8,2048]{4,3,2,1,0:T(8,128)(2,1)S(1)} %maximum_bitcast_fusion), kind=kLoop, calls=%fused_computation.5 | loop fusion | flops 4194304 | bytes 16777216 | tf_op jit(solution)/shard_map/stack | solution.py:53
  233.4 6.4 %fusion.18 = f32[2048,352]{0,1:T(8,128)S(1)} fusion(bf16[2048,2048]{1,0:T(8,128)(2,1)} %bitcast.160, bf16[1,352,2048]{2,1,0:T(8,128)(2,1)} %param.29), kind=kOutput, calls=%fused_computation.39 | convolution fusion | flops 2952790016 | bytes 12713984 | tf_op jit(solution)/shard_map/dot_general | solution.py:61
  240.0 3.5 fusion.5
  243.5 4.8 %convolution_convert_fusion = bf16[2048,2048]{1,0:T(8,128)(2,1)S(1)} fusion(bf16[2048,352]{0,1:T(8,128)(2,1)S(1)} %fusion.5, bf16[1,352,2048]{2,1,0:T(8,128)(2,1)S(1)} %copy-done), kind=kOutput, calls=%fused_computation.6 | convolution fusion | flops 2956984320 | bytes 11272192 | tf_op jit(solution)/shard_map/dot_general | solution.py:66
  248.3 0.5 slice_bitcast_fusion.2
  248.8 0.5 collective-permute-start.11
  249.4 3.6 collective-permute-done.11
  253.1 0.8 fusion.2
  253.8 0.3 collective-permute-start.12
  254.2 1.9 collective-permute-done.10
  256.1 44.9 %collective-permute-done.12 = bf16[64,8,2048]{2,1,0:T(8,128)(2,1)S(1)} collective-permute-done((bf16[64,8,2048]{2,1,0:T(8,128)(2,1)S(1)}, bf16[64,8,2048]{2,1,0:T(8,128)(2,1)S(1)}, u32[]{:S(2)}, u32[]{:S(2)}) %collective-permute-start.12) | collective-permute-done | bytes 2097184 | tf_op jit(solution)/shard_map/ppermute | solution.py:111
  301.0 2.6 add_convert_fusion
  303.6 6.5 %all-to-all-start.1 = ((bf16[64,8,2048]{2,1,0:T(8,128)(2,1)}), bf16[64,8,2048]{2,1,0:T(8,128)(2,1)S(1)}, u32[]{:S(2)}, u32[]{:S(2)}) async-start(bf16[64,8,2048]{2,1,0:T(8,128)(2,1)} %add_convert_fusion), calls=%async_computation.2 | async-start | bytes 4194304 | tf_op jit(solution)/shard_map/all_to_all | solution.py:78
  310.1 0.8 select_reduce_fusion
  310.9 52.1 %all-to-all-done.1 = bf16[64,8,2048]{2,1,0:T(8,128)(2,1)S(1)} async-done(((bf16[64,8,2048]{2,1,0:T(8,128)(2,1)}), bf16[64,8,2048]{2,1,0:T(8,128)(2,1)S(1)}, u32[]{:S(2)}, u32[]{:S(2)}) %all-to-all-start.1) | async-done | bytes 2097184 | tf_op jit(solution)/shard_map/all_to_all | solution.py:78
  363.0 3.0 fusion.7
  (73 shorter events, 3.0 us)
Async XLA Ops:
  6.5 237.0 %copy-start = (bf16[1,352,2048]{2,1,0:T(8,128)(2,1)S(1)}, bf16[1,352,2048]{2,1,0:T(8,128)(2,1)}, u32[]{:S(2)}) copy-start(bf16[1,352,2048]{2,1,0:T(8,128)(2,1)} %param.31) | copy-start | bytes 4325380
  6.5 101.8 %reduce-scatter.2.cloned.1.call-start = ((), (), s32[]{:S(2)}) async-start(), calls=%async_computation.3 | async-start | bytes 2359296 | tf_op jit(solution)/shard_map/reduce_scatter | solution.py:276
  7.9 1.0 copy-start.6
  11.4 19.1 %copy-start.4 = (bf16[1024,128]{1,0:T(8,128)(2,1)S(1)}, bf16[1024,128]{1,0:T(8,128)(2,1)}, u32[]{:S(2)}) copy-start(bf16[1024,128]{1,0:T(8,128)(2,1)} %param.20) | copy-start | bytes 786436
  11.5 19.1 %copy-start.5 = (bf16[1024,128]{1,0:T(8,128)(2,1)S(1)}, bf16[1024,128]{1,0:T(8,128)(2,1)}, u32[]{:S(2)}) copy-start(bf16[1024,128]{1,0:T(8,128)(2,1)} %param.19) | copy-start | bytes 786436
  16.8 16.1 %collective-permute-start = (f32[4,8320]{1,0:T(4,128)}, f32[4,8320]{1,0:T(4,128)}, u32[]{:S(2)}, u32[]{:S(2)}) collective-permute-start(f32[4,8320]{1,0:T(4,128)} %pad_maximum_fusion.1), channel_id=1, source_target_pairs={{0,32},{16,48},{32,64},{48,80},{64,96},{80,112},{96,128},{112,144}... | collective-permute-start | bytes 399368 | tf_op jit(solution)/shard_map/ppermute | solution.py:38
  23.1 9.8 %collective-permute-start.1 = (f32[4,8320]{1,0:T(4,128)}, f32[4,8320]{1,0:T(4,128)}, u32[]{:S(2)}, u32[]{:S(2)}) collective-permute-start(f32[4,8320]{1,0:T(4,128)} %pad_maximum_fusion.1), channel_id=1, source_target_pairs={{0,16},{16,32},{32,48},{48,64},{64,80},{80,96},{96,112},{112,128},... | collective-permute-start | bytes 399368 | tf_op jit(solution)/shard_map/ppermute | solution.py:38
  26.0 6.9 %collective-permute-start.2 = (f32[4,8320]{1,0:T(4,128)}, f32[4,8320]{1,0:T(4,128)}, u32[]{:S(2)}, u32[]{:S(2)}) collective-permute-start(f32[4,8320]{1,0:T(4,128)} %pad_maximum_fusion.1), channel_id=1, source_target_pairs={{0,48},{16,64},{32,80},{48,96},{64,112},{80,128},{96,144},{112,160... | collective-permute-start | bytes 399368 | tf_op jit(solution)/shard_map/ppermute | solution.py:38
  36.2 11.9 %collective-permute-start.3 = (f32[4,8320]{1,0:T(4,128)}, f32[4,8320]{1,0:T(4,128)}, u32[]{:S(2)}, u32[]{:S(2)}) collective-permute-start(f32[4,8320]{1,0:T(4,128)} %pad_maximum_fusion.2), channel_id=1, source_target_pairs={{0,128},{16,144},{32,160},{48,176},{64,192},{80,208},{96,224},{112... | collective-permute-start | bytes 399368 | tf_op jit(solution)/shard_map/ppermute | solution.py:38
  40.6 7.5 %collective-permute-start.4 = (f32[4,8320]{1,0:T(4,128)}, f32[4,8320]{1,0:T(4,128)}, u32[]{:S(2)}, u32[]{:S(2)}) collective-permute-start(f32[4,8320]{1,0:T(4,128)} %pad_maximum_fusion.2), channel_id=1, source_target_pairs={{0,64},{16,80},{32,96},{48,112},{64,128},{80,144},{96,160},{112,17... | collective-permute-start | bytes 399368 | tf_op jit(solution)/shard_map/ppermute | solution.py:38
  43.5 5.5 %collective-permute-start.5 = (f32[4,8320]{1,0:T(4,128)}, f32[4,8320]{1,0:T(4,128)}, u32[]{:S(2)}, u32[]{:S(2)}) collective-permute-start(f32[4,8320]{1,0:T(4,128)} %pad_maximum_fusion.2), channel_id=1, source_target_pairs={{0,192},{16,208},{32,224},{48,240},{1,193},{17,209},{33,225},{49,2... | collective-permute-start | bytes 399368 | tf_op jit(solution)/shard_map/ppermute | solution.py:38
  52.0 1.0 copy-start.7
  52.0 1.4 copy-start.12
  54.8 1.9 copy-start.2
  58.1 6.6 %collective-permute-start.6 = (bf16[8,64,2048]{2,1,0:T(8,128)(2,1)}, bf16[8,64,2048]{2,1,0:T(8,128)(2,1)S(1)}, u32[]{:S(2)}, u32[]{:S(2)}) collective-permute-start(bf16[8,64,2048]{2,1,0:T(8,128)(2,1)} %dynamic-slice_bitcast_fusion), channel_id=1, source_target_pairs={{0,1},{1,0},{2,3},{3,2},{4,5},{5,4},{6,7},{7,6},{8,9},{9,8},{10,11... | collective-permute-start | bytes 6291464 | tf_op jit(solution)/shard_map/ppermute | solution.py:111
  60.8 7.7 %copy-start.8 = (s32[64,6]{0,1:T(8,128)S(1)}, s32[64,6]{0,1:T(8,128)}, u32[]{:S(2)}) copy-start(s32[64,6]{0,1:T(8,128)} %param.27) | copy-start | bytes 4612
  68.5 39.9 %copy-start.3 = (bf16[64,2048]{1,0:T(8,128)(2,1)S(1)}, bf16[64,2048]{1,0:T(8,128)(2,1)}, u32[]{:S(2)}) copy-start(bf16[64,2048]{1,0:T(8,128)(2,1)} %param.25) | copy-start | bytes 786436
  68.5 41.0 %copy-start.9 = (f32[2048]{0:T(1024)S(1)}, f32[2048]{0:T(1024)}, u32[]{:S(2)}) copy-start(f32[2048]{0:T(1024)} %param.26) | copy-start | bytes 24580
  173.0 44.2 %collective-permute-start.7 = (bf16[64,8,2048]{2,1,0:T(8,128)(2,1)S(1)}, bf16[64,8,2048]{2,1,0:T(8,128)(2,1)S(1)}, u32[]{:S(2)}, u32[]{:S(2)}) collective-permute-start(bf16[64,8,2048]{2,1,0:T(8,128)(2,1)S(1)} %all_to_all.10), channel_id=1, source_target_pairs={{0,2},{2,0},{1,3},{3,1},{4,6},{6,4},{5,7},{7,5},{8,10},{10,8},{9,1... | collective-permute-start | bytes 6291464 | tf_op jit(solution)/shard_map/ppermute | solution.py:111
  173.0 48.4 %collective-permute-start.8 = (bf16[64,8,2048]{2,1,0:T(8,128)(2,1)S(1)}, bf16[64,8,2048]{2,1,0:T(8,128)(2,1)S(1)}, u32[]{:S(2)}, u32[]{:S(2)}) collective-permute-start(bf16[64,8,2048]{2,1,0:T(8,128)(2,1)S(1)} %all_to_all.10), channel_id=1, source_target_pairs={{0,1},{1,0},{2,3},{3,2},{4,5},{5,4},{6,7},{7,6},{8,9},{9,8},{10,11... | collective-permute-start | bytes 6291464 | tf_op jit(solution)/shard_map/ppermute | solution.py:111
  217.2 7.6 %collective-permute-start.9 = (bf16[64,8,2048]{2,1,0:T(8,128)(2,1)S(1)}, bf16[64,8,2048]{2,1,0:T(8,128)(2,1)S(1)}, u32[]{:S(2)}, u32[]{:S(2)}) collective-permute-start(bf16[64,8,2048]{2,1,0:T(8,128)(2,1)S(1)} %collective-permute-done.7), channel_id=1, source_target_pairs={{0,1},{1,0},{2,3},{3,2},{4,5},{5,4},{6,7},{7,6},{8,9},{9,8},{10,11... | collective-permute-start | bytes 6291464 | tf_op jit(solution)/shard_map/ppermute | solution.py:111
  233.4 6.4 %copy-start.1 = (bf16[2,2,64,8,2048]{4,3,2,1,0:T(8,128)(2,1)S(1)}, bf16[2,2,64,8,2048]{4,3,2,1,0:T(8,128)(2,1)}, u32[]{:S(2)}) copy-start(bf16[2,2,64,8,2048]{4,3,2,1,0:T(8,128)(2,1)} %pad_maximum_fusion) | copy-start | bytes 25165828
  233.4 6.6 %copy-start.11 = (bf16[1,352,2048]{2,1,0:T(8,128)(2,1)S(1)}, bf16[1,352,2048]{2,1,0:T(8,128)(2,1)}, u32[]{:S(2)}) copy-start(bf16[1,352,2048]{2,1,0:T(8,128)(2,1)} %param.30) | copy-start | bytes 4325380
  248.8 4.2 %collective-permute-start.11 = (bf16[64,8,2048]{2,1,0:T(8,128)(2,1)S(1)}, bf16[64,8,2048]{2,1,0:T(8,128)(2,1)S(1)}, u32[]{:S(2)}, u32[]{:S(2)}) collective-permute-start(bf16[64,8,2048]{2,1,0:T(8,128)(2,1)S(1)} %get-tuple-element.73), channel_id=1, source_target_pairs={{0,1},{1,0},{2,3},{3,2},{4,5},{5,4},{6,7},{7,6},{8,9},{9,8},{10,11... | collective-permute-start | bytes 6291464 | tf_op jit(solution)/shard_map/ppermute | solution.py:111
  249.3 6.8 %collective-permute-start.10 = (bf16[64,8,2048]{2,1,0:T(8,128)(2,1)S(1)}, bf16[64,8,2048]{2,1,0:T(8,128)(2,1)S(1)}, u32[]{:S(2)}, u32[]{:S(2)}) collective-permute-start(bf16[64,8,2048]{2,1,0:T(8,128)(2,1)S(1)} %get-tuple-element.72), channel_id=1, source_target_pairs={{0,1},{1,0},{2,3},{3,2},{4,5},{5,4},{6,7},{7,6},{8,9},{9,8},{10,11... | collective-permute-start | bytes 6291464 | tf_op jit(solution)/shard_map/ppermute | solution.py:111
  253.8 47.2 %collective-permute-start.12 = (bf16[64,8,2048]{2,1,0:T(8,128)(2,1)S(1)}, bf16[64,8,2048]{2,1,0:T(8,128)(2,1)S(1)}, u32[]{:S(2)}, u32[]{:S(2)}) collective-permute-start(bf16[64,8,2048]{2,1,0:T(8,128)(2,1)S(1)} %fusion.2), channel_id=1, source_target_pairs={{0,2},{2,0},{1,3},{3,1},{4,6},{6,4},{5,7},{7,5},{8,10},{10,8},{9,1... | collective-permute-start | bytes 6291464 | tf_op jit(solution)/shard_map/ppermute | solution.py:111
  303.6 6.5 %copy-start.10 = (f32[64,6]{0,1:T(8,128)S(1)}, f32[64,6]{0,1:T(8,128)}, u32[]{:S(2)}) copy-start(f32[64,6]{0,1:T(8,128)} %param.28) | copy-start | bytes 4612
  303.6 59.4 %all-to-all-start.1 = ((bf16[64,8,2048]{2,1,0:T(8,128)(2,1)}), bf16[64,8,2048]{2,1,0:T(8,128)(2,1)S(1)}, u32[]{:S(2)}, u32[]{:S(2)}) async-start(bf16[64,8,2048]{2,1,0:T(8,128)(2,1)} %add_convert_fusion), calls=%async_computation.2 | async-start | bytes 4194304 | tf_op jit(solution)/shard_map/all_to_all | solution.py:78
Sparse Core Ops, SparseCore 0:
  68.6 39.6 reduce-scatter.1
